TPU v7x, 256 devices: a whole 4x4x8 slice. The times are simulated.
256 devices in a mesh: seq: 32 (over z, x), grp: 8 (over y, core).
Axes of the slice: x: 4, y: 4, z: 8, core: 2. Of those that a mesh axis runs over, the one named last changes fastest.
Arguments:
- in_gate: bfloat16 [65536, 512], P(('grp', 'seq')), parts along dimension 0, may hold values from -6 to 6
- values: bfloat16 [65536, 512], P(('grp', 'seq')), parts along dimension 0, may hold values from -6 to 6
- out_gate: bfloat16 [65536, 512], P(('grp', 'seq')), parts along dimension 0, may hold values from -6 to 6
- filter_taps: bfloat16 [8192, 512], P('seq'), may hold values from -0.0625 to 0.0625
- skip_gain: float32 [512], replicated, may hold values from -4 to 4
Outputs:
- mixed: bfloat16 [65536, 512], P(('grp', 'seq')), parts along dimension 0
There are 8 independent parts, one for each index of `grp`. A program takes and returns all parts, laid end to end along the dimension named above; an argument that names none is the same for every part. Nothing has to cross between parts.
All inputs are finite; a program needn't handle non-finite values.
Results may differ from a plain program's by a relative error of at most 0.001.
Values sent between devices are 32-bit elements; how exact they have to be, the bound alone decides.
No kernel may reach another device: no remote copies, remote signals or barrier semaphores. Data moves between devices by JAX's collectives and lax.ppermute only.
A program may use at most 64 MiB of HBM per device.

v0:
```python
import jax
import jax.numpy as jnp
from jax import lax
from jax.sharding import PartitionSpec as P

exact_mode = lax.Precision.HIGHEST


def angle_table(rows, cols, period):
    product = jnp.arange(rows, dtype=jnp.int32)[:, None] * jnp.arange(cols, dtype=jnp.int32)[None, :]
    return (product % period).astype(jnp.float32) * (2.0 * jnp.pi / period)


def dft_tables(side, filled):
    first = angle_table(side, filled, side)
    stage_a = jnp.concatenate([jnp.cos(first), -jnp.sin(first)], axis=0)
    second = angle_table(side, side, side)
    cos_b, sin_b = jnp.cos(second), jnp.sin(second)
    forward_b = jnp.block([[cos_b, -sin_b], [sin_b, cos_b]])
    inverse_b = jnp.block([[cos_b, sin_b], [-sin_b, cos_b]])
    twist = angle_table(side, side, side * side)
    return stage_a, forward_b, inverse_b, jnp.cos(twist), jnp.sin(twist)


def causal_conv(signals, taps_count):
    _, ch, n = signals.shape
    side = 128
    filled = n // side
    stage_a, forward_b, inverse_b, twist_cos, twist_sin = dft_tables(side, filled)
    x = signals.reshape(2 * ch, filled, side)
    a = jnp.einsum("kn,bnm->bkm", stage_a, x, precision=exact_mode)
    a_re, a_im = a[:, :side], a[:, side:]
    b_re = a_re * twist_cos + a_im * twist_sin
    b_im = a_im * twist_cos - a_re * twist_sin
    spec = jnp.einsum(
        "bkm,mj->bkj", jnp.concatenate([b_re, b_im], axis=-1), forward_b, precision=exact_mode
    )
    g_re, g_im = spec[:ch, :, :side], spec[:ch, :, side:]
    h_re, h_im = spec[ch:, :, :side], spec[ch:, :, side:]
    prod = jnp.concatenate([g_re * h_re - g_im * h_im, g_re * h_im + g_im * h_re], axis=-1)
    q = jnp.einsum("bkj,jm->bkm", prod, inverse_b, precision=exact_mode)
    q_re, q_im = q[..., :side], q[..., side:]
    r_re = q_re * twist_cos - q_im * twist_sin
    r_im = q_im * twist_cos + q_re * twist_sin
    y = jnp.einsum(
        "kn,bkm->bnm", stage_a, jnp.concatenate([r_re, r_im], axis=1), precision=exact_mode
    )
    return y.reshape(ch, n) * (1.0 / (side * side))


def local(in_gate, values, out_gate, filter_taps, skip_gain):
    gated = in_gate.astype(jnp.float32) * values.astype(jnp.float32)
    taps = filter_taps.astype(jnp.float32)
    both = jnp.stack([gated.T, taps.T])
    spread = lax.all_to_all(both, "seq", split_axis=1, concat_axis=2, tiled=True)
    conv = causal_conv(spread, spread.shape[2])
    back = lax.all_to_all(conv, "seq", split_axis=1, concat_axis=0, tiled=True)
    total = back.T + skip_gain[None, :] * gated
    return (out_gate.astype(jnp.float32) * total).astype(jnp.bfloat16)


def solution(mesh):
    in_specs = (
        P(("grp", "seq"), None),
        P(("grp", "seq"), None),
        P(("grp", "seq"), None),
        P("seq", None),
        P(),
    )
    out_specs = P(("grp", "seq"), None)
    return jax.shard_map(local, mesh=mesh, in_specs=in_specs, out_specs=out_specs, check_vma=False)
```

profile of v0, /device:TPU:8, one launch (start us, length us, event | category | flops | bytes accessed | tf_op | source)
XLA Modules:
  0.0 85.3 jit_solution(18196858233162477548)
XLA Ops:
  0.0 1.1 %copy.22 = bf16[256,512]{0,1:T(8,128)(2,1)S(1)} copy(bf16[256,512]{1,0:T(8,128)(2,1)} %param.5) | data formatting | bytes 524288 | tf_op args[0]
  1.1 1.1 %copy.23 = bf16[256,512]{0,1:T(8,128)(2,1)S(1)} copy(bf16[256,512]{1,0:T(8,128)(2,1)} %param.6) | data formatting | bytes 524288 | tf_op args[1]
  2.2 1.1 %copy.24 = bf16[256,512]{0,1:T(8,128)(2,1)S(1)} copy(bf16[256,512]{1,0:T(8,128)(2,1)} %param.8) | data formatting | bytes 524288 | tf_op args[3]
  3.3 0.1 fusion.20
  3.4 0.1 pad_maximum_fusion
  3.5 1.8 %copy.25 = f32[2,512,256]{2,0,1:T(2,128)} copy(f32[2,512,256]{2,1,0:T(8,128)S(1)} %pad_maximum_fusion) | data formatting | bytes 2097152 | tf_op jit(solution)/shard_map/stack | solution.py:54
  5.2 11.3 %all-to-all-start = ((f32[2,512,256]{2,0,1:T(2,128)}), f32[2,512,256]{2,0,1:T(2,128)S(1)}, u32[]{:S(2)}, u32[]{:S(2)}) async-start(f32[2,512,256]{2,0,1:T(2,128)} %copy.25), calls=%async_computation | async-start | bytes 2097152 | tf_op jit(solution)/shard_map/all_to_all | solution.py:55
  16.6 0.3 fusion.47
  16.8 0.1 copy.28
  16.9 0.1 copy.29
  17.0 0.2 sine_negate_fusion
  17.2 0.3 fusion.52
  17.5 0.3 fusion.45
  17.7 26.9 %all-to-all-done = f32[2,512,256]{2,0,1:T(2,128)S(1)} async-done(((f32[2,512,256]{2,0,1:T(2,128)}), f32[2,512,256]{2,0,1:T(2,128)S(1)}, u32[]{:S(2)}, u32[]{:S(2)}) %all-to-all-start) | async-done | bytes 1048608 | tf_op jit(solution)/shard_map/all_to_all | solution.py:55
  44.6 0.1 copy.26
  44.7 0.6 copy.27
  45.3 0.1 reshape.48
  45.4 3.5 %convolution_bitcast_fusion = f32[32,256,128]{1,2,0:T(8,128)S(1)} fusion(f32[32,64,128]{2,1,0:T(8,128)S(1)} %reshape.48, f32[128,64]{0,1:T(8,128)S(1)} %get-tuple-element.11, f32[128,64]{0,1:T(8,128)S(1)} %get-tuple-element.12), kind=kOutput, calls=%fused_computation.4 | convolution fusion | flops 805322752 | bytes 5308416 | tf_op jit(solution)/shard_map/kn,bnm->bkm/dot_general | solution.py:31
  48.9 0.6 multiply_add_fusion
  49.5 7.2 %fusion = f32[32,128,256]{2,1,0:T(8,128)S(1)} fusion(f32[32,128,128]{1,2,0:T(8,128)S(1)} %get-tuple-element.6, f32[32,128,128]{1,2,0:T(8,128)S(1)} %get-tuple-element.5, f32[128,128]{1,0:T(8,128)S(1)} %get-tuple-element.14, f32[128,128]{1,0:T(8,128)S(1)} %get-tuple-element.13, f32[128,128]{1,0:T(8,128)S(1)} %fusion.52), kind=kOutput, calls=%fused_computation | convolution fusion | flops 3222470656 | bytes 8585216 | tf_op jit(solution)/shard_map/bkm,mj->bkj/dot_general | solution.py:35
  56.7 0.3 multiply_subtract_fusion.2
  57.0 1.9 %fusion.4 = f32[16,128,256]{2,1,0:T(8,128)S(1)} fusion(f32[16,128,128]{2,1,0:T(8,128)S(1)} %get-tuple-element.8, f32[16,128,128]{2,1,0:T(8,128)S(1)} %get-tuple-element.7, f32[128,128]{1,0:T(8,128)S(1)} %get-tuple-element.14, f32[128,128]{1,0:T(8,128)S(1)} %fusion.52, f32[128,128]{1,0:T(8,128)S(1)} %get-tuple-element.13), kind=kOutput, calls=%fused_computation.5 | convolution fusion | flops 1611333632 | bytes 4390912 | tf_op jit(solution)/shard_map/bkj,jm->bkm/dot_general | solution.py:41
  58.9 0.3 multiply_subtract_fusion.1
  59.2 1.5 %fusion.15 = f32[16,64,128]{2,1,0:T(8,128)S(1)} fusion(f32[16,128,128]{2,1,0:T(8,128)S(1)} %get-tuple-element.10, f32[16,128,128]{2,1,0:T(8,128)S(1)} %get-tuple-element.9, f32[128,64]{0,1:T(8,128)S(1)} %get-tuple-element.11, f32[128,64]{0,1:T(8,128)S(1)} %get-tuple-element.12), kind=kOutput, calls=%fused_computation.16 | convolution fusion | flops 403324928 | bytes 2686976 | tf_op jit(solution)/shard_map/kn,bkm->bnm/dot_general | solution.py:45
  60.7 0.0 copy-start.1
  60.7 0.1 mul.326
  60.9 1.1 %copy.31 = f32[16,32,256]{2,0,1:T(8,128)} copy(f32[16,32,256]{2,1,0:T(8,128)S(1)} %mul.326) | data formatting | bytes 1048576 | tf_op jit(solution)/shard_map/mul | solution.py:48
  62.0 5.6 %all-to-all-start.1 = ((f32[16,32,256]{2,0,1:T(8,128)}), f32[16,32,256]{2,0,1:T(8,128)S(1)}, u32[]{:S(2)}, u32[]{:S(2)}) async-start(f32[16,32,256]{2,0,1:T(8,128)} %copy.31), calls=%async_computation.1 | async-start | bytes 1048576 | tf_op jit(solution)/shard_map/all_to_all | solution.py:57
  67.5 0.1 copy.21
  67.7 16.7 %all-to-all-done.1 = f32[16,32,256]{2,0,1:T(8,128)S(1)} async-done(((f32[16,32,256]{2,0,1:T(8,128)}), f32[16,32,256]{2,0,1:T(8,128)S(1)}, u32[]{:S(2)}, u32[]{:S(2)}) %all-to-all-start.1) | async-done | bytes 524320 | tf_op jit(solution)/shard_map/all_to_all | solution.py:57
  84.3 0.2 fusion.19
  84.5 0.8 copy.32
  (4 shorter events, 0.0 us)
Async XLA Ops:
  5.2 39.4 %all-to-all-start = ((f32[2,512,256]{2,0,1:T(2,128)}), f32[2,512,256]{2,0,1:T(2,128)S(1)}, u32[]{:S(2)}, u32[]{:S(2)}) async-start(f32[2,512,256]{2,0,1:T(2,128)} %copy.25), calls=%async_computation | async-start | bytes 2097152 | tf_op jit(solution)/shard_map/all_to_all | solution.py:55
  60.7 6.9 %copy-start = (bf16[256,512]{1,0:T(8,128)(2,1)S(1)}, bf16[256,512]{1,0:T(8,128)(2,1)}, u32[]{:S(2)}) copy-start(bf16[256,512]{1,0:T(8,128)(2,1)} %param.7) | copy-start | bytes 786436
  60.7 23.6 %copy-start.1 = (f32[512]{0:T(512)S(1)}, f32[512]{0:T(512)}, u32[]{:S(2)}) copy-start(f32[512]{0:T(512)} %param.9) | copy-start | bytes 6148
  62.0 22.4 %all-to-all-start.1 = ((f32[16,32,256]{2,0,1:T(8,128)}), f32[16,32,256]{2,0,1:T(8,128)S(1)}, u32[]{:S(2)}, u32[]{:S(2)}) async-start(f32[16,32,256]{2,0,1:T(8,128)} %copy.31), calls=%async_computation.1 | async-start | bytes 1048576 | tf_op jit(solution)/shard_map/all_to_all | solution.py:57
where the time goes:
time: 85.7 us; the launch traced here: 85.3 us
  waiting for transfers between devices  43.5 us (51%)
  starting transfers between devices  16.9 us (20%)
  matrix products  14 us (16%)
  local copies, waits for them, and re-layouts  8.2 us (10%)
  other arithmetic  2.51 us (3%)
    all_to_all x1, waiting for transfers between devices, local(): lax.all_to_all(both, 'seq', split_axis=1, concat_axis=2, tiled=True)  26.9 us
    all_to_all x1, waiting for transfers between devices, local(): back = lax.all_to_all(conv, 'seq', split_axis=1, concat_axis=0, tiled=True)  16.7 us
    all_to_all x1, starting transfers between devices, local(): lax.all_to_all(both, 'seq', split_axis=1, concat_axis=2, tiled=True)  11.3 us
    dot_general x1, matrix products, causal_conv(): jnp.einsum('bkm,mj->bkj', jnp.concatenate([b_re, b_im], axis=-1), forward...  7.19 us
    all_to_all x1, starting transfers between devices, local(): back = lax.all_to_all(conv, 'seq', split_axis=1, concat_axis=0, tiled=True)  5.57 us
    dot_general x1, matrix products, causal_conv(): a = jnp.einsum('kn,bnm->bkm', stage_a, x, precision=exact_mode)  3.47 us
    unnamed x8, local copies, waits for them, and re-layouts  3.39 us
    dot_general x1, matrix products, causal_conv(): q = jnp.einsum('bkj,jm->bkm', prod, inverse_b, precision=exact_mode)  1.87 us
  transfers between devices with their start and end apart: 2, of which 2 were waited for; matrix products, arithmetic and copies ran while one was open for 1% of the time, Pallas kernels for 0%

commit v1 on v0

v1 whole, which is shorter than its diff:
```python
import jax
import jax.numpy as jnp
from jax import lax
from jax.sharding import PartitionSpec as P

exact_mode = lax.Precision.HIGHEST
SIDE = 128


def angle_table(rows, cols, period):
    product = jnp.arange(rows, dtype=jnp.int32)[:, None] * jnp.arange(cols, dtype=jnp.int32)[None, :]
    return (product % period).astype(jnp.float32) * (2.0 * jnp.pi / period)


def dft_tables(filled):
    first = angle_table(SIDE, filled, SIDE)
    stage_a = jnp.concatenate([jnp.cos(first), -jnp.sin(first)], axis=0)
    second = angle_table(SIDE, SIDE, SIDE)
    cos_b, sin_b = jnp.cos(second), jnp.sin(second)
    forward_b = jnp.block([[cos_b, -sin_b], [sin_b, cos_b]])
    inverse_b = jnp.block([[cos_b, sin_b], [-sin_b, cos_b]])
    twist = angle_table(SIDE, SIDE, SIDE * SIDE)
    return stage_a, forward_b, inverse_b, jnp.cos(twist), jnp.sin(twist)


def spectrum(signal, tables):
    stage_a, forward_b, _, twist_cos, twist_sin = tables
    ch, n = signal.shape
    x = signal.reshape(ch, n // SIDE, SIDE)
    a = jnp.einsum("kn,bnm->bkm", stage_a, x, precision=exact_mode)
    a_re, a_im = a[:, :SIDE], a[:, SIDE:]
    b_re = a_re * twist_cos + a_im * twist_sin
    b_im = a_im * twist_cos - a_re * twist_sin
    return jnp.einsum(
        "bkm,mj->bkj", jnp.concatenate([b_re, b_im], axis=-1), forward_b, precision=exact_mode
    )


def inverse_prefix(spec_g, spec_h, tables, n):
    stage_a, _, inverse_b, twist_cos, twist_sin = tables
    ch = spec_g.shape[0]
    g_re, g_im = spec_g[..., :SIDE], spec_g[..., SIDE:]
    h_re, h_im = spec_h[..., :SIDE], spec_h[..., SIDE:]
    prod = jnp.concatenate([g_re * h_re - g_im * h_im, g_re * h_im + g_im * h_re], axis=-1)
    q = jnp.einsum("bkj,jm->bkm", prod, inverse_b, precision=exact_mode)
    q_re, q_im = q[..., :SIDE], q[..., SIDE:]
    r_re = q_re * twist_cos - q_im * twist_sin
    r_im = q_im * twist_cos + q_re * twist_sin
    y = jnp.einsum(
        "kn,bkm->bnm", stage_a, jnp.concatenate([r_re, r_im], axis=1), precision=exact_mode
    )
    return y.reshape(ch, n) * (1.0 / (SIDE * SIDE))


def local(in_gate, values, out_gate, filter_taps, skip_gain):
    own_rows, channels = in_gate.shape
    copies = lax.axis_size("grp")
    copy_index = lax.axis_index("grp")
    piece = own_rows // copies
    gated = in_gate.astype(jnp.float32) * values.astype(jnp.float32)
    taps_part = lax.dynamic_slice_in_dim(filter_taps, copy_index * piece, piece, axis=0)
    taps_part = taps_part.astype(jnp.float32).T
    taps_spread = lax.all_to_all(taps_part, "seq", split_axis=0, concat_axis=1, tiled=True)
    gated_spread = lax.all_to_all(gated.T, "seq", split_axis=0, concat_axis=1, tiled=True)
    taps_all = lax.all_gather(taps_spread, "grp", axis=0)
    ch = taps_all.shape[1]
    taps_all = taps_all.reshape(copies, ch, -1, piece)
    taps_full = jnp.transpose(taps_all, (1, 2, 0, 3)).reshape(ch, -1)
    n = taps_full.shape[1]
    tables = dft_tables(n // SIDE)
    spec_h = spectrum(taps_full, tables)
    spec_g = spectrum(gated_spread, tables)
    conv = inverse_prefix(spec_g, spec_h, tables, n)
    back = lax.all_to_all(conv, "seq", split_axis=1, concat_axis=0, tiled=True)
    total = back.T + skip_gain[None, :] * gated
    return (out_gate.astype(jnp.float32) * total).astype(jnp.bfloat16)


def solution(mesh):
    in_specs = (
        P(("grp", "seq"), None),
        P(("grp", "seq"), None),
        P(("grp", "seq"), None),
        P("seq", None),
        P(),
    )
    out_specs = P(("grp", "seq"), None)
    return jax.shard_map(local, mesh=mesh, in_specs=in_specs, out_specs=out_specs, check_vma=False)
```

time: 85.7 us -> 105 us (1.23)
  waiting for transfers between devices: 43.5 us -> 25 us
  blocking collectives: 0 us -> 13.3 us
  local copies, waits for them, and re-layouts: 8.2 us -> 17.3 us
  starting transfers between devices: 16.9 us -> 25.6 us
  other arithmetic: 2.51 us -> 5.58 us
  matrix products: 14 us -> 17 us
    all_to_all x1 -> x2, waiting for transfers between devices: 26.9 us -> 6.93 us  [the longest x1 6.92 us: local(): lax.all_to_all(taps_part, 'seq', split_axis=0, concat_axis=1, tiled=True)]
    all_gather x0 -> x1, blocking collectives: none -> 13.3 us  [local(): taps_all = lax.all_gather(taps_spread, 'grp', axis=0)]
    all_to_all x1 -> x2, starting transfers between devices: 11.3 us -> 15.9 us  [the longest x1 11.3 us: local(): lax.all_to_all(taps_part, 'seq', split_axis=0, concat_axis=1, tiled=True)]
    all_to_all x1, starting transfers between devices: 5.57 us -> 9.7 us  [local(): back = lax.all_to_all(conv, 'seq', split_axis=1, concat_axis=0, tiled=True)]
    transpose x0 -> x1, local copies, waits for them, and re-layouts: none -> 2.97 us  [local(): taps_full = jnp.transpose(taps_all, (1, 2, 0, 3)).reshape(ch, -1)]
    dot_general x4 -> x6, matrix products: 14 us -> 17 us  [the longest x2 6.98 us: spectrum(): jnp.einsum('bkm,mj->bkj', jnp.concatenate([b_re, b_im], axis=-1), forward...]
    unnamed x8 -> x22, local copies, waits for them, and re-layouts: 3.39 us -> 4.91 us
    all_to_all x1, waiting for transfers between devices: 16.7 us -> 18.1 us  [local(): back = lax.all_to_all(conv, 'seq', split_axis=1, concat_axis=0, tiled=True)]
  transfers between devices with their start and end apart: 2 -> 3, of which waited for: 2 -> 2; matrix products, arithmetic and copies ran while one was open for 1% -> 16% of each run, Pallas kernels for 0% -> 0%
where the time goes in v1:
time: 105 us; the launch traced here: 104 us
  starting transfers between devices  25.6 us (24%)
  waiting for transfers between devices  25 us (24%)
  local copies, waits for them, and re-layouts  17.3 us (16%)
  matrix products  17 us (16%)
  blocking collectives  13.3 us (13%)
  other arithmetic  5.58 us (5%)
    all_to_all x1, waiting for transfers between devices, local(): back = lax.all_to_all(conv, 'seq', split_axis=1, concat_axis=0, tiled=True)  18.1 us
    all_gather x1, blocking collectives, local(): taps_all = lax.all_gather(taps_spread, 'grp', axis=0)  13.3 us
    all_to_all x1, starting transfers between devices, local(): lax.all_to_all(taps_part, 'seq', split_axis=0, concat_axis=1, tiled=True)  11.3 us
    all_to_all x1, starting transfers between devices, local(): back = lax.all_to_all(conv, 'seq', split_axis=1, concat_axis=0, tiled=True)  9.7 us
    dot_general x2, matrix products, spectrum(): jnp.einsum('bkm,mj->bkj', jnp.concatenate([b_re, b_im], axis=-1), forward...  6.98 us
    all_to_all x1, waiting for transfers between devices, local(): lax.all_to_all(taps_part, 'seq', split_axis=0, concat_axis=1, tiled=True)  6.92 us
    dot_general x2, matrix products, spectrum(): a = jnp.einsum('kn,bnm->bkm', stage_a, x, precision=exact_mode)  5.55 us
    unnamed x22, local copies, waits for them, and re-layouts  4.91 us
  transfers between devices with their start and end apart: 3, of which 2 were waited for; matrix products, arithmetic and copies ran while one was open for 16% of the time, Pallas kernels for 0%

profile of v1, /device:TPU:8, one launch (start us, length us, event | category | flops | bytes accessed | tf_op | source)
XLA Modules:
  0.0 104.1 jit_solution(2851928520764787250)
XLA Ops:
  0.0 0.9 copy-done
  1.1 0.8 reshape.65
  1.9 11.3 %all-to-all-start.1 = ((f32[32,1,512]{2,1,0:T(1,128)}), f32[32,1,512]{2,1,0:T(1,128)S(1)}, u32[]{:S(2)}, u32[]{:S(2)}) async-start(f32[32,1,512]{2,1,0:T(1,128)} %reshape.65), calls=%async_computation.1 | async-start | bytes 131072 | tf_op jit(solution)/shard_map/all_to_all | solution.py:63
  13.2 1.1 %copy.32 = bf16[256,512]{0,1:T(8,128)(2,1)S(1)} copy(bf16[256,512]{1,0:T(8,128)(2,1)} %param.5) | data formatting | bytes 524288 | tf_op args[0]
  14.3 1.1 %copy.33 = bf16[256,512]{0,1:T(8,128)(2,1)S(1)} copy(bf16[256,512]{1,0:T(8,128)(2,1)} %param.6) | data formatting | bytes 524288 | tf_op args[1]
  15.4 0.9 convert_multiply_fusion
  16.3 6.9 %all-to-all-done.1 = f32[32,1,512]{2,1,0:T(1,128)S(1)} async-done(((f32[32,1,512]{2,1,0:T(1,128)}), f32[32,1,512]{2,1,0:T(1,128)S(1)}, u32[]{:S(2)}, u32[]{:S(2)}) %all-to-all-start.1) | async-done | bytes 65568 | tf_op jit(solution)/shard_map/all_to_all | solution.py:63
  23.2 4.6 %all-to-all-start = ((f32[32,16,256]{2,1,0:T(8,128)}), f32[32,16,256]{2,1,0:T(8,128)}, u32[]{:S(2)}, u32[]{:S(2)}) async-start(f32[32,16,256]{2,1,0:T(8,128)} %bitcast.1), calls=%async_computation | async-start | bytes 1048576 | tf_op jit(solution)/shard_map/all_to_all | solution.py:64
  28.1 0.7 copy.35
  29.1 0.7 copy.36
  29.8 0.8 sine_negate_fusion
  30.8 0.9 fusion.47
  31.8 0.5 broadcast.90
  32.3 0.8 reduce
  33.4 13.3 %all_gather.7 = f32[8,16,1024]{2,1,0:T(8,128)S(1)} all-gather(f32[1,16,1024]{2,1,0:T(8,128)S(1)} %all_gather.6), channel_id=1, replica_groups=mesh['seq'=32,'grp'=8] {'grp'}, dimensions={0}, use_global_device_ids=true | all-gather | bytes 589824 | tf_op jit(solution)/shard_map/all_gather | solution.py:65
  46.8 0.7 reshape.60
  47.5 3.0 %copy.40 = f32[16,32,8,32]{3,2,1,0:T(8,128)} copy(f32[16,32,8,32]{3,1,0,2:T(8,128)S(1)} %bitcast.41) | data formatting | bytes 1048576 | tf_op jit(solution)/shard_map/transpose | solution.py:68
  50.4 2.2 %reshape_reshape.3 = f32[16,64,128]{2,1,0:T(8,128)S(1)} reshape(f32[16,32,8,32]{3,2,1,0:T(8,128)} %copy.40) | data formatting | bytes 1048576 | tf_op jit(solution)/shard_map/reshape;reshape | solution.py:29
  52.7 2.6 %convolution_bitcast_fusion = f32[16,256,128]{1,2,0:T(8,128)S(1)} fusion(f32[16,64,128]{2,1,0:T(8,128)S(1)} %reshape_reshape.3, f32[128,64]{0,1:T(8,128)} %get-tuple-element.15, f32[128,64]{0,1:T(8,128)} %get-tuple-element.16), kind=kOutput, calls=%fused_computation.16 | convolution fusion | flops 402669568 | bytes 2686976 | tf_op jit(solution)/shard_map/kn,bnm->bkm/dot_general | solution.py:30
  55.3 1.4 %copy.34 = f32[16,32,256]{2,1,0:T(8,128)S(1)} copy(f32[16,32,256]{2,0,1:T(8,128)} %bitcast.2) | data formatting | bytes 1048576 | tf_op jit(solution)/shard_map/all_to_all | solution.py:64
  56.6 0.8 reshape.59
  57.5 2.9 %convolution_bitcast_fusion.1 = f32[16,256,128]{1,2,0:T(8,128)S(1)} fusion(f32[16,64,128]{2,1,0:T(8,128)} %reshape.59, f32[128,64]{0,1:T(8,128)} %get-tuple-element.15, f32[128,64]{0,1:T(8,128)} %get-tuple-element.16), kind=kOutput, calls=%fused_computation.17 | convolution fusion | flops 402669568 | bytes 2686976 | tf_op jit(solution)/shard_map/kn,bnm->bkm/dot_general | solution.py:30
  60.5 0.6 multiply_add_fusion.3
  61.3 3.5 %fusion = f32[16,128,256]{2,1,0:T(8,128)S(1)} fusion(f32[16,128,128]{1,2,0:T(8,128)S(1)} %get-tuple-element.10, f32[16,128,128]{1,2,0:T(8,128)S(1)} %get-tuple-element.9, f32[128,128]{1,0:T(8,128)S(1)} %copy-done.1, f32[128,128]{1,0:T(8,128)S(1)} %get-tuple-element.17, f32[128,128]{1,0:T(8,128)S(1)} %fusion.54), kind=kOutput, calls=%fused_computation | convolution fusion | flops 1611333632 | bytes 4390912 | tf_op jit(solution)/shard_map/bkm,mj->bkj/dot_general | solution.py:34
  64.8 3.4 %fusion.4 = f32[16,128,256]{2,1,0:T(8,128)S(1)} fusion(f32[16,128,128]{1,2,0:T(8,128)S(1)} %get-tuple-element.13, f32[16,128,128]{1,2,0:T(8,128)S(1)} %get-tuple-element.14, f32[128,128]{1,0:T(8,128)S(1)} %copy-done.1, f32[128,128]{1,0:T(8,128)S(1)} %get-tuple-element.17, f32[128,128]{1,0:T(8,128)S(1)} %fusion.54), kind=kOutput, calls=%fused_computation.4 | convolution fusion | flops 1611333632 | bytes 4390912 | tf_op jit(solution)/shard_map/bkm,mj->bkj/dot_general | solution.py:34
  68.6 2.3 %fusion.8 = f32[16,128,256]{1,2,0:T(8,128)S(1)} fusion(f32[16,128,128]{2,1,0:T(8,128)S(1)} %get-tuple-element.6, f32[16,128,128]{2,1,0:T(8,128)S(1)} %get-tuple-element.5, f32[128,128]{1,0:T(8,128)S(1)} %copy-done.1, f32[128,128]{1,0:T(8,128)S(1)} %fusion.54, f32[128,128]{1,0:T(8,128)S(1)} %get-tuple-element.17), kind=kOutput, calls=%fused_computation.8 | convolution fusion | flops 1611333632 | bytes 4390912 | tf_op jit(solution)/shard_map/bkj,jm->bkm/dot_general | solution.py:45
  71.3 0.4 copy-done.4
  71.7 2.2 %fusion.19 = f32[16,64,128]{2,1,0:T(8,128)S(1)} fusion(f32[16,128,128]{1,2,0:T(8,128)S(1)} %get-tuple-element.8, f32[16,128,128]{1,2,0:T(8,128)S(1)} %get-tuple-element.7, f32[128,64]{0,1:T(8,128)S(1)} %copy-done.4, f32[128,64]{0,1:T(8,128)S(1)} %copy-done.5), kind=kOutput, calls=%fused_computation.19 | convolution fusion | flops 403324928 | bytes 2686976 | tf_op jit(solution)/shard_map/kn,bkm->bnm/dot_general | solution.py:49
  74.0 1.1 %copy.45 = f32[16,32,256]{2,0,1:T(8,128)} copy(f32[16,32,256]{2,1,0:T(8,128)S(1)} %mul.396) | data formatting | bytes 1048576 | tf_op jit(solution)/shard_map/mul | solution.py:52
  75.1 9.7 %all-to-all-start.2 = ((f32[16,32,256]{2,0,1:T(8,128)}), f32[16,32,256]{2,0,1:T(8,128)S(1)}, u32[]{:S(2)}, u32[]{:S(2)}) async-start(f32[16,32,256]{2,0,1:T(8,128)} %copy.45), calls=%async_computation.2 | async-start | bytes 1048576 | tf_op jit(solution)/shard_map/all_to_all | solution.py:74
  85.0 18.1 %all-to-all-done.2 = f32[16,32,256]{2,0,1:T(8,128)S(1)} async-done(((f32[16,32,256]{2,0,1:T(8,128)}), f32[16,32,256]{2,0,1:T(8,128)S(1)}, u32[]{:S(2)}, u32[]{:S(2)}) %all-to-all-start.2) | async-done | bytes 524320 | tf_op jit(solution)/shard_map/all_to_all | solution.py:74
  103.2 0.8 copy.46
  (29 shorter events, 2.6 us)
Async XLA Ops:
  0.0 1.0 copy-start
  1.9 21.3 %all-to-all-start.1 = ((f32[32,1,512]{2,1,0:T(1,128)}), f32[32,1,512]{2,1,0:T(1,128)S(1)}, u32[]{:S(2)}, u32[]{:S(2)}) async-start(f32[32,1,512]{2,1,0:T(1,128)} %reshape.65), calls=%async_computation.1 | async-start | bytes 131072 | tf_op jit(solution)/shard_map/all_to_all | solution.py:63
  23.2 32.1 %all-to-all-start = ((f32[32,16,256]{2,1,0:T(8,128)}), f32[32,16,256]{2,1,0:T(8,128)}, u32[]{:S(2)}, u32[]{:S(2)}) async-start(f32[32,16,256]{2,1,0:T(8,128)} %bitcast.1), calls=%async_computation | async-start | bytes 1048576 | tf_op jit(solution)/shard_map/all_to_all | solution.py:64
  57.5 3.0 %copy-start.2 = (f32[128,128]{0,1:T(8,128)S(1)}, f32[128,128]{0,1:T(8,128)}, u32[]{:S(2)}) copy-start(f32[128,128]{0,1:T(8,128)} %copy.35) | copy-start | bytes 196612
  57.5 3.0 %copy-start.3 = (f32[128,128]{0,1:T(8,128)S(1)}, f32[128,128]{0,1:T(8,128)}, u32[]{:S(2)}) copy-start(f32[128,128]{0,1:T(8,128)} %copy.36) | copy-start | bytes 196612
  60.4 0.8 copy-start.1
  70.9 0.8 copy-start.4
  70.9 0.8 copy-start.5
  73.8 11.0 %copy-start.6 = (bf16[256,512]{1,0:T(8,128)(2,1)S(1)}, bf16[256,512]{1,0:T(8,128)(2,1)}, u32[]{:S(2)}) copy-start(bf16[256,512]{1,0:T(8,128)(2,1)} %param.7) | copy-start | bytes 786436
  73.9 29.2 %copy-start.7 = (f32[512]{0:T(512)S(1)}, f32[512]{0:T(512)}, u32[]{:S(2)}) copy-start(f32[512]{0:T(512)} %param.9) | copy-start | bytes 6148
  75.1 27.9 %all-to-all-start.2 = ((f32[16,32,256]{2,0,1:T(8,128)}), f32[16,32,256]{2,0,1:T(8,128)S(1)}, u32[]{:S(2)}, u32[]{:S(2)}) async-start(f32[16,32,256]{2,0,1:T(8,128)} %copy.45), calls=%async_computation.2 | async-start | bytes 1048576 | tf_op jit(solution)/shard_map/all_to_all | solution.py:74

commit v2 on v0

--- a/solution.py
+++ b/solution.py
@@ -3,7 +3,7 @@
 from jax import lax
 from jax.sharding import PartitionSpec as P
 
-exact_mode = lax.Precision.HIGHEST
+exact_mode = lax.Precision.HIGH
 
 
 def angle_table(rows, cols, period):

time: 85.7 us -> 78.9 us (0.921)
  matrix products: 14 us -> 7.14 us
    dot_general x1, matrix products: 7.19 us -> 3.58 us  [causal_conv(): jnp.einsum('bkm,mj->bkj', jnp.concatenate([b_re, b_im], axis=-1), forward...]
    dot_general x1, matrix products: 3.47 us -> 1.83 us  [causal_conv(): a = jnp.einsum('kn,bnm->bkm', stage_a, x, precision=exact_mode)]
    dot_general x1, matrix products: 1.87 us -> 1.01 us  [causal_conv(): q = jnp.einsum('bkj,jm->bkm', prod, inverse_b, precision=exact_mode)]
  transfers between devices with their start and end apart: 2 -> 2, of which waited for: 2 -> 2; matrix products, arithmetic and copies ran while one was open for 1% -> 2% of each run, Pallas kernels for 0% -> 0%
where the time goes in v2:
time: 78.9 us; the launch traced here: 78.5 us
  waiting for transfers between devices  43.5 us (55%)
  starting transfers between devices  16.9 us (21%)
  local copies, waits for them, and re-layouts  8.2 us (10%)
  matrix products  7.14 us (9%)
  other arithmetic  2.51 us (3%)
    all_to_all x1, waiting for transfers between devices, local(): lax.all_to_all(both, 'seq', split_axis=1, concat_axis=2, tiled=True)  26.9 us
    all_to_all x1, waiting for transfers between devices, local(): back = lax.all_to_all(conv, 'seq', split_axis=1, concat_axis=0, tiled=True)  16.7 us
    all_to_all x1, starting transfers between devices, local(): lax.all_to_all(both, 'seq', split_axis=1, concat_axis=2, tiled=True)  11.3 us
    all_to_all x1, starting transfers between devices, local(): back = lax.all_to_all(conv, 'seq', split_axis=1, concat_axis=0, tiled=True)  5.58 us
    dot_general x1, matrix products, causal_conv(): jnp.einsum('bkm,mj->bkj', jnp.concatenate([b_re, b_im], axis=-1), forward...  3.58 us
    unnamed x8, local copies, waits for them, and re-layouts  3.39 us
    dot_general x1, matrix products, causal_conv(): a = jnp.einsum('kn,bnm->bkm', stage_a, x, precision=exact_mode)  1.83 us
    another operation x1, local copies, waits for them, and re-layouts, local(): both = jnp.stack([gated.T, taps.T])  1.78 us
  transfers between devices with their start and end apart: 2, of which 2 were waited for; matrix products, arithmetic and copies ran while one was open for 2% of the time, Pallas kernels for 0%

profile of v2, /device:TPU:8, one launch (start us, length us, event | category | flops | bytes accessed | tf_op | source)
XLA Modules:
  0.0 78.5 jit_solution(8276583197447418815)
XLA Ops:
  0.0 1.1 %copy.22 = bf16[256,512]{0,1:T(8,128)(2,1)S(1)} copy(bf16[256,512]{1,0:T(8,128)(2,1)} %param.5) | data formatting | bytes 524288 | tf_op args[0]
  1.1 1.1 %copy.23 = bf16[256,512]{0,1:T(8,128)(2,1)S(1)} copy(bf16[256,512]{1,0:T(8,128)(2,1)} %param.6) | data formatting | bytes 524288 | tf_op args[1]
  2.2 1.1 %copy.24 = bf16[256,512]{0,1:T(8,128)(2,1)S(1)} copy(bf16[256,512]{1,0:T(8,128)(2,1)} %param.8) | data formatting | bytes 524288 | tf_op args[3]
  3.3 0.1 fusion.20
  3.4 0.1 pad_maximum_fusion
  3.5 1.8 %copy.25 = f32[2,512,256]{2,0,1:T(2,128)} copy(f32[2,512,256]{2,1,0:T(8,128)S(1)} %pad_maximum_fusion) | data formatting | bytes 2097152 | tf_op jit(solution)/shard_map/stack | solution.py:54
  5.2 11.3 %all-to-all-start = ((f32[2,512,256]{2,0,1:T(2,128)}), f32[2,512,256]{2,0,1:T(2,128)S(1)}, u32[]{:S(2)}, u32[]{:S(2)}) async-start(f32[2,512,256]{2,0,1:T(2,128)} %copy.25), calls=%async_computation | async-start | bytes 2097152 | tf_op jit(solution)/shard_map/all_to_all | solution.py:55
  16.6 0.3 fusion.47
  16.8 0.1 copy.28
  16.9 0.1 copy.29
  17.0 0.2 sine_negate_fusion
  17.2 0.3 fusion.52
  17.5 0.3 fusion.45
  17.7 26.9 %all-to-all-done = f32[2,512,256]{2,0,1:T(2,128)S(1)} async-done(((f32[2,512,256]{2,0,1:T(2,128)}), f32[2,512,256]{2,0,1:T(2,128)S(1)}, u32[]{:S(2)}, u32[]{:S(2)}) %all-to-all-start) | async-done | bytes 1048608 | tf_op jit(solution)/shard_map/all_to_all | solution.py:55
  44.6 0.1 copy.26
  44.7 0.6 copy.27
  45.3 0.1 reshape.48
  45.4 1.8 %convolution_bitcast_fusion = f32[32,256,128]{1,2,0:T(8,128)S(1)} fusion(f32[32,64,128]{2,1,0:T(8,128)S(1)} %reshape.48, f32[128,64]{0,1:T(8,128)S(1)} %get-tuple-element.11, f32[128,64]{0,1:T(8,128)S(1)} %get-tuple-element.12), kind=kOutput, calls=%fused_computation.4 | convolution fusion | flops 402669568 | bytes 5308416 | tf_op jit(solution)/shard_map/kn,bnm->bkm/dot_general | solution.py:31
  47.2 0.6 multiply_add_fusion
  47.9 3.6 %fusion = f32[32,128,256]{2,1,0:T(8,128)S(1)} fusion(f32[32,128,128]{1,2,0:T(8,128)S(1)} %get-tuple-element.6, f32[32,128,128]{1,2,0:T(8,128)S(1)} %get-tuple-element.5, f32[128,128]{1,0:T(8,128)S(1)} %get-tuple-element.14, f32[128,128]{1,0:T(8,128)S(1)} %get-tuple-element.13, f32[128,128]{1,0:T(8,128)S(1)} %fusion.52), kind=kOutput, calls=%fused_computation | convolution fusion | flops 1611857920 | bytes 8585216 | tf_op jit(solution)/shard_map/bkm,mj->bkj/dot_general | solution.py:35
  51.4 0.3 multiply_subtract_fusion.2
  51.8 1.0 %fusion.4 = f32[16,128,256]{2,1,0:T(8,128)S(1)} fusion(f32[16,128,128]{2,1,0:T(8,128)S(1)} %get-tuple-element.8, f32[16,128,128]{2,1,0:T(8,128)S(1)} %get-tuple-element.7, f32[128,128]{1,0:T(8,128)S(1)} %get-tuple-element.14, f32[128,128]{1,0:T(8,128)S(1)} %fusion.52, f32[128,128]{1,0:T(8,128)S(1)} %get-tuple-element.13), kind=kOutput, calls=%fused_computation.5 | convolution fusion | flops 806027264 | bytes 4390912 | tf_op jit(solution)/shard_map/bkj,jm->bkm/dot_general | solution.py:41
  52.8 0.3 multiply_subtract_fusion.1
  53.1 0.7 fusion.15
  53.8 0.0 copy-start
  53.8 0.1 mul.326
  54.0 1.1 %copy.31 = f32[16,32,256]{2,0,1:T(8,128)} copy(f32[16,32,256]{2,1,0:T(8,128)S(1)} %mul.326) | data formatting | bytes 1048576 | tf_op jit(solution)/shard_map/mul | solution.py:48
  55.1 5.6 %all-to-all-start.1 = ((f32[16,32,256]{2,0,1:T(8,128)}), f32[16,32,256]{2,0,1:T(8,128)S(1)}, u32[]{:S(2)}, u32[]{:S(2)}) async-start(f32[16,32,256]{2,0,1:T(8,128)} %copy.31), calls=%async_computation.1 | async-start | bytes 1048576 | tf_op jit(solution)/shard_map/all_to_all | solution.py:57
  60.7 0.1 copy.21
  60.8 16.7 %all-to-all-done.1 = f32[16,32,256]{2,0,1:T(8,128)S(1)} async-done(((f32[16,32,256]{2,0,1:T(8,128)}), f32[16,32,256]{2,0,1:T(8,128)S(1)}, u32[]{:S(2)}, u32[]{:S(2)}) %all-to-all-start.1) | async-done | bytes 524320 | tf_op jit(solution)/shard_map/all_to_all | solution.py:57
  77.5 0.2 fusion.19
  77.7 0.8 %copy.32 = bf16[256,512]{1,0:T(8,128)(2,1)} copy(bf16[256,512]{0,1:T(8,128)(2,1)S(1)} %fusion.19) | data formatting | bytes 524288 | tf_op jit(solution)/shard_map/convert_element_type | solution.py:59
  (4 shorter events, 0.0 us)
Async XLA Ops:
  5.2 39.4 %all-to-all-start = ((f32[2,512,256]{2,0,1:T(2,128)}), f32[2,512,256]{2,0,1:T(2,128)S(1)}, u32[]{:S(2)}, u32[]{:S(2)}) async-start(f32[2,512,256]{2,0,1:T(2,128)} %copy.25), calls=%async_computation | async-start | bytes 2097152 | tf_op jit(solution)/shard_map/all_to_all | solution.py:55
  53.8 6.9 %copy-start = (bf16[256,512]{1,0:T(8,128)(2,1)S(1)}, bf16[256,512]{1,0:T(8,128)(2,1)}, u32[]{:S(2)}) copy-start(bf16[256,512]{1,0:T(8,128)(2,1)} %param.7) | copy-start | bytes 786436
  53.8 23.7 %copy-start.1 = (f32[512]{0:T(512)S(1)}, f32[512]{0:T(512)}, u32[]{:S(2)}) copy-start(f32[512]{0:T(512)} %param.9) | copy-start | bytes 6148
  55.1 22.4 %all-to-all-start.1 = ((f32[16,32,256]{2,0,1:T(8,128)}), f32[16,32,256]{2,0,1:T(8,128)S(1)}, u32[]{:S(2)}, u32[]{:S(2)}) async-start(f32[16,32,256]{2,0,1:T(8,128)} %copy.31), calls=%async_computation.1 | async-start | bytes 1048576 | tf_op jit(solution)/shard_map/all_to_all | solution.py:57

commit v3 on v1

--- a/solution.py
+++ b/solution.py
@@ -3,7 +3,7 @@
 from jax import lax
 from jax.sharding import PartitionSpec as P
 
-exact_mode = lax.Precision.HIGHEST
+exact_mode = lax.Precision.HIGH
 SIDE = 128
 
 
@@ -55,21 +55,24 @@
 def local(in_gate, values, out_gate, filter_taps, skip_gain):
     own_rows, channels = in_gate.shape
     copies = lax.axis_size("grp")
-    copy_index = lax.axis_index("grp")
-    piece = own_rows // copies
+    core = lax.axis_index("grp") % 2
+    half = own_rows // 2
     gated = in_gate.astype(jnp.float32) * values.astype(jnp.float32)
-    taps_part = lax.dynamic_slice_in_dim(filter_taps, copy_index * piece, piece, axis=0)
-    taps_part = taps_part.astype(jnp.float32).T
-    taps_spread = lax.all_to_all(taps_part, "seq", split_axis=0, concat_axis=1, tiled=True)
-    gated_spread = lax.all_to_all(gated.T, "seq", split_axis=0, concat_axis=1, tiled=True)
-    taps_all = lax.all_gather(taps_spread, "grp", axis=0)
-    ch = taps_all.shape[1]
-    taps_all = taps_all.reshape(copies, ch, -1, piece)
-    taps_full = jnp.transpose(taps_all, (1, 2, 0, 3)).reshape(ch, -1)
-    n = taps_full.shape[1]
+    taps_half = lax.dynamic_slice_in_dim(filter_taps, core * half, half, axis=0)
+    payload = jnp.concatenate([gated.T, taps_half.astype(jnp.float32).T], axis=1)
+    spread = lax.all_to_all(payload, "seq", split_axis=0, concat_axis=1, tiled=True)
+    ch = spread.shape[0]
+    spread = spread.reshape(ch, -1, own_rows + half)
+    gated_spread = spread[:, :, :own_rows].reshape(ch, -1)
+    mine = spread[:, :, own_rows:]
+    theirs = lax.ppermute(mine, "grp", [(g, g ^ 1) for g in range(copies)])
+    n = gated_spread.shape[1]
     tables = dft_tables(n // SIDE)
+    spec_g = spectrum(gated_spread, tables)
+    first = jnp.where(core == 0, mine, theirs)
+    second = jnp.where(core == 0, theirs, mine)
+    taps_full = jnp.stack([first, second], axis=2).reshape(ch, -1)
     spec_h = spectrum(taps_full, tables)
-    spec_g = spectrum(gated_spread, tables)
     conv = inverse_prefix(spec_g, spec_h, tables, n)
     back = lax.all_to_all(conv, "seq", split_axis=1, concat_axis=0, tiled=True)
     total = back.T + skip_gain[None, :] * gated

time: 105 us -> 75.1 us (0.72)
  waiting for transfers between devices: 25 us -> 39.7 us
  blocking collectives: 13.3 us -> 0 us
  local copies, waits for them, and re-layouts: 17.3 us -> 6.48 us
  matrix products: 17 us -> 7.88 us
  starting transfers between devices: 25.6 us -> 16.7 us
  other arithmetic: 5.58 us -> 3.73 us
    all_to_all x2 -> x1, waiting for transfers between devices: 6.93 us -> 21.5 us  [local(): lax.all_to_all(payload, 'seq', split_axis=0, concat_axis=1, tiled=True)]
    all_gather x1 -> x0, blocking collectives: 13.3 us -> none  [local(): taps_all = lax.all_gather(taps_spread, 'grp', axis=0)]
    all_to_all x2 -> x1, starting transfers between devices: 15.9 us -> 11.3 us  [local(): lax.all_to_all(payload, 'seq', split_axis=0, concat_axis=1, tiled=True)]
    all_to_all x1, starting transfers between devices: 9.7 us -> 5.13 us  [local(): back = lax.all_to_all(conv, 'seq', split_axis=1, concat_axis=0, tiled=True)]
    dot_general x2, matrix products: 5.55 us -> 2.05 us  [spectrum(): a = jnp.einsum('kn,bnm->bkm', stage_a, x, precision=exact_mode)]
    dot_general x2, matrix products: 6.98 us -> 3.69 us  [spectrum(): jnp.einsum('bkm,mj->bkj', jnp.concatenate([b_re, b_im], axis=-1), forward...]
    transpose x1 -> x0, local copies, waits for them, and re-layouts: 2.97 us -> none  [local(): taps_full = jnp.transpose(taps_all, (1, 2, 0, 3)).reshape(ch, -1)]
    another operation x1, local copies, waits for them, and re-layouts: 2.22 us -> 0.04 us  [spectrum(): x = signal.reshape(ch, n // SIDE, SIDE)]
  transfers between devices with their start and end apart: 3 -> 3, of which waited for: 2 -> 3; matrix products, arithmetic and copies ran while one was open for 16% -> 4% of each run, Pallas kernels for 0% -> 0%
where the time goes in v3:
time: 75.1 us; the launch traced here: 74.8 us
  waiting for transfers between devices  39.7 us (53%)
  starting transfers between devices  16.7 us (22%)
  matrix products  7.88 us (10%)
  local copies, waits for them, and re-layouts  6.48 us (9%)
  other arithmetic  3.73 us (5%)
    all_to_all x1, waiting for transfers between devices, local(): lax.all_to_all(payload, 'seq', split_axis=0, concat_axis=1, tiled=True)  21.5 us
    all_to_all x1, waiting for transfers between devices, local(): back = lax.all_to_all(conv, 'seq', split_axis=1, concat_axis=0, tiled=True)  18.1 us
    all_to_all x1, starting transfers between devices, local(): lax.all_to_all(payload, 'seq', split_axis=0, concat_axis=1, tiled=True)  11.3 us
    all_to_all x1, starting transfers between devices, local(): back = lax.all_to_all(conv, 'seq', split_axis=1, concat_axis=0, tiled=True)  5.13 us
    dot_general x2, matrix products, spectrum(): jnp.einsum('bkm,mj->bkj', jnp.concatenate([b_re, b_im], axis=-1), forward...  3.69 us
    unnamed x10, local copies, waits for them, and re-layouts  3.38 us
    dot_general x2, matrix products, spectrum(): a = jnp.einsum('kn,bnm->bkm', stage_a, x, precision=exact_mode)  2.05 us
  transfers between devices with their start and end apart: 3, of which 3 were waited for; matrix products, arithmetic and copies ran while one was open for 4% of the time, Pallas kernels for 0%

profile of v3, /device:TPU:8, one launch (start us, length us, event | category | flops | bytes accessed | tf_op | source)
XLA Modules:
  0.0 74.8 jit_solution(10463541401204154834)
XLA Ops:
  0.0 0.9 %copy-done = bf16[256,512]{1,0:T(8,128)(2,1)S(1)} copy-done((bf16[256,512]{1,0:T(8,128)(2,1)S(1)}, bf16[256,512]{1,0:T(8,128)(2,1)}, u32[]{:S(2)}) %copy-start) | copy-done | bytes 262168
  1.0 0.1 copy.35
  1.1 1.1 %copy.17 = bf16[256,512]{0,1:T(8,128)(2,1)S(1)} copy(bf16[256,512]{1,0:T(8,128)(2,1)} %param.5) | data formatting | bytes 524288 | tf_op args[0]
  2.2 1.1 %copy.18 = bf16[256,512]{0,1:T(8,128)(2,1)S(1)} copy(bf16[256,512]{1,0:T(8,128)(2,1)} %param.6) | data formatting | bytes 524288 | tf_op args[1]
  3.4 1.0 %pad_maximum_fusion = f32[512,384]{1,0:T(8,128)} fusion(f32[512,128]{1,0:T(8,128)S(1)} %convert_bitcast_fusion, f32[512,256]{1,0:T(8,128)S(1)} %fusion.24), kind=kLoop, calls=%fused_computation.28 | loop fusion | flops 196608 | bytes 1572864 | tf_op jit(solution)/shard_map/concatenate | solution.py:62
  4.3 11.3 %all-to-all-start = ((f32[32,16,384]{2,1,0:T(8,128)}), f32[32,16,384]{2,1,0:T(8,128)S(1)}, u32[]{:S(2)}, u32[]{:S(2)}) async-start(f32[32,16,384]{2,1,0:T(8,128)} %bitcast.2), calls=%async_computation | async-start | bytes 1572864 | tf_op jit(solution)/shard_map/all_to_all | solution.py:63
  15.6 0.3 fusion.51
  16.0 0.3 fusion.50
  16.4 0.2 sine_negate_fusion
  16.5 0.3 fusion.55
  16.8 0.3 fusion.48
  17.1 21.5 %all-to-all-done = f32[32,16,384]{2,1,0:T(8,128)S(1)} async-done(((f32[32,16,384]{2,1,0:T(8,128)}), f32[32,16,384]{2,1,0:T(8,128)S(1)}, u32[]{:S(2)}, u32[]{:S(2)}) %all-to-all-start) | async-done | bytes 786464 | tf_op jit(solution)/shard_map/all_to_all | solution.py:63
  38.6 0.3 collective-permute-start
  38.9 0.3 copy.20
  39.2 1.0 %convolution_bitcast_fusion.1 = f32[16,256,128]{1,2,0:T(8,128)S(1)} fusion(f32[16,64,128]{2,1,0:T(8,128)S(1)} %reshape_reshape.6, f32[128,64]{0,1:T(8,128)S(1)} %get-tuple-element.17, f32[128,64]{0,1:T(8,128)S(1)} %get-tuple-element.18), kind=kOutput, calls=%fused_computation.17 | convolution fusion | flops 201342976 | bytes 2686976 | tf_op jit(solution)/shard_map/kn,bnm->bkm/dot_general | solution.py:30
  40.3 0.1 collective-permute-done
  40.5 0.4 copy.24
  40.9 1.0 %convolution_bitcast_fusion = f32[16,256,128]{1,2,0:T(8,128)S(1)} fusion(f32[16,64,128]{2,1,0:T(8,128)S(1)} %bitcast.44, f32[128,64]{0,1:T(8,128)S(1)} %get-tuple-element.17, f32[128,64]{0,1:T(8,128)S(1)} %get-tuple-element.18), kind=kOutput, calls=%fused_computation.16 | convolution fusion | flops 201342976 | bytes 2686976 | tf_op jit(solution)/shard_map/kn,bnm->bkm/dot_general | solution.py:30
  41.9 0.6 multiply_add_fusion.3
  42.6 1.8 %fusion = f32[16,128,256]{2,1,0:T(8,128)S(1)} fusion(f32[16,128,128]{1,2,0:T(8,128)S(1)} %get-tuple-element.10, f32[16,128,128]{1,2,0:T(8,128)S(1)} %get-tuple-element.9, f32[128,128]{1,0:T(8,128)S(1)} %get-tuple-element.20, f32[128,128]{1,0:T(8,128)S(1)} %get-tuple-element.19, f32[128,128]{1,0:T(8,128)S(1)} %fusion.55), kind=kOutput, calls=%fused_computation | convolution fusion | flops 806027264 | bytes 4390912 | tf_op jit(solution)/shard_map/bkm,mj->bkj/dot_general | solution.py:34
  44.4 1.8 %fusion.4 = f32[16,128,256]{2,1,0:T(8,128)S(1)} fusion(f32[16,128,128]{1,2,0:T(8,128)S(1)} %get-tuple-element.15, f32[16,128,128]{1,2,0:T(8,128)S(1)} %get-tuple-element.16, f32[128,128]{1,0:T(8,128)S(1)} %get-tuple-element.20, f32[128,128]{1,0:T(8,128)S(1)} %get-tuple-element.19, f32[128,128]{1,0:T(8,128)S(1)} %fusion.55), kind=kOutput, calls=%fused_computation.4 | convolution fusion | flops 806027264 | bytes 4390912 | tf_op jit(solution)/shard_map/bkm,mj->bkj/dot_general | solution.py:34
  46.3 0.3 multiply_subtract_fusion.1
  46.6 1.1 %fusion.8 = f32[16,128,256]{1,2,0:T(8,128)S(1)} fusion(f32[16,128,128]{2,1,0:T(8,128)S(1)} %get-tuple-element.6, f32[16,128,128]{2,1,0:T(8,128)S(1)} %get-tuple-element.5, f32[128,128]{1,0:T(8,128)S(1)} %get-tuple-element.20, f32[128,128]{1,0:T(8,128)S(1)} %fusion.55, f32[128,128]{1,0:T(8,128)S(1)} %get-tuple-element.19), kind=kOutput, calls=%fused_computation.8 | convolution fusion | flops 806027264 | bytes 4390912 | tf_op jit(solution)/shard_map/bkj,jm->bkm/dot_general | solution.py:45
  47.7 0.3 multiply_subtract_fusion
  48.0 1.1 %fusion.19 = f32[16,64,128]{2,1,0:T(8,128)S(1)} fusion(f32[16,128,128]{1,2,0:T(8,128)S(1)} %get-tuple-element.8, f32[16,128,128]{1,2,0:T(8,128)S(1)} %get-tuple-element.7, f32[128,64]{0,1:T(8,128)S(1)} %get-tuple-element.17, f32[128,64]{0,1:T(8,128)S(1)} %get-tuple-element.18), kind=kOutput, calls=%fused_computation.19 | convolution fusion | flops 201998336 | bytes 2686976 | tf_op jit(solution)/shard_map/kn,bkm->bnm/dot_general | solution.py:49
  49.1 0.1 mul.396
  49.3 1.1 %copy.29 = f32[16,32,256]{2,0,1:T(8,128)} copy(f32[16,32,256]{2,1,0:T(8,128)S(1)} %mul.396) | data formatting | bytes 1048576 | tf_op jit(solution)/shard_map/mul | solution.py:52
  50.4 5.1 %all-to-all-start.1 = ((f32[16,32,256]{2,0,1:T(8,128)}), f32[16,32,256]{2,0,1:T(8,128)S(1)}, u32[]{:S(2)}, u32[]{:S(2)}) async-start(f32[16,32,256]{2,0,1:T(8,128)} %copy.29), calls=%async_computation.1 | async-start | bytes 1048576 | tf_op jit(solution)/shard_map/all_to_all | solution.py:77
  55.5 0.1 copy.16
  55.7 18.1 %all-to-all-done.1 = f32[16,32,256]{2,0,1:T(8,128)S(1)} async-done(((f32[16,32,256]{2,0,1:T(8,128)}), f32[16,32,256]{2,0,1:T(8,128)S(1)}, u32[]{:S(2)}, u32[]{:S(2)}) %all-to-all-start.1) | async-done | bytes 524320 | tf_op jit(solution)/shard_map/all_to_all | solution.py:77
  73.8 0.2 fusion.23
  73.9 0.8 %copy.30 = bf16[256,512]{1,0:T(8,128)(2,1)} copy(bf16[256,512]{0,1:T(8,128)(2,1)S(1)} %fusion.23) | data formatting | bytes 524288 | tf_op jit(solution)/shard_map/convert_element_type | solution.py:79
  (15 shorter events, 0.5 us)
Async XLA Ops:
  0.0 1.0 %copy-start = (bf16[256,512]{1,0:T(8,128)(2,1)S(1)}, bf16[256,512]{1,0:T(8,128)(2,1)}, u32[]{:S(2)}) copy-start(bf16[256,512]{1,0:T(8,128)(2,1)} %param.8) | copy-start | bytes 786436
  4.3 34.2 %all-to-all-start = ((f32[32,16,384]{2,1,0:T(8,128)}), f32[32,16,384]{2,1,0:T(8,128)S(1)}, u32[]{:S(2)}, u32[]{:S(2)}) async-start(f32[32,16,384]{2,1,0:T(8,128)} %bitcast.2), calls=%async_computation | async-start | bytes 1572864 | tf_op jit(solution)/shard_map/all_to_all | solution.py:63
  38.6 1.8 %collective-permute-start = (f32[16,32,128]{2,0,1:T(8,128)S(1)}, f32[16,32,128]{2,0,1:T(8,128)S(1)}, u32[]{:S(2)}, u32[]{:S(2)}) collective-permute-start(f32[16,32,128]{2,0,1:T(8,128)S(1)} %slice.52), channel_id=1, source_target_pairs={{0,1},{1,0},{2,3},{3,2},{4,5},{5,4},{6,7},{7,6},{8,9},{9,8},{10,11... | collective-permute-start | bytes 786440 | tf_op jit(solution)/shard_map/ppermute | solution.py:68
  49.1 6.4 %copy-start.1 = (bf16[256,512]{1,0:T(8,128)(2,1)S(1)}, bf16[256,512]{1,0:T(8,128)(2,1)}, u32[]{:S(2)}) copy-start(bf16[256,512]{1,0:T(8,128)(2,1)} %param.7) | copy-start | bytes 786436
  49.1 24.7 %copy-start.2 = (f32[512]{0:T(512)S(1)}, f32[512]{0:T(512)}, u32[]{:S(2)}) copy-start(f32[512]{0:T(512)} %param.9) | copy-start | bytes 6148
  50.4 23.4 %all-to-all-start.1 = ((f32[16,32,256]{2,0,1:T(8,128)}), f32[16,32,256]{2,0,1:T(8,128)S(1)}, u32[]{:S(2)}, u32[]{:S(2)}) async-start(f32[16,32,256]{2,0,1:T(8,128)} %copy.29), calls=%async_computation.1 | async-start | bytes 1048576 | tf_op jit(solution)/shard_map/all_to_all | solution.py:77

commit v4 on v3

--- a/solution.py
+++ b/solution.py
@@ -1,6 +1,8 @@
 import jax
 import jax.numpy as jnp
 from jax import lax
+from jax.experimental import pallas as pl
+from jax.experimental.pallas import tpu as pltpu
 from jax.sharding import PartitionSpec as P
 
 exact_mode = lax.Precision.HIGH
@@ -52,14 +54,37 @@
     return y.reshape(ch, n) * (1.0 / (SIDE * SIDE))
 
 
+def prologue_kernel(gate_ref, values_ref, taps_ref, out_ref):
+    rows = gate_ref.shape[0]
+    gated = gate_ref[...].astype(jnp.float32) * values_ref[...].astype(jnp.float32)
+    out_ref[:, :rows] = gated.T
+    out_ref[:, rows:] = taps_ref[...].astype(jnp.float32).T
+
+
+def epilogue_kernel(back_ref, gate_ref, values_ref, out_gate_ref, skip_ref, out_ref):
+    gated = gate_ref[...].astype(jnp.float32) * values_ref[...].astype(jnp.float32)
+    total = back_ref[...].T + skip_ref[...] * gated
+    out_ref[...] = (out_gate_ref[...].astype(jnp.float32) * total).astype(out_ref.dtype)
+
+
+def vmem_call(kernel, out_shape, count):
+    return pl.pallas_call(
+        kernel,
+        out_shape=out_shape,
+        in_specs=[pl.BlockSpec(memory_space=pltpu.VMEM)] * count,
+        out_specs=pl.BlockSpec(memory_space=pltpu.VMEM),
+    )
+
+
 def local(in_gate, values, out_gate, filter_taps, skip_gain):
     own_rows, channels = in_gate.shape
     copies = lax.axis_size("grp")
     core = lax.axis_index("grp") % 2
     half = own_rows // 2
-    gated = in_gate.astype(jnp.float32) * values.astype(jnp.float32)
     taps_half = lax.dynamic_slice_in_dim(filter_taps, core * half, half, axis=0)
-    payload = jnp.concatenate([gated.T, taps_half.astype(jnp.float32).T], axis=1)
+    payload = vmem_call(
+        prologue_kernel, jax.ShapeDtypeStruct((channels, own_rows + half), jnp.float32), 3
+    )(in_gate, values, taps_half)
     spread = lax.all_to_all(payload, "seq", split_axis=0, concat_axis=1, tiled=True)
     ch = spread.shape[0]
     spread = spread.reshape(ch, -1, own_rows + half)
@@ -75,8 +100,9 @@
     spec_h = spectrum(taps_full, tables)
     conv = inverse_prefix(spec_g, spec_h, tables, n)
     back = lax.all_to_all(conv, "seq", split_axis=1, concat_axis=0, tiled=True)
-    total = back.T + skip_gain[None, :] * gated
-    return (out_gate.astype(jnp.float32) * total).astype(jnp.bfloat16)
+    return vmem_call(epilogue_kernel, jax.ShapeDtypeStruct(in_gate.shape, jnp.bfloat16), 5)(
+        back, in_gate, values, out_gate, skip_gain.reshape(1, channels)
+    )
 
 
 def solution(mesh):

time: 75.1 us -> 74.8 us (level)
  blocking collectives: 0 us -> 23.3 us
  waiting for transfers between devices: 39.7 us -> 21.6 us
  starting transfers between devices: 16.7 us -> 11.6 us
  Pallas kernels: 0 us -> 4.37 us
  local copies, waits for them, and re-layouts: 6.48 us -> 3.07 us
  other arithmetic: 3.73 us -> 2.54 us
    all_to_all x0 -> x1, blocking collectives: none -> 23.3 us  [local(): back = lax.all_to_all(conv, 'seq', split_axis=1, concat_axis=0, tiled=True)]
    all_to_all x1 -> x0, waiting for transfers between devices: 18.1 us -> none  [local(): back = lax.all_to_all(conv, 'seq', split_axis=1, concat_axis=0, tiled=True)]
    all_to_all x1 -> x0, starting transfers between devices: 5.13 us -> none  [local(): back = lax.all_to_all(conv, 'seq', split_axis=1, concat_axis=0, tiled=True)]
    pallas_call x0 -> x2, Pallas kernels: none -> 4.37 us  [the longest x1 2.19 us: local(): vmem_call(epilogue_kernel, jax.ShapeDtypeStruct(in_gate.shape, jnp.bfloat...]
    unnamed x10 -> x2, local copies, waits for them, and re-layouts: 3.38 us -> 0.95 us
    concatenate x1 -> x0, other arithmetic: 0.95 us -> none  [local(): jnp.concatenate([gated.T, taps_half.astype(jnp.float32).T], axis=1)]
    convert_element_type x1 -> x0, local copies, waits for them, and re-layouts: 0.84 us -> none  [local(): return (out_gate.astype(jnp.float32) * total).astype(jnp.bfloat16)]
    mul x2, local copies, waits for them, and re-layouts: 1.25 us -> 0.46 us  [inverse_prefix(): return y.reshape(ch, n) * (1.0 / (SIDE * SIDE))]
  transfers between devices with their start and end apart: 3 -> 2, of which waited for: 3 -> 2; matrix products, arithmetic and copies ran while one was open for 4% -> 4% of each run, Pallas kernels for 0% -> 0%
where the time goes in v4:
time: 74.8 us; the launch traced here: 74.5 us
  blocking collectives  23.3 us (31%)
  waiting for transfers between devices  21.6 us (29%)
  starting transfers between devices  11.6 us (16%)
  matrix products  7.88 us (11%)
  Pallas kernels  4.37 us (6%)
  local copies, waits for them, and re-layouts  3.07 us (4%)
  other arithmetic  2.54 us (3%)
    all_to_all x1, blocking collectives, local(): back = lax.all_to_all(conv, 'seq', split_axis=1, concat_axis=0, tiled=True)  23.3 us
    all_to_all x1, waiting for transfers between devices, local(): lax.all_to_all(payload, 'seq', split_axis=0, concat_axis=1, tiled=True)  21.5 us
    all_to_all x1, starting transfers between devices, local(): lax.all_to_all(payload, 'seq', split_axis=0, concat_axis=1, tiled=True)  11.3 us
    dot_general x2, matrix products, spectrum(): jnp.einsum('bkm,mj->bkj', jnp.concatenate([b_re, b_im], axis=-1), forward...  3.69 us
    pallas_call x1, Pallas kernels, local(): vmem_call(epilogue_kernel, jax.ShapeDtypeStruct(in_gate.shape, jnp.bfloat...  2.19 us
    pallas_call x1, Pallas kernels, local(): vmem_call(prologue_kernel, jax.ShapeDtypeStruct((channels, own_rows + hal...  2.18 us
    dot_general x2, matrix products, spectrum(): a = jnp.einsum('kn,bnm->bkm', stage_a, x, precision=exact_mode)  2.05 us
  transfers between devices with their start and end apart: 2, of which 2 were waited for; matrix products, arithmetic and copies ran while one was open for 4% of the time, Pallas kernels for 0%

profile of v4, /device:TPU:8, one launch (start us, length us, event | category | flops | bytes accessed | tf_op | source)
XLA Modules:
  0.0 74.5 jit_solution(2241293033295387480)
XLA Ops:
  0.0 0.0 copy-start
  0.0 0.9 %copy-done = bf16[256,512]{1,0:T(8,128)(2,1)S(1)} copy-done((bf16[256,512]{1,0:T(8,128)(2,1)S(1)}, bf16[256,512]{1,0:T(8,128)(2,1)}, u32[]{:S(2)}) %copy-start) | copy-done | bytes 262168
  1.0 0.7 constant_dynamic-slice_fusion.taps_ref
  1.6 2.2 %shard_map.55 = f32[512,384]{1,0:T(8,128)} custom-call(bf16[256,512]{1,0:T(8,128)(2,1)} %gate_ref.3, bf16[256,512]{1,0:T(8,128)(2,1)} %values_ref.3, bf16[128,512]{1,0:T(8,128)(2,1)} %constant_dynamic-slice_fusion.taps_ref), custom_call_target="tpu_custom_call" | custom-call | tf_op jit(solution)/shard_map/pallas_call | solution.py:85
  3.8 11.3 %all-to-all-start = ((f32[32,16,384]{2,1,0:T(8,128)}), f32[32,16,384]{2,1,0:T(8,128)S(1)}, u32[]{:S(2)}, u32[]{:S(2)}) async-start(f32[32,16,384]{2,1,0:T(8,128)} %bitcast.34), calls=%async_computation | async-start | bytes 1572864 | tf_op jit(solution)/shard_map/all_to_all | solution.py:88
  15.1 0.3 fusion.48
  15.4 0.1 copy.7
  15.5 0.3 fusion.47
  15.7 0.1 copy.8
  15.8 0.2 sine_negate_fusion
  16.0 0.3 fusion.52
  16.3 0.3 fusion.45
  16.5 21.5 %all-to-all-done = f32[32,16,384]{2,1,0:T(8,128)S(1)} async-done(((f32[32,16,384]{2,1,0:T(8,128)}), f32[32,16,384]{2,1,0:T(8,128)S(1)}, u32[]{:S(2)}, u32[]{:S(2)}) %all-to-all-start) | async-done | bytes 786464 | tf_op jit(solution)/shard_map/all_to_all | solution.py:88
  38.0 0.1 slice.48
  38.1 0.3 collective-permute-start
  38.4 0.3 copy.6
  38.7 1.0 %convolution_bitcast_fusion.1 = f32[16,256,128]{1,2,0:T(8,128)S(1)} fusion(f32[16,64,128]{2,1,0:T(8,128)S(1)} %reshape_reshape.6, f32[128,64]{0,1:T(8,128)S(1)} %get-tuple-element.17, f32[128,64]{0,1:T(8,128)S(1)} %get-tuple-element.18), kind=kOutput, calls=%fused_computation.17 | convolution fusion | flops 201342976 | bytes 2686976 | tf_op jit(solution)/shard_map/kn,bnm->bkm/dot_general | solution.py:32
  39.8 0.1 collective-permute-done
  40.0 0.4 copy.10
  40.4 1.0 %convolution_bitcast_fusion = f32[16,256,128]{1,2,0:T(8,128)S(1)} fusion(f32[16,64,128]{2,1,0:T(8,128)S(1)} %bitcast.36, f32[128,64]{0,1:T(8,128)S(1)} %get-tuple-element.17, f32[128,64]{0,1:T(8,128)S(1)} %get-tuple-element.18), kind=kOutput, calls=%fused_computation.16 | convolution fusion | flops 201342976 | bytes 2686976 | tf_op jit(solution)/shard_map/kn,bnm->bkm/dot_general | solution.py:32
  41.4 0.6 multiply_add_fusion.3
  42.0 1.8 %fusion = f32[16,128,256]{2,1,0:T(8,128)S(1)} fusion(f32[16,128,128]{1,2,0:T(8,128)S(1)} %get-tuple-element.10, f32[16,128,128]{1,2,0:T(8,128)S(1)} %get-tuple-element.9, f32[128,128]{1,0:T(8,128)S(1)} %get-tuple-element.20, f32[128,128]{1,0:T(8,128)S(1)} %get-tuple-element.19, f32[128,128]{1,0:T(8,128)S(1)} %fusion.52), kind=kOutput, calls=%fused_computation | convolution fusion | flops 806027264 | bytes 4390912 | tf_op jit(solution)/shard_map/bkm,mj->bkj/dot_general | solution.py:36
  43.9 1.8 %fusion.4 = f32[16,128,256]{2,1,0:T(8,128)S(1)} fusion(f32[16,128,128]{1,2,0:T(8,128)S(1)} %get-tuple-element.15, f32[16,128,128]{1,2,0:T(8,128)S(1)} %get-tuple-element.16, f32[128,128]{1,0:T(8,128)S(1)} %get-tuple-element.20, f32[128,128]{1,0:T(8,128)S(1)} %get-tuple-element.19, f32[128,128]{1,0:T(8,128)S(1)} %fusion.52), kind=kOutput, calls=%fused_computation.4 | convolution fusion | flops 806027264 | bytes 4390912 | tf_op jit(solution)/shard_map/bkm,mj->bkj/dot_general | solution.py:36
  45.7 0.3 multiply_subtract_fusion.1
  46.1 1.1 %fusion.8 = f32[16,128,256]{1,2,0:T(8,128)S(1)} fusion(f32[16,128,128]{2,1,0:T(8,128)S(1)} %get-tuple-element.6, f32[16,128,128]{2,1,0:T(8,128)S(1)} %get-tuple-element.5, f32[128,128]{1,0:T(8,128)S(1)} %get-tuple-element.20, f32[128,128]{1,0:T(8,128)S(1)} %fusion.52, f32[128,128]{1,0:T(8,128)S(1)} %get-tuple-element.19), kind=kOutput, calls=%fused_computation.8 | convolution fusion | flops 806027264 | bytes 4390912 | tf_op jit(solution)/shard_map/bkj,jm->bkm/dot_general | solution.py:47
  47.1 0.3 multiply_subtract_fusion
  47.5 1.1 %fusion.19 = f32[16,64,128]{2,1,0:T(8,128)S(1)} fusion(f32[16,128,128]{1,2,0:T(8,128)S(1)} %get-tuple-element.8, f32[16,128,128]{1,2,0:T(8,128)S(1)} %get-tuple-element.7, f32[128,64]{0,1:T(8,128)S(1)} %get-tuple-element.17, f32[128,64]{0,1:T(8,128)S(1)} %get-tuple-element.18), kind=kOutput, calls=%fused_computation.19 | convolution fusion | flops 201998336 | bytes 2686976 | tf_op jit(solution)/shard_map/kn,bkm->bnm/dot_general | solution.py:51
  48.6 0.1 mul.381
  48.7 0.3 copy.15
  49.0 23.3 %all_to_all.32 = f32[16,32,256]{2,0,1:T(8,128)} all-to-all(f32[16,32,256]{2,0,1:T(8,128)S(1)} %copy.15), channel_id=1, replica_groups=mesh['seq'=32,'grp'=8] {'seq'}, dimensions={1} | all-to-all | bytes 1048576 | tf_op jit(solution)/shard_map/all_to_all | solution.py:102
  72.3 2.2 %shard_map.56 = bf16[256,512]{1,0:T(8,128)(2,1)} custom-call(f32[512,256]{1,0:T(8,128)} %bitcast.35, bf16[256,512]{1,0:T(8,128)(2,1)} %gate_ref.3, bf16[256,512]{1,0:T(8,128)(2,1)} %values_ref.3, bf16[256,512]{1,0:T(8,128)(2,1)} %out_gate_ref.1, f32[1,512]{1,0:T(1,128)} %bitcast.37), custom_call_target="tpu_custom_call" | custom-call | tf_op jit(solution)/shard_map/pallas_call | solution.py:103
  (4 shorter events, 0.1 us)
Async XLA Ops:
  0.0 1.0 %copy-start = (bf16[256,512]{1,0:T(8,128)(2,1)S(1)}, bf16[256,512]{1,0:T(8,128)(2,1)}, u32[]{:S(2)}) copy-start(bf16[256,512]{1,0:T(8,128)(2,1)} %param.8) | copy-start | bytes 786436
  3.8 34.2 %all-to-all-start = ((f32[32,16,384]{2,1,0:T(8,128)}), f32[32,16,384]{2,1,0:T(8,128)S(1)}, u32[]{:S(2)}, u32[]{:S(2)}) async-start(f32[32,16,384]{2,1,0:T(8,128)} %bitcast.34), calls=%async_computation | async-start | bytes 1572864 | tf_op jit(solution)/shard_map/all_to_all | solution.py:88
  38.1 1.8 %collective-permute-start = (f32[16,32,128]{2,0,1:T(8,128)S(1)}, f32[16,32,128]{2,0,1:T(8,128)S(1)}, u32[]{:S(2)}, u32[]{:S(2)}) collective-permute-start(f32[16,32,128]{2,0,1:T(8,128)S(1)} %slice.52), channel_id=1, source_target_pairs={{0,1},{1,0},{2,3},{3,2},{4,5},{5,4},{6,7},{7,6},{8,9},{9,8},{10,11... | collective-permute-start | bytes 786440 | tf_op jit(solution)/shard_map/ppermute | solution.py:93

commit v5 on v3

--- a/solution.py
+++ b/solution.py
@@ -1,6 +1,8 @@
 import jax
 import jax.numpy as jnp
 from jax import lax
+from jax.experimental import pallas as pl
+from jax.experimental.pallas import tpu as pltpu
 from jax.sharding import PartitionSpec as P
 
 exact_mode = lax.Precision.HIGH
@@ -52,14 +54,71 @@
     return y.reshape(ch, n) * (1.0 / (SIDE * SIDE))
 
 
+def prologue_kernel(core_ref, gate_ref, values_ref, taps_ref, out_ref):
+    step = pl.program_id(0)
+    gated_steps = pl.num_programs(0) - 1
+
+    @pl.when(step < gated_steps)
+    def _():
+        gated = gate_ref[...].astype(jnp.float32) * values_ref[...].astype(jnp.float32)
+        out_ref[...] = gated.T
+
+    @pl.when(step == gated_steps)
+    def _():
+        out_ref[...] = taps_ref[...].astype(jnp.float32).T
+
+
+def epilogue_kernel(back_ref, gate_ref, values_ref, out_gate_ref, skip_ref, out_ref):
+    gated = gate_ref[...].astype(jnp.float32) * values_ref[...].astype(jnp.float32)
+    total = back_ref[...].T + skip_ref[...] * gated
+    out_ref[...] = (out_gate_ref[...].astype(jnp.float32) * total).astype(out_ref.dtype)
+
+
+def prologue(core, in_gate, values, filter_taps):
+    rows, channels = in_gate.shape
+    half = rows // 2
+    gated_steps = rows // half
+    last = gated_steps - 1
+    row_block = pl.BlockSpec((half, channels), lambda j, c: (jnp.minimum(j, last), 0))
+    taps_block = pl.BlockSpec((half, channels), lambda j, c: (c[0], 0))
+    grid_spec = pltpu.PrefetchScalarGridSpec(
+        num_scalar_prefetch=1,
+        grid=(gated_steps + 1,),
+        in_specs=[row_block, row_block, taps_block],
+        out_specs=pl.BlockSpec((channels, half), lambda j, c: (0, j)),
+    )
+    return pl.pallas_call(
+        prologue_kernel,
+        grid_spec=grid_spec,
+        out_shape=jax.ShapeDtypeStruct((channels, rows + half), jnp.float32),
+    )(core.reshape(1), in_gate, values, filter_taps)
+
+
+def epilogue(back, in_gate, values, out_gate, skip_gain):
+    rows, channels = in_gate.shape
+    width = 128
+    col_block = pl.BlockSpec((rows, width), lambda j: (0, j))
+    return pl.pallas_call(
+        epilogue_kernel,
+        grid=(channels // width,),
+        in_specs=[
+            pl.BlockSpec((width, rows), lambda j: (j, 0)),
+            col_block,
+            col_block,
+            col_block,
+            pl.BlockSpec((1, width), lambda j: (0, j)),
+        ],
+        out_specs=col_block,
+        out_shape=jax.ShapeDtypeStruct((rows, channels), jnp.bfloat16),
+    )(back, in_gate, values, out_gate, skip_gain.reshape(1, channels))
+
+
 def local(in_gate, values, out_gate, filter_taps, skip_gain):
     own_rows, channels = in_gate.shape
     copies = lax.axis_size("grp")
     core = lax.axis_index("grp") % 2
     half = own_rows // 2
-    gated = in_gate.astype(jnp.float32) * values.astype(jnp.float32)
-    taps_half = lax.dynamic_slice_in_dim(filter_taps, core * half, half, axis=0)
-    payload = jnp.concatenate([gated.T, taps_half.astype(jnp.float32).T], axis=1)
+    payload = prologue(core.astype(jnp.int32), in_gate, values, filter_taps)
     spread = lax.all_to_all(payload, "seq", split_axis=0, concat_axis=1, tiled=True)
     ch = spread.shape[0]
     spread = spread.reshape(ch, -1, own_rows + half)
@@ -75,8 +134,7 @@
     spec_h = spectrum(taps_full, tables)
     conv = inverse_prefix(spec_g, spec_h, tables, n)
     back = lax.all_to_all(conv, "seq", split_axis=1, concat_axis=0, tiled=True)
-    total = back.T + skip_gain[None, :] * gated
-    return (out_gate.astype(jnp.float32) * total).astype(jnp.bfloat16)
+    return epilogue(back, in_gate, values, out_gate, skip_gain)
 
 
 def solution(mesh):

time: 75.1 us -> 75 us (level)
  blocking collectives: 0 us -> 23.3 us
  waiting for transfers between devices: 39.7 us -> 21.6 us
  Pallas kernels: 0 us -> 6.22 us
  starting transfers between devices: 16.7 us -> 11.6 us
  local copies, waits for them, and re-layouts: 6.48 us -> 1.46 us
  other arithmetic: 3.73 us -> 2.54 us
    all_to_all x0 -> x1, blocking collectives: none -> 23.3 us  [local(): back = lax.all_to_all(conv, 'seq', split_axis=1, concat_axis=0, tiled=True)]
    all_to_all x1 -> x0, waiting for transfers between devices: 18.1 us -> none  [local(): back = lax.all_to_all(conv, 'seq', split_axis=1, concat_axis=0, tiled=True)]
    pallas_call x0 -> x2, Pallas kernels: none -> 6.22 us  [the longest x1 3.46 us: epilogue(): pl.pallas_call(epilogue_kernel, grid=(channels // width,), in_specs=[pl.B...]
    all_to_all x1 -> x0, starting transfers between devices: 5.13 us -> none  [local(): back = lax.all_to_all(conv, 'seq', split_axis=1, concat_axis=0, tiled=True)]
    unnamed x10 -> x0, local copies, waits for them, and re-layouts: 3.38 us -> none
    concatenate x1 -> x0, other arithmetic: 0.95 us -> none  [local(): jnp.concatenate([gated.T, taps_half.astype(jnp.float32).T], axis=1)]
    convert_element_type x1 -> x0, local copies, waits for them, and re-layouts: 0.84 us -> none  [local(): return (out_gate.astype(jnp.float32) * total).astype(jnp.bfloat16)]
    mul x2, local copies, waits for them, and re-layouts: 1.25 us -> 0.46 us  [inverse_prefix(): return y.reshape(ch, n) * (1.0 / (SIDE * SIDE))]
  transfers between devices with their start and end apart: 3 -> 2, of which waited for: 3 -> 2; matrix products, arithmetic and copies ran while one was open for 4% -> 4% of each run, Pallas kernels for 0% -> 0%
where the time goes in v5:
time: 75 us; the launch traced here: 74.8 us
  blocking collectives  23.3 us (31%)
  waiting for transfers between devices  21.6 us (29%)
  starting transfers between devices  11.6 us (15%)
  matrix products  7.89 us (11%)
  Pallas kernels  6.22 us (8%)
  other arithmetic  2.54 us (3%)
  local copies, waits for them, and re-layouts  1.46 us (2%)
    all_to_all x1, blocking collectives, local(): back = lax.all_to_all(conv, 'seq', split_axis=1, concat_axis=0, tiled=True)  23.3 us
    all_to_all x1, waiting for transfers between devices, local(): lax.all_to_all(payload, 'seq', split_axis=0, concat_axis=1, tiled=True)  21.5 us
    all_to_all x1, starting transfers between devices, local(): lax.all_to_all(payload, 'seq', split_axis=0, concat_axis=1, tiled=True)  11.3 us
    dot_general x2, matrix products, spectrum(): jnp.einsum('bkm,mj->bkj', jnp.concatenate([b_re, b_im], axis=-1), forward...  3.69 us
    pallas_call x1, Pallas kernels, epilogue(): pl.pallas_call(epilogue_kernel, grid=(channels // width,), in_specs=[pl.B...  3.46 us
    pallas_call x1, Pallas kernels, prologue(): pl.pallas_call(prologue_kernel, grid_spec=grid_spec, out_shape=jax.ShapeD...  2.76 us
    dot_general x2, matrix products, spectrum(): a = jnp.einsum('kn,bnm->bkm', stage_a, x, precision=exact_mode)  2.05 us
  transfers between devices with their start and end apart: 2, of which 2 were waited for; matrix products, arithmetic and copies ran while one was open for 4% of the time, Pallas kernels for 0%

profile of v5, /device:TPU:8, one launch (start us, length us, event | category | flops | bytes accessed | tf_op | source)
XLA Modules:
  0.0 74.8 jit_solution(6299300872904182376)
XLA Ops:
  0.0 2.8 %shard_map.55 = f32[512,384]{1,0:T(8,128)} custom-call(s32[1]{0:T(128)} %bitcast.core_ref, bf16[256,512]{1,0:T(8,128)(2,1)} %gate_ref.3, bf16[256,512]{1,0:T(8,128)(2,1)} %values_ref.3, bf16[256,512]{1,0:T(8,128)(2,1)} %taps_ref.1), custom_call_target="tpu_custom_call" | custom-call | tf_op jit(solution)/shard_map/pallas_call | solution.py:90
  2.8 11.3 %all-to-all-start = ((f32[32,16,384]{2,1,0:T(8,128)}), f32[32,16,384]{2,1,0:T(8,128)S(1)}, u32[]{:S(2)}, u32[]{:S(2)}) async-start(f32[32,16,384]{2,1,0:T(8,128)} %bitcast.35), calls=%async_computation | async-start | bytes 1572864 | tf_op jit(solution)/shard_map/all_to_all | solution.py:122
  14.1 0.3 fusion.48
  14.4 0.1 copy.7
  14.4 0.3 fusion.47
  14.7 0.1 copy.8
  14.8 0.2 sine_negate_fusion
  15.0 0.3 fusion.52
  15.2 0.3 fusion.45
  15.5 21.5 %all-to-all-done = f32[32,16,384]{2,1,0:T(8,128)S(1)} async-done(((f32[32,16,384]{2,1,0:T(8,128)}), f32[32,16,384]{2,1,0:T(8,128)S(1)}, u32[]{:S(2)}, u32[]{:S(2)}) %all-to-all-start) | async-done | bytes 786464 | tf_op jit(solution)/shard_map/all_to_all | solution.py:122
  37.0 0.1 slice.48
  37.1 0.3 collective-permute-start
  37.3 0.3 copy.6
  37.7 1.0 %convolution_bitcast_fusion.1 = f32[16,256,128]{1,2,0:T(8,128)S(1)} fusion(f32[16,64,128]{2,1,0:T(8,128)S(1)} %reshape_reshape.6, f32[128,64]{0,1:T(8,128)S(1)} %get-tuple-element.17, f32[128,64]{0,1:T(8,128)S(1)} %get-tuple-element.18), kind=kOutput, calls=%fused_computation.17 | convolution fusion | flops 201342976 | bytes 2686976 | tf_op jit(solution)/shard_map/kn,bnm->bkm/dot_general | solution.py:32
  38.7 0.1 collective-permute-done
  38.9 0.4 copy.10
  39.4 1.0 %convolution_bitcast_fusion = f32[16,256,128]{1,2,0:T(8,128)S(1)} fusion(f32[16,64,128]{2,1,0:T(8,128)S(1)} %bitcast.37, f32[128,64]{0,1:T(8,128)S(1)} %get-tuple-element.17, f32[128,64]{0,1:T(8,128)S(1)} %get-tuple-element.18), kind=kOutput, calls=%fused_computation.16 | convolution fusion | flops 201342976 | bytes 2686976 | tf_op jit(solution)/shard_map/kn,bnm->bkm/dot_general | solution.py:32
  40.4 0.6 multiply_add_fusion.3
  41.0 1.8 %fusion = f32[16,128,256]{2,1,0:T(8,128)S(1)} fusion(f32[16,128,128]{1,2,0:T(8,128)S(1)} %get-tuple-element.10, f32[16,128,128]{1,2,0:T(8,128)S(1)} %get-tuple-element.9, f32[128,128]{1,0:T(8,128)S(1)} %get-tuple-element.20, f32[128,128]{1,0:T(8,128)S(1)} %get-tuple-element.19, f32[128,128]{1,0:T(8,128)S(1)} %fusion.52), kind=kOutput, calls=%fused_computation | convolution fusion | flops 806027264 | bytes 4390912 | tf_op jit(solution)/shard_map/bkm,mj->bkj/dot_general | solution.py:36
  42.9 1.8 %fusion.4 = f32[16,128,256]{2,1,0:T(8,128)S(1)} fusion(f32[16,128,128]{1,2,0:T(8,128)S(1)} %get-tuple-element.15, f32[16,128,128]{1,2,0:T(8,128)S(1)} %get-tuple-element.16, f32[128,128]{1,0:T(8,128)S(1)} %get-tuple-element.20, f32[128,128]{1,0:T(8,128)S(1)} %get-tuple-element.19, f32[128,128]{1,0:T(8,128)S(1)} %fusion.52), kind=kOutput, calls=%fused_computation.4 | convolution fusion | flops 806027264 | bytes 4390912 | tf_op jit(solution)/shard_map/bkm,mj->bkj/dot_general | solution.py:36
  44.7 0.3 multiply_subtract_fusion.1
  45.0 1.1 %fusion.8 = f32[16,128,256]{1,2,0:T(8,128)S(1)} fusion(f32[16,128,128]{2,1,0:T(8,128)S(1)} %get-tuple-element.6, f32[16,128,128]{2,1,0:T(8,128)S(1)} %get-tuple-element.5, f32[128,128]{1,0:T(8,128)S(1)} %get-tuple-element.20, f32[128,128]{1,0:T(8,128)S(1)} %fusion.52, f32[128,128]{1,0:T(8,128)S(1)} %get-tuple-element.19), kind=kOutput, calls=%fused_computation.8 | convolution fusion | flops 806027264 | bytes 4390912 | tf_op jit(solution)/shard_map/bkj,jm->bkm/dot_general | solution.py:47
  46.1 0.3 multiply_subtract_fusion
  46.5 1.1 %fusion.19 = f32[16,64,128]{2,1,0:T(8,128)S(1)} fusion(f32[16,128,128]{1,2,0:T(8,128)S(1)} %get-tuple-element.8, f32[16,128,128]{1,2,0:T(8,128)S(1)} %get-tuple-element.7, f32[128,64]{0,1:T(8,128)S(1)} %get-tuple-element.17, f32[128,64]{0,1:T(8,128)S(1)} %get-tuple-element.18), kind=kOutput, calls=%fused_computation.19 | convolution fusion | flops 201998336 | bytes 2686976 | tf_op jit(solution)/shard_map/kn,bkm->bnm/dot_general | solution.py:51
  47.5 0.1 mul.377
  47.7 0.3 copy.15
  48.0 23.3 %all_to_all.32 = f32[16,32,256]{2,0,1:T(8,128)} all-to-all(f32[16,32,256]{2,0,1:T(8,128)S(1)} %copy.15), channel_id=1, replica_groups=mesh['seq'=32,'grp'=8] {'seq'}, dimensions={1} | all-to-all | bytes 1048576 | tf_op jit(solution)/shard_map/all_to_all | solution.py:136
  71.3 3.5 %shard_map.56 = bf16[256,512]{1,0:T(8,128)(2,1)} custom-call(f32[512,256]{1,0:T(8,128)} %bitcast.36, bf16[256,512]{1,0:T(8,128)(2,1)} %gate_ref.3, bf16[256,512]{1,0:T(8,128)(2,1)} %values_ref.3, bf16[256,512]{1,0:T(8,128)(2,1)} %out_gate_ref.1, f32[1,512]{1,0:T(1,128)} %bitcast.38), custom_call_target="tpu_custom_call" | custom-call | tf_op jit(solution)/shard_map/pallas_call | solution.py:101
  (4 shorter events, 0.1 us)
Async XLA Ops:
  2.8 34.2 %all-to-all-start = ((f32[32,16,384]{2,1,0:T(8,128)}), f32[32,16,384]{2,1,0:T(8,128)S(1)}, u32[]{:S(2)}, u32[]{:S(2)}) async-start(f32[32,16,384]{2,1,0:T(8,128)} %bitcast.35), calls=%async_computation | async-start | bytes 1572864 | tf_op jit(solution)/shard_map/all_to_all | solution.py:122
  37.1 1.8 %collective-permute-start = (f32[16,32,128]{2,0,1:T(8,128)S(1)}, f32[16,32,128]{2,0,1:T(8,128)S(1)}, u32[]{:S(2)}, u32[]{:S(2)}) collective-permute-start(f32[16,32,128]{2,0,1:T(8,128)S(1)} %slice.52), channel_id=1, source_target_pairs={{0,1},{1,0},{2,3},{3,2},{4,5},{5,4},{6,7},{7,6},{8,9},{9,8},{10,11... | collective-permute-start | bytes 786440 | tf_op jit(solution)/shard_map/ppermute | solution.py:127

commit v6 on v5

--- a/solution.py
+++ b/solution.py
@@ -68,12 +68,6 @@
         out_ref[...] = taps_ref[...].astype(jnp.float32).T
 
 
-def epilogue_kernel(back_ref, gate_ref, values_ref, out_gate_ref, skip_ref, out_ref):
-    gated = gate_ref[...].astype(jnp.float32) * values_ref[...].astype(jnp.float32)
-    total = back_ref[...].T + skip_ref[...] * gated
-    out_ref[...] = (out_gate_ref[...].astype(jnp.float32) * total).astype(out_ref.dtype)
-
-
 def prologue(core, in_gate, values, filter_taps):
     rows, channels = in_gate.shape
     half = rows // 2
@@ -92,25 +86,6 @@
         grid_spec=grid_spec,
         out_shape=jax.ShapeDtypeStruct((channels, rows + half), jnp.float32),
     )(core.reshape(1), in_gate, values, filter_taps)
-
-
-def epilogue(back, in_gate, values, out_gate, skip_gain):
-    rows, channels = in_gate.shape
-    width = 128
-    col_block = pl.BlockSpec((rows, width), lambda j: (0, j))
-    return pl.pallas_call(
-        epilogue_kernel,
-        grid=(channels // width,),
-        in_specs=[
-            pl.BlockSpec((width, rows), lambda j: (j, 0)),
-            col_block,
-            col_block,
-            col_block,
-            pl.BlockSpec((1, width), lambda j: (0, j)),
-        ],
-        out_specs=col_block,
-        out_shape=jax.ShapeDtypeStruct((rows, channels), jnp.bfloat16),
-    )(back, in_gate, values, out_gate, skip_gain.reshape(1, channels))
 
 
 def local(in_gate, values, out_gate, filter_taps, skip_gain):
@@ -134,7 +109,9 @@
     spec_h = spectrum(taps_full, tables)
     conv = inverse_prefix(spec_g, spec_h, tables, n)
     back = lax.all_to_all(conv, "seq", split_axis=1, concat_axis=0, tiled=True)
-    return epilogue(back, in_gate, values, out_gate, skip_gain)
+    gated = in_gate.astype(jnp.float32) * values.astype(jnp.float32)
+    total = back.T + skip_gain[None, :] * gated
+    return (out_gate.astype(jnp.float32) * total).astype(jnp.bfloat16)
 
 
 def solution(mesh):

time: 75 us -> 73.5 us (0.980)
  blocking collectives: 23.3 us -> 0 us
  waiting for transfers between devices: 21.6 us -> 39.4 us
  starting transfers between devices: 11.6 us -> 16.7 us
  Pallas kernels: 6.22 us -> 2.74 us
  local copies, waits for them, and re-layouts: 1.46 us -> 3.51 us
    all_to_all x1 -> x0, blocking collectives: 23.3 us -> none  [local(): back = lax.all_to_all(conv, 'seq', split_axis=1, concat_axis=0, tiled=True)]
    all_to_all x0 -> x1, waiting for transfers between devices: none -> 17.8 us  [local(): back = lax.all_to_all(conv, 'seq', split_axis=1, concat_axis=0, tiled=True)]
    all_to_all x0 -> x1, starting transfers between devices: none -> 5.13 us  [local(): back = lax.all_to_all(conv, 'seq', split_axis=1, concat_axis=0, tiled=True)]
    pallas_call x1 -> x0, Pallas kernels: 3.46 us -> none  [epilogue(): pl.pallas_call(epilogue_kernel, grid=(channels // width,), in_specs=[pl.B...]
    convert_element_type x0 -> x1, local copies, waits for them, and re-layouts: none -> 0.84 us  [local(): return (out_gate.astype(jnp.float32) * total).astype(jnp.bfloat16)]
    mul x2, local copies, waits for them, and re-layouts: 0.46 us -> 1.25 us  [inverse_prefix(): return y.reshape(ch, n) * (1.0 / (SIDE * SIDE))]
  transfers between devices with their start and end apart: 2 -> 3, of which waited for: 2 -> 3; matrix products, arithmetic and copies ran while one was open for 4% -> 4% of each run, Pallas kernels for 0% -> 0%
where the time goes in v6:
time: 73.5 us; the launch traced here: 73.2 us
  waiting for transfers between devices  39.4 us (54%)
  starting transfers between devices  16.7 us (23%)
  matrix products  7.88 us (11%)
  local copies, waits for them, and re-layouts  3.51 us (5%)
  Pallas kernels  2.74 us (4%)
  other arithmetic  2.7 us (4%)
    all_to_all x1, waiting for transfers between devices, local(): lax.all_to_all(payload, 'seq', split_axis=0, concat_axis=1, tiled=True)  21.5 us
    all_to_all x1, waiting for transfers between devices, local(): back = lax.all_to_all(conv, 'seq', split_axis=1, concat_axis=0, tiled=True)  17.8 us
    all_to_all x1, starting transfers between devices, local(): lax.all_to_all(payload, 'seq', split_axis=0, concat_axis=1, tiled=True)  11.3 us
    all_to_all x1, starting transfers between devices, local(): back = lax.all_to_all(conv, 'seq', split_axis=1, concat_axis=0, tiled=True)  5.13 us
    dot_general x2, matrix products, spectrum(): jnp.einsum('bkm,mj->bkj', jnp.concatenate([b_re, b_im], axis=-1), forward...  3.68 us
    pallas_call x1, Pallas kernels, prologue(): pl.pallas_call(prologue_kernel, grid_spec=grid_spec, out_shape=jax.ShapeD...  2.74 us
    dot_general x2, matrix products, spectrum(): a = jnp.einsum('kn,bnm->bkm', stage_a, x, precision=exact_mode)  2.05 us
  transfers between devices with their start and end apart: 3, of which 3 were waited for; matrix products, arithmetic and copies ran while one was open for 4% of the time, Pallas kernels for 0%

profile of v6, /device:TPU:8, one launch (start us, length us, event | category | flops | bytes accessed | tf_op | source)
XLA Modules:
  0.0 73.2 jit_solution(439518803626407245)
XLA Ops:
  0.0 2.7 %shard_map.55 = f32[512,384]{1,0:T(8,128)} custom-call(s32[1]{0:T(128)} %bitcast.core_ref, bf16[256,512]{1,0:T(8,128)(2,1)} %gate_ref.1, bf16[256,512]{1,0:T(8,128)(2,1)} %values_ref.1, bf16[256,512]{1,0:T(8,128)(2,1)} %taps_ref.1), custom_call_target="tpu_custom_call" | custom-call | tf_op jit(solution)/shard_map/pallas_call | solution.py:84
  2.7 11.3 %all-to-all-start = ((f32[32,16,384]{2,1,0:T(8,128)}), f32[32,16,384]{2,1,0:T(8,128)S(1)}, u32[]{:S(2)}, u32[]{:S(2)}) async-start(f32[32,16,384]{2,1,0:T(8,128)} %bitcast.41), calls=%async_computation | async-start | bytes 1572864 | tf_op jit(solution)/shard_map/all_to_all | solution.py:97
  14.1 0.3 fusion.50
  14.3 0.1 copy.18
  14.4 0.3 fusion.49
  14.7 0.1 copy.19
  14.8 0.2 sine_negate_fusion
  15.0 0.3 fusion.54
  15.2 0.3 fusion.47
  15.5 21.5 %all-to-all-done = f32[32,16,384]{2,1,0:T(8,128)S(1)} async-done(((f32[32,16,384]{2,1,0:T(8,128)}), f32[32,16,384]{2,1,0:T(8,128)S(1)}, u32[]{:S(2)}, u32[]{:S(2)}) %all-to-all-start) | async-done | bytes 786464 | tf_op jit(solution)/shard_map/all_to_all | solution.py:97
  37.0 0.3 collective-permute-start
  37.3 0.3 copy.17
  37.7 1.0 %convolution_bitcast_fusion.1 = f32[16,256,128]{1,2,0:T(8,128)S(1)} fusion(f32[16,64,128]{2,1,0:T(8,128)S(1)} %reshape_reshape.6, f32[128,64]{0,1:T(8,128)S(1)} %get-tuple-element.17, f32[128,64]{0,1:T(8,128)S(1)} %get-tuple-element.18), kind=kOutput, calls=%fused_computation.17 | convolution fusion | flops 201342976 | bytes 2686976 | tf_op jit(solution)/shard_map/kn,bnm->bkm/dot_general | solution.py:32
  38.7 0.1 collective-permute-done
  38.9 0.4 copy.21
  39.3 1.0 %convolution_bitcast_fusion = f32[16,256,128]{1,2,0:T(8,128)S(1)} fusion(f32[16,64,128]{2,1,0:T(8,128)S(1)} %bitcast.42, f32[128,64]{0,1:T(8,128)S(1)} %get-tuple-element.17, f32[128,64]{0,1:T(8,128)S(1)} %get-tuple-element.18), kind=kOutput, calls=%fused_computation.16 | convolution fusion | flops 201342976 | bytes 2686976 | tf_op jit(solution)/shard_map/kn,bnm->bkm/dot_general | solution.py:32
  40.4 0.6 multiply_add_fusion.3
  41.0 1.8 %fusion = f32[16,128,256]{2,1,0:T(8,128)S(1)} fusion(f32[16,128,128]{1,2,0:T(8,128)S(1)} %get-tuple-element.10, f32[16,128,128]{1,2,0:T(8,128)S(1)} %get-tuple-element.9, f32[128,128]{1,0:T(8,128)S(1)} %get-tuple-element.20, f32[128,128]{1,0:T(8,128)S(1)} %get-tuple-element.19, f32[128,128]{1,0:T(8,128)S(1)} %fusion.54), kind=kOutput, calls=%fused_computation | convolution fusion | flops 806027264 | bytes 4390912 | tf_op jit(solution)/shard_map/bkm,mj->bkj/dot_general | solution.py:36
  42.8 1.8 %fusion.4 = f32[16,128,256]{2,1,0:T(8,128)S(1)} fusion(f32[16,128,128]{1,2,0:T(8,128)S(1)} %get-tuple-element.15, f32[16,128,128]{1,2,0:T(8,128)S(1)} %get-tuple-element.16, f32[128,128]{1,0:T(8,128)S(1)} %get-tuple-element.20, f32[128,128]{1,0:T(8,128)S(1)} %get-tuple-element.19, f32[128,128]{1,0:T(8,128)S(1)} %fusion.54), kind=kOutput, calls=%fused_computation.4 | convolution fusion | flops 806027264 | bytes 4390912 | tf_op jit(solution)/shard_map/bkm,mj->bkj/dot_general | solution.py:36
  44.7 0.3 multiply_subtract_fusion.1
  45.0 1.1 %fusion.8 = f32[16,128,256]{1,2,0:T(8,128)S(1)} fusion(f32[16,128,128]{2,1,0:T(8,128)S(1)} %get-tuple-element.6, f32[16,128,128]{2,1,0:T(8,128)S(1)} %get-tuple-element.5, f32[128,128]{1,0:T(8,128)S(1)} %get-tuple-element.20, f32[128,128]{1,0:T(8,128)S(1)} %fusion.54, f32[128,128]{1,0:T(8,128)S(1)} %get-tuple-element.19), kind=kOutput, calls=%fused_computation.8 | convolution fusion | flops 806027264 | bytes 4390912 | tf_op jit(solution)/shard_map/bkj,jm->bkm/dot_general | solution.py:47
  46.1 0.3 multiply_subtract_fusion
  46.4 1.1 %fusion.19 = f32[16,64,128]{2,1,0:T(8,128)S(1)} fusion(f32[16,128,128]{1,2,0:T(8,128)S(1)} %get-tuple-element.8, f32[16,128,128]{1,2,0:T(8,128)S(1)} %get-tuple-element.7, f32[128,64]{0,1:T(8,128)S(1)} %get-tuple-element.17, f32[128,64]{0,1:T(8,128)S(1)} %get-tuple-element.18), kind=kOutput, calls=%fused_computation.19 | convolution fusion | flops 201998336 | bytes 2686976 | tf_op jit(solution)/shard_map/kn,bkm->bnm/dot_general | solution.py:51
  47.5 0.1 mul.391
  47.7 1.1 %copy.26 = f32[16,32,256]{2,0,1:T(8,128)} copy(f32[16,32,256]{2,1,0:T(8,128)S(1)} %mul.391) | data formatting | bytes 1048576 | tf_op jit(solution)/shard_map/mul | solution.py:54
  48.8 5.1 %all-to-all-start.1 = ((f32[16,32,256]{2,0,1:T(8,128)}), f32[16,32,256]{2,0,1:T(8,128)S(1)}, u32[]{:S(2)}, u32[]{:S(2)}) async-start(f32[16,32,256]{2,0,1:T(8,128)} %copy.26), calls=%async_computation.1 | async-start | bytes 1048576 | tf_op jit(solution)/shard_map/all_to_all | solution.py:111
  54.0 0.1 copy.27
  54.1 0.1 copy.28
  54.3 0.1 copy.16
  54.4 17.8 %all-to-all-done.1 = f32[16,32,256]{2,0,1:T(8,128)S(1)} async-done(((f32[16,32,256]{2,0,1:T(8,128)}), f32[16,32,256]{2,0,1:T(8,128)S(1)}, u32[]{:S(2)}, u32[]{:S(2)}) %all-to-all-start.1) | async-done | bytes 524320 | tf_op jit(solution)/shard_map/all_to_all | solution.py:111
  72.2 0.2 fusion.23
  72.4 0.8 %copy.29 = bf16[256,512]{1,0:T(8,128)(2,1)} copy(bf16[256,512]{0,1:T(8,128)(2,1)S(1)} %fusion.23) | data formatting | bytes 524288 | tf_op jit(solution)/shard_map/convert_element_type | solution.py:114
  (13 shorter events, 0.2 us)
Async XLA Ops:
  2.7 34.2 %all-to-all-start = ((f32[32,16,384]{2,1,0:T(8,128)}), f32[32,16,384]{2,1,0:T(8,128)S(1)}, u32[]{:S(2)}, u32[]{:S(2)}) async-start(f32[32,16,384]{2,1,0:T(8,128)} %bitcast.41), calls=%async_computation | async-start | bytes 1572864 | tf_op jit(solution)/shard_map/all_to_all | solution.py:97
  37.0 1.8 %collective-permute-start = (f32[16,32,128]{2,0,1:T(8,128)S(1)}, f32[16,32,128]{2,0,1:T(8,128)S(1)}, u32[]{:S(2)}, u32[]{:S(2)}) collective-permute-start(f32[16,32,128]{2,0,1:T(8,128)S(1)} %slice.52), channel_id=1, source_target_pairs={{0,1},{1,0},{2,3},{3,2},{4,5},{5,4},{6,7},{7,6},{8,9},{9,8},{10,11... | collective-permute-start | bytes 786440 | tf_op jit(solution)/shard_map/ppermute | solution.py:102
  47.5 6.4 %copy-start = (bf16[256,512]{1,0:T(8,128)(2,1)S(1)}, bf16[256,512]{1,0:T(8,128)(2,1)}, u32[]{:S(2)}) copy-start(bf16[256,512]{1,0:T(8,128)(2,1)} %gate_ref.1) | copy-start | bytes 786436
  47.5 6.6 %copy-start.1 = (bf16[256,512]{1,0:T(8,128)(2,1)S(1)}, bf16[256,512]{1,0:T(8,128)(2,1)}, u32[]{:S(2)}) copy-start(bf16[256,512]{1,0:T(8,128)(2,1)} %values_ref.1) | copy-start | bytes 786436
  47.5 6.7 %copy-start.2 = (bf16[256,512]{1,0:T(8,128)(2,1)S(1)}, bf16[256,512]{1,0:T(8,128)(2,1)}, u32[]{:S(2)}) copy-start(bf16[256,512]{1,0:T(8,128)(2,1)} %param.7) | copy-start | bytes 786436
  47.7 24.5 %copy-start.3 = (f32[512]{0:T(512)S(1)}, f32[512]{0:T(512)}, u32[]{:S(2)}) copy-start(f32[512]{0:T(512)} %param.9) | copy-start | bytes 6148
  48.8 23.4 %all-to-all-start.1 = ((f32[16,32,256]{2,0,1:T(8,128)}), f32[16,32,256]{2,0,1:T(8,128)S(1)}, u32[]{:S(2)}, u32[]{:S(2)}) async-start(f32[16,32,256]{2,0,1:T(8,128)} %copy.26), calls=%async_computation.1 | async-start | bytes 1048576 | tf_op jit(solution)/shard_map/all_to_all | solution.py:111

commit v7 on v6

--- a/solution.py
+++ b/solution.py
@@ -15,22 +15,27 @@
 
 
 def dft_tables(filled):
-    first = angle_table(SIDE, filled, SIDE)
+    rows = SIDE // 2 + 8
+    first = angle_table(rows, filled, SIDE)
     stage_a = jnp.concatenate([jnp.cos(first), -jnp.sin(first)], axis=0)
     second = angle_table(SIDE, SIDE, SIDE)
     cos_b, sin_b = jnp.cos(second), jnp.sin(second)
     forward_b = jnp.block([[cos_b, -sin_b], [sin_b, cos_b]])
     inverse_b = jnp.block([[cos_b, sin_b], [-sin_b, cos_b]])
-    twist = angle_table(SIDE, SIDE, SIDE * SIDE)
-    return stage_a, forward_b, inverse_b, jnp.cos(twist), jnp.sin(twist)
+    twist = angle_table(rows, SIDE, SIDE * SIDE)
+    row = jnp.arange(rows, dtype=jnp.int32)
+    weight = jnp.where((row == 0) | (row == SIDE // 2), 1.0, jnp.where(row < SIDE // 2, 2.0, 0.0))
+    stage_inv = stage_a * jnp.concatenate([weight, weight])[:, None]
+    return stage_a, forward_b, inverse_b, jnp.cos(twist), jnp.sin(twist), stage_inv
 
 
 def spectrum(signal, tables):
-    stage_a, forward_b, _, twist_cos, twist_sin = tables
+    stage_a, forward_b, _, twist_cos, twist_sin, _ = tables
+    rows = twist_cos.shape[0]
     ch, n = signal.shape
     x = signal.reshape(ch, n // SIDE, SIDE)
     a = jnp.einsum("kn,bnm->bkm", stage_a, x, precision=exact_mode)
-    a_re, a_im = a[:, :SIDE], a[:, SIDE:]
+    a_re, a_im = a[:, :rows], a[:, rows:]
     b_re = a_re * twist_cos + a_im * twist_sin
     b_im = a_im * twist_cos - a_re * twist_sin
     return jnp.einsum(
@@ -39,8 +44,7 @@
 
 
 def inverse_prefix(spec_g, spec_h, tables, n):
-    stage_a, _, inverse_b, twist_cos, twist_sin = tables
-    ch = spec_g.shape[0]
+    _, _, inverse_b, twist_cos, twist_sin, stage_inv = tables
     g_re, g_im = spec_g[..., :SIDE], spec_g[..., SIDE:]
     h_re, h_im = spec_h[..., :SIDE], spec_h[..., SIDE:]
     prod = jnp.concatenate([g_re * h_re - g_im * h_im, g_re * h_im + g_im * h_re], axis=-1)
@@ -49,9 +53,9 @@
     r_re = q_re * twist_cos - q_im * twist_sin
     r_im = q_im * twist_cos + q_re * twist_sin
     y = jnp.einsum(
-        "kn,bkm->bnm", stage_a, jnp.concatenate([r_re, r_im], axis=1), precision=exact_mode
+        "kn,bkm->bnm", stage_inv, jnp.concatenate([r_re, r_im], axis=1), precision=exact_mode
     )
-    return y.reshape(ch, n) * (1.0 / (SIDE * SIDE))
+    return y.reshape(y.shape[0], n) * (1.0 / (SIDE * SIDE))
 
 
 def prologue_kernel(core_ref, gate_ref, values_ref, taps_ref, out_ref):

time: 73.5 us -> 68.8 us (0.936)
  matrix products: 7.88 us -> 3.84 us
  other arithmetic: 2.7 us -> 1.68 us
    dot_general x2, matrix products: 3.68 us -> 1.27 us  [spectrum(): jnp.einsum('bkm,mj->bkj', jnp.concatenate([b_re, b_im], axis=-1), forward...]
where the time goes in v7:
time: 68.8 us; the launch traced here: 68.5 us
  waiting for transfers between devices  40 us (58%)
  starting transfers between devices  16.7 us (24%)
  matrix products  3.84 us (6%)
  local copies, waits for them, and re-layouts  3.33 us (5%)
  Pallas kernels  2.73 us (4%)
  other arithmetic  1.68 us (2%)
    all_to_all x1, waiting for transfers between devices, local(): lax.all_to_all(payload, 'seq', split_axis=0, concat_axis=1, tiled=True)  21.9 us
    all_to_all x1, waiting for transfers between devices, local(): back = lax.all_to_all(conv, 'seq', split_axis=1, concat_axis=0, tiled=True)  17.7 us
    all_to_all x1, starting transfers between devices, local(): lax.all_to_all(payload, 'seq', split_axis=0, concat_axis=1, tiled=True)  11.3 us
    all_to_all x1, starting transfers between devices, local(): back = lax.all_to_all(conv, 'seq', split_axis=1, concat_axis=0, tiled=True)  5.26 us
    pallas_call x1, Pallas kernels, prologue(): pl.pallas_call(prologue_kernel, grid_spec=grid_spec, out_shape=jax.ShapeD...  2.73 us
    dot_general x2, matrix products, spectrum(): a = jnp.einsum('kn,bnm->bkm', stage_a, x, precision=exact_mode)  1.48 us
  transfers between devices with their start and end apart: 3, of which 3 were waited for; matrix products, arithmetic and copies ran while one was open for 4% of the time, Pallas kernels for 0%

profile of v7, /device:TPU:8, one launch (start us, length us, event | category | flops | bytes accessed | tf_op | source)
XLA Modules:
  0.0 68.5 jit_solution(16856971442253728769)
XLA Ops:
  0.0 2.7 %shard_map.55 = f32[512,384]{1,0:T(8,128)} custom-call(s32[1]{0:T(128)} %bitcast.core_ref, bf16[256,512]{1,0:T(8,128)(2,1)} %gate_ref.1, bf16[256,512]{1,0:T(8,128)(2,1)} %values_ref.1, bf16[256,512]{1,0:T(8,128)(2,1)} %taps_ref.1), custom_call_target="tpu_custom_call" | custom-call | tf_op jit(solution)/shard_map/pallas_call | solution.py:88
  2.7 11.3 %all-to-all-start = ((f32[32,16,384]{2,1,0:T(8,128)}), f32[32,16,384]{2,1,0:T(8,128)S(1)}, u32[]{:S(2)}, u32[]{:S(2)}) async-start(f32[32,16,384]{2,1,0:T(8,128)} %bitcast.44), calls=%async_computation | async-start | bytes 1572864 | tf_op jit(solution)/shard_map/all_to_all | solution.py:101
  14.1 0.1 pad_maximum_fusion.10
  14.1 0.1 sine_negate_fusion
  14.3 0.3 fusion.52
  14.6 0.2 fusion.53
  14.7 0.3 fusion.47
  15.0 21.9 %all-to-all-done = f32[32,16,384]{2,1,0:T(8,128)S(1)} async-done(((f32[32,16,384]{2,1,0:T(8,128)}), f32[32,16,384]{2,1,0:T(8,128)S(1)}, u32[]{:S(2)}, u32[]{:S(2)}) %all-to-all-start) | async-done | bytes 786464 | tf_op jit(solution)/shard_map/all_to_all | solution.py:101
  37.0 0.1 slice.48
  37.0 0.1 collective-permute-start
  37.1 0.3 copy.10
  37.5 0.7 %convolution_bitcast_fusion.1 = f32[16,144,128]{2,1,0:T(8,128)S(1)} fusion(f32[16,64,128]{2,1,0:T(8,128)S(1)} %reshape_reshape.6, f32[72,64]{0,1:T(8,128)S(1)} %get-tuple-element.17, f32[72,64]{0,1:T(8,128)S(1)} %get-tuple-element.18), kind=kOutput, calls=%fused_computation.1 | convolution fusion | flops 113255424 | bytes 1740800 | tf_op jit(solution)/shard_map/kn,bnm->bkm/dot_general | solution.py:37
  38.2 0.4 collective-permute-done
  38.6 0.1 select_bitcast_fusion.1
  38.7 0.4 copy.11
  39.2 0.7 %convolution_bitcast_fusion = f32[16,144,128]{2,1,0:T(8,128)S(1)} fusion(f32[16,64,128]{2,1,0:T(8,128)S(1)} %bitcast.45, f32[72,64]{0,1:T(8,128)S(1)} %get-tuple-element.17, f32[72,64]{0,1:T(8,128)S(1)} %get-tuple-element.18), kind=kOutput, calls=%fused_computation | convolution fusion | flops 113255424 | bytes 1740800 | tf_op jit(solution)/shard_map/kn,bnm->bkm/dot_general | solution.py:37
  39.9 0.2 multiply_add_fusion.3
  40.2 0.6 fusion.1
  40.8 0.6 fusion.5
  41.5 0.1 multiply_subtract_fusion.1
  41.6 0.6 fusion.9
  42.2 0.1 multiply_subtract_fusion
  42.4 0.5 fusion
  42.8 0.1 mul.404
  43.0 1.1 %copy.12 = f32[16,32,256]{2,0,1:T(8,128)} copy(f32[16,32,256]{2,1,0:T(8,128)S(1)} %mul.404) | data formatting | bytes 1048576 | tf_op jit(solution)/shard_map/mul | solution.py:58
  44.1 5.3 %all-to-all-start.1 = ((f32[16,32,256]{2,0,1:T(8,128)}), f32[16,32,256]{2,0,1:T(8,128)S(1)}, u32[]{:S(2)}, u32[]{:S(2)}) async-start(f32[16,32,256]{2,0,1:T(8,128)} %copy.12), calls=%async_computation.1 | async-start | bytes 1048576 | tf_op jit(solution)/shard_map/all_to_all | solution.py:115
  49.4 0.1 copy.13
  49.5 0.1 copy.14
  49.7 0.1 copy.9
  49.8 17.7 %all-to-all-done.1 = f32[16,32,256]{2,0,1:T(8,128)S(1)} async-done(((f32[16,32,256]{2,0,1:T(8,128)}), f32[16,32,256]{2,0,1:T(8,128)S(1)}, u32[]{:S(2)}, u32[]{:S(2)}) %all-to-all-start.1) | async-done | bytes 524320 | tf_op jit(solution)/shard_map/all_to_all | solution.py:115
  67.5 0.2 fusion.17
  67.7 0.8 %copy.15 = bf16[256,512]{1,0:T(8,128)(2,1)} copy(bf16[256,512]{0,1:T(8,128)(2,1)S(1)} %fusion.17) | data formatting | bytes 524288 | tf_op jit(solution)/shard_map/convert_element_type | solution.py:118
  (12 shorter events, 0.1 us)
Async XLA Ops:
  2.7 34.2 %all-to-all-start = ((f32[32,16,384]{2,1,0:T(8,128)}), f32[32,16,384]{2,1,0:T(8,128)S(1)}, u32[]{:S(2)}, u32[]{:S(2)}) async-start(f32[32,16,384]{2,1,0:T(8,128)} %bitcast.44), calls=%async_computation | async-start | bytes 1572864 | tf_op jit(solution)/shard_map/all_to_all | solution.py:101
  37.0 1.6 %collective-permute-start = (f32[16,32,128]{2,0,1:T(8,128)S(1)}, f32[16,32,128]{2,0,1:T(8,128)S(1)}, u32[]{:S(2)}, u32[]{:S(2)}) collective-permute-start(f32[16,32,128]{2,0,1:T(8,128)S(1)} %slice.52), channel_id=1, source_target_pairs={{0,1},{1,0},{2,3},{3,2},{4,5},{5,4},{6,7},{7,6},{8,9},{9,8},{10,11... | collective-permute-start | bytes 786440 | tf_op jit(solution)/shard_map/ppermute | solution.py:106
  43.0 6.4 %copy-start = (bf16[256,512]{1,0:T(8,128)(2,1)S(1)}, bf16[256,512]{1,0:T(8,128)(2,1)}, u32[]{:S(2)}) copy-start(bf16[256,512]{1,0:T(8,128)(2,1)} %gate_ref.1) | copy-start | bytes 786436
  43.0 6.5 %copy-start.1 = (bf16[256,512]{1,0:T(8,128)(2,1)S(1)}, bf16[256,512]{1,0:T(8,128)(2,1)}, u32[]{:S(2)}) copy-start(bf16[256,512]{1,0:T(8,128)(2,1)} %values_ref.1) | copy-start | bytes 786436
  44.1 5.6 %copy-start.2 = (bf16[256,512]{1,0:T(8,128)(2,1)S(1)}, bf16[256,512]{1,0:T(8,128)(2,1)}, u32[]{:S(2)}) copy-start(bf16[256,512]{1,0:T(8,128)(2,1)} %param.7) | copy-start | bytes 786436
  44.1 23.4 %copy-start.3 = (f32[512]{0:T(512)S(1)}, f32[512]{0:T(512)}, u32[]{:S(2)}) copy-start(f32[512]{0:T(512)} %param.9) | copy-start | bytes 6148
  44.1 23.4 %all-to-all-start.1 = ((f32[16,32,256]{2,0,1:T(8,128)}), f32[16,32,256]{2,0,1:T(8,128)S(1)}, u32[]{:S(2)}, u32[]{:S(2)}) async-start(f32[16,32,256]{2,0,1:T(8,128)} %copy.12), calls=%async_computation.1 | async-start | bytes 1048576 | tf_op jit(solution)/shard_map/all_to_all | solution.py:115

commit v8 on v7

--- a/solution.py
+++ b/solution.py
@@ -58,6 +58,85 @@
     return y.reshape(y.shape[0], n) * (1.0 / (SIDE * SIDE))
 
 
+def split_bf16(x):
+    hi = x.astype(jnp.bfloat16)
+    return hi, (x - hi.astype(jnp.float32)).astype(jnp.bfloat16)
+
+
+def dot3_left(w_hi, w_lo, x):
+    x_hi, x_lo = split_bf16(x)
+    f32 = jnp.float32
+    return (
+        jnp.dot(w_hi, x_hi, preferred_element_type=f32)
+        + jnp.dot(w_lo, x_hi, preferred_element_type=f32)
+        + jnp.dot(w_hi, x_lo, preferred_element_type=f32)
+    )
+
+
+def dot3_right(x, w_hi, w_lo):
+    x_hi, x_lo = split_bf16(x)
+    f32 = jnp.float32
+    return (
+        jnp.dot(x_hi, w_hi, preferred_element_type=f32)
+        + jnp.dot(x_lo, w_hi, preferred_element_type=f32)
+        + jnp.dot(x_hi, w_lo, preferred_element_type=f32)
+    )
+
+
+def transform_kernel(
+    g_ref, h_ref, a_hi, a_lo, bf_hi, bf_lo, bi_hi, bi_lo, tc_ref, ts_ref, ai_hi, ai_lo, out_ref
+):
+    rows = tc_ref.shape[0]
+    tc, ts = tc_ref[...], ts_ref[...]
+    for c in range(g_ref.shape[0]):
+        x = jnp.concatenate([g_ref[c], h_ref[c]], axis=1)
+        a = dot3_left(a_hi[...], a_lo[...], x)
+        parts = []
+        for cols in (slice(0, SIDE), slice(SIDE, 2 * SIDE)):
+            a_re, a_im = a[:rows, cols], a[rows:, cols]
+            b_re = a_re * tc + a_im * ts
+            b_im = a_im * tc - a_re * ts
+            parts.append(jnp.concatenate([b_re, b_im], axis=1))
+        spec = dot3_right(jnp.concatenate(parts, axis=0), bf_hi[...], bf_lo[...])
+        g_re, g_im = spec[:rows, :SIDE], spec[:rows, SIDE:]
+        h_re, h_im = spec[rows:, :SIDE], spec[rows:, SIDE:]
+        prod = jnp.concatenate([g_re * h_re - g_im * h_im, g_re * h_im + g_im * h_re], axis=1)
+        q = dot3_right(prod, bi_hi[...], bi_lo[...])
+        q_re, q_im = q[:, :SIDE], q[:, SIDE:]
+        r = jnp.concatenate([q_re * tc - q_im * ts, q_im * tc + q_re * ts], axis=0)
+        out_ref[c] = dot3_left(ai_hi[...], ai_lo[...], r) * (1.0 / (SIDE * SIDE))
+
+
+def split_table(x):
+    hi = lax.reduce_precision(x, exponent_bits=8, mantissa_bits=7)
+    return hi.astype(jnp.bfloat16), (x - hi).astype(jnp.bfloat16)
+
+
+def fused_conv(gated_spread, taps_full):
+    ch, n = gated_spread.shape
+    filled = n // SIDE
+    stage_a, forward_b, inverse_b, twist_cos, twist_sin, stage_inv = dft_tables(filled)
+    tables = [
+        *split_table(stage_a),
+        *split_table(forward_b),
+        *split_table(inverse_b),
+        twist_cos,
+        twist_sin,
+        *split_table(stage_inv.T),
+    ]
+    per_step = 8
+    sig_block = pl.BlockSpec((per_step, filled, SIDE), lambda i: (i, 0, 0))
+    table_specs = [pl.BlockSpec(t.shape, lambda i: (0, 0)) for t in tables]
+    out = pl.pallas_call(
+        transform_kernel,
+        grid=(ch // per_step,),
+        in_specs=[sig_block, sig_block] + table_specs,
+        out_specs=sig_block,
+        out_shape=jax.ShapeDtypeStruct((ch, filled, SIDE), jnp.float32),
+    )(gated_spread.reshape(ch, filled, SIDE), taps_full.reshape(ch, filled, SIDE), *tables)
+    return out.reshape(ch, n)
+
+
 def prologue_kernel(core_ref, gate_ref, values_ref, taps_ref, out_ref):
     step = pl.program_id(0)
     gated_steps = pl.num_programs(0) - 1
@@ -104,14 +183,10 @@
     gated_spread = spread[:, :, :own_rows].reshape(ch, -1)
     mine = spread[:, :, own_rows:]
     theirs = lax.ppermute(mine, "grp", [(g, g ^ 1) for g in range(copies)])
-    n = gated_spread.shape[1]
-    tables = dft_tables(n // SIDE)
-    spec_g = spectrum(gated_spread, tables)
     first = jnp.where(core == 0, mine, theirs)
     second = jnp.where(core == 0, theirs, mine)
     taps_full = jnp.stack([first, second], axis=2).reshape(ch, -1)
-    spec_h = spectrum(taps_full, tables)
-    conv = inverse_prefix(spec_g, spec_h, tables, n)
+    conv = fused_conv(gated_spread, taps_full)
     back = lax.all_to_all(conv, "seq", split_axis=1, concat_axis=0, tiled=True)
     gated = in_gate.astype(jnp.float32) * values.astype(jnp.float32)
     total = back.T + skip_gain[None, :] * gated

time: 68.8 us -> 82.9 us (1.20)
  Pallas kernels: 2.73 us -> 16.4 us
  local copies, waits for them, and re-layouts: 3.33 us -> 8.99 us
  matrix products: 3.84 us -> 0 us
  waiting for transfers between devices: 40 us -> 36.9 us
  other arithmetic: 1.68 us -> 3.4 us
    pallas_call x0 -> x1, Pallas kernels: none -> 13.7 us  [fused_conv(): pl.pallas_call(transform_kernel, grid=(ch // per_step,), in_specs=[sig_bl...]
    dot_general x6 -> x0, matrix products: 3.84 us -> none  [the longest x2 1.48 us: spectrum(): a = jnp.einsum('kn,bnm->bkm', stage_a, x, precision=exact_mode)]
    all_to_all x0 -> x2, local copies, waits for them, and re-layouts: none -> 2.3 us  [local(): back = lax.all_to_all(conv, 'seq', split_axis=1, concat_axis=0, tiled=True)]
    convert_element_type x0 -> x3, other arithmetic: none -> 1.61 us  [split_table(): return (hi.astype(jnp.bfloat16), (x - hi).astype(jnp.bfloat16))]
    unnamed x11, local copies, waits for them, and re-layouts: 0.42 us -> 2.02 us
    all_to_all x1, waiting for transfers between devices: 21.9 us -> 20.5 us  [local(): lax.all_to_all(payload, 'seq', split_axis=0, concat_axis=1, tiled=True)]
    convert_element_type x0 -> x2, local copies, waits for them, and re-layouts: none -> 1.42 us  [split_table(): return (hi.astype(jnp.bfloat16), (x - hi).astype(jnp.bfloat16))]
    all_to_all x1, waiting for transfers between devices: 17.7 us -> 16.4 us  [local(): back = lax.all_to_all(conv, 'seq', split_axis=1, concat_axis=0, tiled=True)]
  transfers between devices with their start and end apart: 3 -> 3, of which waited for: 3 -> 2; matrix products, arithmetic and copies ran while one was open for 4% -> 7% of each run, Pallas kernels for 0% -> 0%
where the time goes in v8:
time: 82.9 us; the launch traced here: 82.5 us
  waiting for transfers between devices  36.9 us (45%)
  starting transfers between devices  16.7 us (20%)
  Pallas kernels  16.4 us (20%)
  local copies, waits for them, and re-layouts  8.99 us (11%)
  other arithmetic  3.4 us (4%)
    all_to_all x1, waiting for transfers between devices, local(): lax.all_to_all(payload, 'seq', split_axis=0, concat_axis=1, tiled=True)  20.5 us
    all_to_all x1, waiting for transfers between devices, local(): back = lax.all_to_all(conv, 'seq', split_axis=1, concat_axis=0, tiled=True)  16.4 us
    pallas_call x1, Pallas kernels, fused_conv(): pl.pallas_call(transform_kernel, grid=(ch // per_step,), in_specs=[sig_bl...  13.7 us
    all_to_all x1, starting transfers between devices, local(): lax.all_to_all(payload, 'seq', split_axis=0, concat_axis=1, tiled=True)  11.3 us
    all_to_all x1, starting transfers between devices, local(): back = lax.all_to_all(conv, 'seq', split_axis=1, concat_axis=0, tiled=True)  5.27 us
    pallas_call x1, Pallas kernels, prologue(): pl.pallas_call(prologue_kernel, grid_spec=grid_spec, out_shape=jax.ShapeD...  2.73 us
    all_to_all x2, local copies, waits for them, and re-layouts, local(): back = lax.all_to_all(conv, 'seq', split_axis=1, concat_axis=0, tiled=True)  2.3 us
    unnamed x11, local copies, waits for them, and re-layouts  2.02 us
  transfers between devices with their start and end apart: 3, of which 2 were waited for; matrix products, arithmetic and copies ran while one was open for 7% of the time, Pallas kernels for 0%

profile of v8, /device:TPU:8, one launch (start us, length us, event | category | flops | bytes accessed | tf_op | source)
XLA Modules:
  0.0 82.5 jit_solution(9314396967234480912)
XLA Ops:
  0.0 2.7 %shard_map.55 = f32[512,384]{1,0:T(8,128)} custom-call(s32[1]{0:T(128)} %bitcast.core_ref, bf16[256,512]{1,0:T(8,128)(2,1)} %gate_ref.1, bf16[256,512]{1,0:T(8,128)(2,1)} %values_ref.1, bf16[256,512]{1,0:T(8,128)(2,1)} %taps_ref.1), custom_call_target="tpu_custom_call" | custom-call | tf_op jit(solution)/shard_map/pallas_call | solution.py:167
  2.7 11.3 %all-to-all-start = ((f32[32,16,384]{2,1,0:T(8,128)}), f32[32,16,384]{2,1,0:T(8,128)S(1)}, u32[]{:S(2)}, u32[]{:S(2)}) async-start(f32[32,16,384]{2,1,0:T(8,128)} %bitcast.24), calls=%async_computation | async-start | bytes 1572864 | tf_op jit(solution)/shard_map/all_to_all | solution.py:180
  14.1 0.3 fusion.28
  14.3 0.1 sine_negate_fusion
  14.5 0.1 fusion.6
  14.6 0.8 fusion.29
  15.4 0.3 fusion.23
  15.7 0.8 fusion.5
  16.5 20.5 %all-to-all-done = f32[32,16,384]{2,1,0:T(8,128)S(1)} async-done(((f32[32,16,384]{2,1,0:T(8,128)}), f32[32,16,384]{2,1,0:T(8,128)S(1)}, u32[]{:S(2)}, u32[]{:S(2)}) %all-to-all-start) | async-done | bytes 786464 | tf_op jit(solution)/shard_map/all_to_all | solution.py:180
  37.0 0.1 collective-permute-start
  37.1 0.1 pad_maximum_fusion.6
  37.1 0.7 copy.23.a_hi
  37.9 0.7 copy.24.a_lo
  38.6 0.7 fusion.7
  39.3 0.1 slice.8
  39.3 0.3 copy.21
  39.6 0.8 reshape_reshape.6.g_ref
  40.5 0.0 collective-permute-done
  40.6 1.2 %copy.22 = f32[16,32,2,128]{3,2,1,0:T(2,128)} copy(f32[16,32,2,128]{3,0,1,2:T(8,128)S(1)} %pad_maximum_fusion) | data formatting | bytes 1048576 | tf_op jit(solution)/shard_map/stack | solution.py:188
  41.8 13.7 %shard_map.56 = f32[16,64,128]{2,1,0:T(8,128)} custom-call(f32[16,64,128]{2,1,0:T(8,128)} %reshape_reshape.6.g_ref, f32[16,64,128]{2,1,0:T(8,128)} %bitcast.25, bf16[144,64]{1,0:T(8,128)(2,1)} %copy.23.a_hi, bf16[144,64]{1,0:T(8,128)(2,1)} %copy.24.a_lo, bf16[256,256]{1,0:T(8,128)(2,1)} %get-tuple-element.9.bf_hi, bf16[256,256]{1,0:T(8,128)(2,1)} %get-tuple-element.8.bf_lo, ...), custom_call_target="tpu_custom_call" | custom-call | tf_op jit(solution)/shard_map/pallas_call | solution.py:130
  55.5 1.2 %all_to_all.29 = f32[16,32,256]{2,1,0:T(8,128)S(1)} reshape(f32[16,64,128]{2,1,0:T(8,128)} %shard_map.56) | data formatting | bytes 1048576 | tf_op jit(solution)/shard_map/all_to_all | solution.py:190
  56.7 1.1 %copy.25 = f32[16,32,256]{2,0,1:T(8,128)} copy(f32[16,32,256]{2,1,0:T(8,128)S(1)} %all_to_all.29) | data formatting | bytes 1048576 | tf_op jit(solution)/shard_map/all_to_all | solution.py:190
  57.8 5.3 %all-to-all-start.1 = ((f32[16,32,256]{2,0,1:T(8,128)}), f32[16,32,256]{2,0,1:T(8,128)S(1)}, u32[]{:S(2)}, u32[]{:S(2)}) async-start(f32[16,32,256]{2,0,1:T(8,128)} %copy.25), calls=%async_computation.1 | async-start | bytes 1048576 | tf_op jit(solution)/shard_map/all_to_all | solution.py:190
  63.1 0.0 copy-start.1
  63.1 0.1 copy.26
  63.2 0.8 copy-done.1
  64.0 0.1 copy.27
  64.1 0.8 copy-done.2
  65.0 0.1 copy.20
  65.1 16.4 %all-to-all-done.1 = f32[16,32,256]{2,0,1:T(8,128)S(1)} async-done(((f32[16,32,256]{2,0,1:T(8,128)}), f32[16,32,256]{2,0,1:T(8,128)S(1)}, u32[]{:S(2)}, u32[]{:S(2)}) %all-to-all-start.1) | async-done | bytes 524320 | tf_op jit(solution)/shard_map/all_to_all | solution.py:190
  81.5 0.2 fusion.1
  81.7 0.8 %copy.28 = bf16[256,512]{1,0:T(8,128)(2,1)} copy(bf16[256,512]{0,1:T(8,128)(2,1)S(1)} %fusion.1) | data formatting | bytes 524288 | tf_op jit(solution)/shard_map/convert_element_type | solution.py:193
  (9 shorter events, 0.1 us)
Async XLA Ops:
  2.7 34.2 %all-to-all-start = ((f32[32,16,384]{2,1,0:T(8,128)}), f32[32,16,384]{2,1,0:T(8,128)S(1)}, u32[]{:S(2)}, u32[]{:S(2)}) async-start(f32[32,16,384]{2,1,0:T(8,128)} %bitcast.24), calls=%async_computation | async-start | bytes 1572864 | tf_op jit(solution)/shard_map/all_to_all | solution.py:180
  37.0 3.5 %collective-permute-start = (f32[16,32,128]{2,0,1:T(8,128)S(1)}, f32[16,32,128]{2,0,1:T(8,128)S(1)}, u32[]{:S(2)}, u32[]{:S(2)}) collective-permute-start(f32[16,32,128]{2,0,1:T(8,128)S(1)} %slice.9), channel_id=1, source_target_pairs={{0,1},{1,0},{2,3},{3,2},{4,5},{5,4},{6,7},{7,6},{8,9},{9,8},{10,11... | collective-permute-start | bytes 786440 | tf_op jit(solution)/shard_map/ppermute | solution.py:185
  57.8 5.3 %copy-start = (bf16[256,512]{1,0:T(8,128)(2,1)S(1)}, bf16[256,512]{1,0:T(8,128)(2,1)}, u32[]{:S(2)}) copy-start(bf16[256,512]{1,0:T(8,128)(2,1)} %gate_ref.1) | copy-start | bytes 786436
  57.8 23.7 %all-to-all-start.1 = ((f32[16,32,256]{2,0,1:T(8,128)}), f32[16,32,256]{2,0,1:T(8,128)S(1)}, u32[]{:S(2)}, u32[]{:S(2)}) async-start(f32[16,32,256]{2,0,1:T(8,128)} %copy.25), calls=%async_computation.1 | async-start | bytes 1048576 | tf_op jit(solution)/shard_map/all_to_all | solution.py:190
  63.1 1.0 %copy-start.1 = (bf16[256,512]{1,0:T(8,128)(2,1)S(1)}, bf16[256,512]{1,0:T(8,128)(2,1)}, u32[]{:S(2)}) copy-start(bf16[256,512]{1,0:T(8,128)(2,1)} %values_ref.1) | copy-start | bytes 786436
  64.0 0.9 %copy-start.2 = (bf16[256,512]{1,0:T(8,128)(2,1)S(1)}, bf16[256,512]{1,0:T(8,128)(2,1)}, u32[]{:S(2)}) copy-start(bf16[256,512]{1,0:T(8,128)(2,1)} %param.7) | copy-start | bytes 786436
  65.0 16.5 %copy-start.3 = (f32[512]{0:T(512)S(1)}, f32[512]{0:T(512)}, u32[]{:S(2)}) copy-start(f32[512]{0:T(512)} %param.9) | copy-start | bytes 6148

commit v9 on v7

--- a/solution.py
+++ b/solution.py
@@ -25,7 +25,7 @@
     twist = angle_table(rows, SIDE, SIDE * SIDE)
     row = jnp.arange(rows, dtype=jnp.int32)
     weight = jnp.where((row == 0) | (row == SIDE // 2), 1.0, jnp.where(row < SIDE // 2, 2.0, 0.0))
-    stage_inv = stage_a * jnp.concatenate([weight, weight])[:, None]
+    stage_inv = stage_a * (jnp.concatenate([weight, weight])[:, None] / (SIDE * SIDE))
     return stage_a, forward_b, inverse_b, jnp.cos(twist), jnp.sin(twist), stage_inv
 
 
@@ -55,21 +55,33 @@
     y = jnp.einsum(
         "kn,bkm->bnm", stage_inv, jnp.concatenate([r_re, r_im], axis=1), precision=exact_mode
     )
-    return y.reshape(y.shape[0], n) * (1.0 / (SIDE * SIDE))
+    return y.reshape(y.shape[0], n)
 
 
 def prologue_kernel(core_ref, gate_ref, values_ref, taps_ref, out_ref):
     step = pl.program_id(0)
     gated_steps = pl.num_programs(0) - 1
 
+    rows = gate_ref.shape[0]
+    eye = (
+        lax.broadcasted_iota(jnp.int32, (rows, rows), 0)
+        == lax.broadcasted_iota(jnp.int32, (rows, rows), 1)
+    ).astype(jnp.bfloat16)
+    dims = (((0,), (0,)), ((), ()))
+
+    def flip(x):
+        return lax.dot_general(x, eye, dims, preferred_element_type=jnp.float32)
+
     @pl.when(step < gated_steps)
     def _():
         gated = gate_ref[...].astype(jnp.float32) * values_ref[...].astype(jnp.float32)
-        out_ref[...] = gated.T
+        high = gated.astype(jnp.bfloat16)
+        low = (gated - high.astype(jnp.float32)).astype(jnp.bfloat16)
+        out_ref[...] = flip(high) + flip(low)
 
     @pl.when(step == gated_steps)
     def _():
-        out_ref[...] = taps_ref[...].astype(jnp.float32).T
+        out_ref[...] = flip(taps_ref[...])
 
 
 def prologue(core, in_gate, values, filter_taps):

time: 68.8 us -> 69 us (level)
    mul x2 -> x0, local copies, waits for them, and re-layouts: 1.25 us -> none  [inverse_prefix(): return y.reshape(y.shape[0], n) * (1.0 / (SIDE * SIDE))]
    all_to_all x0 -> x2, local copies, waits for them, and re-layouts: none -> 1.25 us  [local(): back = lax.all_to_all(conv, 'seq', split_axis=1, concat_axis=0, tiled=True)]
  transfers between devices with their start and end apart: 3 -> 3, of which waited for: 3 -> 3; matrix products, arithmetic and copies ran while one was open for 4% -> 3% of each run, Pallas kernels for 0% -> 0%
where the time goes in v9:
time: 69 us; the launch traced here: 68.8 us
  waiting for transfers between devices  40 us (58%)
  starting transfers between devices  16.7 us (24%)
  matrix products  3.84 us (6%)
  local copies, waits for them, and re-layouts  3.33 us (5%)
  Pallas kernels  2.98 us (4%)
  other arithmetic  1.68 us (2%)
    all_to_all x1, waiting for transfers between devices, local(): lax.all_to_all(payload, 'seq', split_axis=0, concat_axis=1, tiled=True)  21.9 us
    all_to_all x1, waiting for transfers between devices, local(): back = lax.all_to_all(conv, 'seq', split_axis=1, concat_axis=0, tiled=True)  17.7 us
    all_to_all x1, starting transfers between devices, local(): lax.all_to_all(payload, 'seq', split_axis=0, concat_axis=1, tiled=True)  11.3 us
    all_to_all x1, starting transfers between devices, local(): back = lax.all_to_all(conv, 'seq', split_axis=1, concat_axis=0, tiled=True)  5.26 us
    pallas_call x1, Pallas kernels, prologue(): pl.pallas_call(prologue_kernel, grid_spec=grid_spec, out_shape=jax.ShapeD...  2.98 us
    dot_general x2, matrix products, spectrum(): a = jnp.einsum('kn,bnm->bkm', stage_a, x, precision=exact_mode)  1.48 us
  transfers between devices with their start and end apart: 3, of which 3 were waited for; matrix products, arithmetic and copies ran while one was open for 3% of the time, Pallas kernels for 0%

profile of v9, /device:TPU:8, one launch (start us, length us, event | category | flops | bytes accessed | tf_op | source)
XLA Modules:
  0.0 68.8 jit_solution(11953189843224368796)
XLA Ops:
  0.0 3.0 %shard_map.55 = f32[512,384]{1,0:T(8,128)} custom-call(s32[1]{0:T(128)} %bitcast.core_ref, bf16[256,512]{1,0:T(8,128)(2,1)} %gate_ref.1, bf16[256,512]{1,0:T(8,128)(2,1)} %values_ref.1, bf16[256,512]{1,0:T(8,128)(2,1)} %taps_ref.1), custom_call_target="tpu_custom_call" | custom-call | tf_op jit(solution)/shard_map/pallas_call | solution.py:100
  3.0 11.3 %all-to-all-start = ((f32[32,16,384]{2,1,0:T(8,128)}), f32[32,16,384]{2,1,0:T(8,128)S(1)}, u32[]{:S(2)}, u32[]{:S(2)}) async-start(f32[32,16,384]{2,1,0:T(8,128)} %bitcast.44), calls=%async_computation | async-start | bytes 1572864 | tf_op jit(solution)/shard_map/all_to_all | solution.py:113
  14.3 0.1 maximum_multiply_fusion
  14.4 0.1 sine_negate_fusion
  14.6 0.3 fusion.51
  14.8 0.2 fusion.52
  15.0 0.3 fusion.46
  15.3 21.9 %all-to-all-done = f32[32,16,384]{2,1,0:T(8,128)S(1)} async-done(((f32[32,16,384]{2,1,0:T(8,128)}), f32[32,16,384]{2,1,0:T(8,128)S(1)}, u32[]{:S(2)}, u32[]{:S(2)}) %all-to-all-start) | async-done | bytes 786464 | tf_op jit(solution)/shard_map/all_to_all | solution.py:113
  37.2 0.1 slice.48
  37.3 0.1 collective-permute-start
  37.4 0.3 copy.10
  37.7 0.7 %convolution_bitcast_fusion.1 = f32[16,144,128]{2,1,0:T(8,128)S(1)} fusion(f32[16,64,128]{2,1,0:T(8,128)S(1)} %reshape_reshape.6, f32[72,64]{0,1:T(8,128)S(1)} %get-tuple-element.17, f32[72,64]{0,1:T(8,128)S(1)} %get-tuple-element.18), kind=kOutput, calls=%fused_computation.1 | convolution fusion | flops 113255424 | bytes 1740800 | tf_op jit(solution)/shard_map/kn,bnm->bkm/dot_general | solution.py:37
  38.5 0.4 collective-permute-done
  38.9 0.1 select_bitcast_fusion.1
  39.0 0.4 copy.11
  39.4 0.7 %convolution_bitcast_fusion = f32[16,144,128]{2,1,0:T(8,128)S(1)} fusion(f32[16,64,128]{2,1,0:T(8,128)S(1)} %bitcast.45, f32[72,64]{0,1:T(8,128)S(1)} %get-tuple-element.17, f32[72,64]{0,1:T(8,128)S(1)} %get-tuple-element.18), kind=kOutput, calls=%fused_computation | convolution fusion | flops 113255424 | bytes 1740800 | tf_op jit(solution)/shard_map/kn,bnm->bkm/dot_general | solution.py:37
  40.2 0.2 multiply_add_fusion.3
  40.4 0.6 fusion
  41.1 0.6 fusion.4
  41.7 0.1 multiply_subtract_fusion.1
  41.8 0.6 fusion.8
  42.5 0.1 multiply_subtract_fusion
  42.6 0.5 convolution_bitcast_fusion.2
  43.1 0.1 all_to_all.29
  43.3 1.1 %copy.12 = f32[16,32,256]{2,0,1:T(8,128)} copy(f32[16,32,256]{2,1,0:T(8,128)S(1)} %all_to_all.29) | data formatting | bytes 1048576 | tf_op jit(solution)/shard_map/all_to_all | solution.py:127
  44.4 5.3 %all-to-all-start.1 = ((f32[16,32,256]{2,0,1:T(8,128)}), f32[16,32,256]{2,0,1:T(8,128)S(1)}, u32[]{:S(2)}, u32[]{:S(2)}) async-start(f32[16,32,256]{2,0,1:T(8,128)} %copy.12), calls=%async_computation.1 | async-start | bytes 1048576 | tf_op jit(solution)/shard_map/all_to_all | solution.py:127
  49.6 0.1 copy.13
  49.8 0.1 copy.14
  49.9 0.1 copy.9
  50.1 17.7 %all-to-all-done.1 = f32[16,32,256]{2,0,1:T(8,128)S(1)} async-done(((f32[16,32,256]{2,0,1:T(8,128)}), f32[16,32,256]{2,0,1:T(8,128)S(1)}, u32[]{:S(2)}, u32[]{:S(2)}) %all-to-all-start.1) | async-done | bytes 524320 | tf_op jit(solution)/shard_map/all_to_all | solution.py:127
  67.7 0.2 fusion.16
  67.9 0.8 %copy.15 = bf16[256,512]{1,0:T(8,128)(2,1)} copy(bf16[256,512]{0,1:T(8,128)(2,1)S(1)} %fusion.16) | data formatting | bytes 524288 | tf_op jit(solution)/shard_map/convert_element_type | solution.py:130
  (12 shorter events, 0.1 us)
Async XLA Ops:
  3.0 34.2 %all-to-all-start = ((f32[32,16,384]{2,1,0:T(8,128)}), f32[32,16,384]{2,1,0:T(8,128)S(1)}, u32[]{:S(2)}, u32[]{:S(2)}) async-start(f32[32,16,384]{2,1,0:T(8,128)} %bitcast.44), calls=%async_computation | async-start | bytes 1572864 | tf_op jit(solution)/shard_map/all_to_all | solution.py:113
  37.3 1.6 %collective-permute-start = (f32[16,32,128]{2,0,1:T(8,128)S(1)}, f32[16,32,128]{2,0,1:T(8,128)S(1)}, u32[]{:S(2)}, u32[]{:S(2)}) collective-permute-start(f32[16,32,128]{2,0,1:T(8,128)S(1)} %slice.52), channel_id=1, source_target_pairs={{0,1},{1,0},{2,3},{3,2},{4,5},{5,4},{6,7},{7,6},{8,9},{9,8},{10,11... | collective-permute-start | bytes 786440 | tf_op jit(solution)/shard_map/ppermute | solution.py:118
  43.2 6.4 %copy-start = (bf16[256,512]{1,0:T(8,128)(2,1)S(1)}, bf16[256,512]{1,0:T(8,128)(2,1)}, u32[]{:S(2)}) copy-start(bf16[256,512]{1,0:T(8,128)(2,1)} %gate_ref.1) | copy-start | bytes 786436
  43.3 6.5 %copy-start.1 = (bf16[256,512]{1,0:T(8,128)(2,1)S(1)}, bf16[256,512]{1,0:T(8,128)(2,1)}, u32[]{:S(2)}) copy-start(bf16[256,512]{1,0:T(8,128)(2,1)} %values_ref.1) | copy-start | bytes 786436
  44.4 5.6 %copy-start.2 = (bf16[256,512]{1,0:T(8,128)(2,1)S(1)}, bf16[256,512]{1,0:T(8,128)(2,1)}, u32[]{:S(2)}) copy-start(bf16[256,512]{1,0:T(8,128)(2,1)} %param.7) | copy-start | bytes 786436
  44.4 23.4 %copy-start.3 = (f32[512]{0:T(512)S(1)}, f32[512]{0:T(512)}, u32[]{:S(2)}) copy-start(f32[512]{0:T(512)} %param.9) | copy-start | bytes 6148
  44.4 23.4 %all-to-all-start.1 = ((f32[16,32,256]{2,0,1:T(8,128)}), f32[16,32,256]{2,0,1:T(8,128)S(1)}, u32[]{:S(2)}, u32[]{:S(2)}) async-start(f32[16,32,256]{2,0,1:T(8,128)} %copy.12), calls=%async_computation.1 | async-start | bytes 1048576 | tf_op jit(solution)/shard_map/all_to_all | solution.py:127

commit v10 on v7

--- a/solution.py
+++ b/solution.py
@@ -58,58 +58,49 @@
     return y.reshape(y.shape[0], n) * (1.0 / (SIDE * SIDE))
 
 
-def prologue_kernel(core_ref, gate_ref, values_ref, taps_ref, out_ref):
-    step = pl.program_id(0)
-    gated_steps = pl.num_programs(0) - 1
-
-    @pl.when(step < gated_steps)
-    def _():
-        gated = gate_ref[...].astype(jnp.float32) * values_ref[...].astype(jnp.float32)
-        out_ref[...] = gated.T
-
-    @pl.when(step == gated_steps)
-    def _():
-        out_ref[...] = taps_ref[...].astype(jnp.float32).T
+def prologue_kernel(gate_ref, values_ref, out_ref):
+    gated = gate_ref[...].astype(jnp.float32) * values_ref[...].astype(jnp.float32)
+    out_ref[...] = gated.T
 
 
-def prologue(core, in_gate, values, filter_taps):
+def prologue(in_gate, values):
     rows, channels = in_gate.shape
-    half = rows // 2
-    gated_steps = rows // half
-    last = gated_steps - 1
-    row_block = pl.BlockSpec((half, channels), lambda j, c: (jnp.minimum(j, last), 0))
-    taps_block = pl.BlockSpec((half, channels), lambda j, c: (c[0], 0))
-    grid_spec = pltpu.PrefetchScalarGridSpec(
-        num_scalar_prefetch=1,
-        grid=(gated_steps + 1,),
-        in_specs=[row_block, row_block, taps_block],
-        out_specs=pl.BlockSpec((channels, half), lambda j, c: (0, j)),
-    )
+    block = rows // 2
     return pl.pallas_call(
         prologue_kernel,
-        grid_spec=grid_spec,
-        out_shape=jax.ShapeDtypeStruct((channels, rows + half), jnp.float32),
-    )(core.reshape(1), in_gate, values, filter_taps)
+        grid=(rows // block,),
+        in_specs=[pl.BlockSpec((block, channels), lambda j: (j, 0))] * 2,
+        out_specs=pl.BlockSpec((channels, block), lambda j: (0, j)),
+        out_shape=jax.ShapeDtypeStruct((channels, rows), jnp.float32),
+    )(in_gate, values)
 
 
 def local(in_gate, values, out_gate, filter_taps, skip_gain):
     own_rows, channels = in_gate.shape
     copies = lax.axis_size("grp")
-    core = lax.axis_index("grp") % 2
-    half = own_rows // 2
-    payload = prologue(core.astype(jnp.int32), in_gate, values, filter_taps)
-    spread = lax.all_to_all(payload, "seq", split_axis=0, concat_axis=1, tiled=True)
-    ch = spread.shape[0]
-    spread = spread.reshape(ch, -1, own_rows + half)
-    gated_spread = spread[:, :, :own_rows].reshape(ch, -1)
-    mine = spread[:, :, own_rows:]
-    theirs = lax.ppermute(mine, "grp", [(g, g ^ 1) for g in range(copies)])
+    groups = lax.axis_size("seq")
+    ch = channels // groups
+    quarter = lax.axis_index("grp") % 4
+    share = ch // 4
+    gated_t = prologue(in_gate, values).reshape(groups, ch, own_rows)
+    taps = filter_taps.astype(jnp.float32).reshape(own_rows, groups, 4, share)
+    taps_part = lax.dynamic_index_in_dim(taps, quarter, axis=2, keepdims=False)
+    payload = jnp.concatenate([gated_t, jnp.transpose(taps_part, (1, 2, 0))], axis=1)
+    spread = lax.all_to_all(payload, "seq", split_axis=0, concat_axis=0, tiled=True)
+    gated_spread = jnp.transpose(spread[:, :ch], (1, 0, 2)).reshape(ch, -1)
+    mine = jnp.transpose(spread[:, ch:], (1, 0, 2)).reshape(share, -1)
+    across = lax.ppermute(mine, "grp", [(g, g ^ 2) for g in range(copies)])
+    pair = lax.ppermute(jnp.stack([mine, across]), "grp", [(g, g ^ 1) for g in range(copies)])
     n = gated_spread.shape[1]
     tables = dft_tables(n // SIDE)
     spec_g = spectrum(gated_spread, tables)
-    first = jnp.where(core == 0, mine, theirs)
-    second = jnp.where(core == 0, theirs, mine)
-    taps_full = jnp.stack([first, second], axis=2).reshape(ch, -1)
+    pieces = []
+    for j in range(4):
+        t = quarter ^ j
+        pieces.append(
+            jnp.where(t == 0, mine, jnp.where(t == 2, across, jnp.where(t == 1, pair[0], pair[1])))
+        )
+    taps_full = jnp.concatenate(pieces, axis=0)
     spec_h = spectrum(taps_full, tables)
     conv = inverse_prefix(spec_g, spec_h, tables, n)
     back = lax.all_to_all(conv, "seq", split_axis=1, concat_axis=0, tiled=True)

time: 68.8 us -> 76.4 us (1.11)
  waiting for transfers between devices: 40 us -> 44.4 us
  other arithmetic: 1.68 us -> 3.94 us
  local copies, waits for them, and re-layouts: 3.33 us -> 4.28 us
    ppermute x1 -> x2, waiting for transfers between devices: 0.42 us -> 4.88 us  [the longest x1 4.1 us: local(): across = lax.ppermute(mine, 'grp', [(g, g ^ 2) for g in range(copies)])]
    concatenate x0 -> x1, other arithmetic: none -> 2.01 us  [local(): jnp.concatenate([gated_t, jnp.transpose(taps_part, (1, 2, 0))], axis=1)]
    reshape x0 -> x2, local copies, waits for them, and re-layouts: none -> 1.23 us  [local(): taps = filter_taps.astype(jnp.float32).reshape(own_rows, groups, 4, share)]
  transfers between devices with their start and end apart: 3 -> 4, of which waited for: 3 -> 4; matrix products, arithmetic and copies ran while one was open for 4% -> 3% of each run, Pallas kernels for 0% -> 0%
where the time goes in v10:
time: 76.4 us; the launch traced here: 76 us
  waiting for transfers between devices  44.4 us (58%)
  starting transfers between devices  17.2 us (23%)
  local copies, waits for them, and re-layouts  4.28 us (6%)
  other arithmetic  3.94 us (5%)
  matrix products  3.84 us (5%)
  Pallas kernels  1.97 us (3%)
    all_to_all x1, waiting for transfers between devices, local(): lax.all_to_all(payload, 'seq', split_axis=0, concat_axis=0, tiled=True)  21.9 us
    all_to_all x1, waiting for transfers between devices, local(): back = lax.all_to_all(conv, 'seq', split_axis=1, concat_axis=0, tiled=True)  17.7 us
    all_to_all x1, starting transfers between devices, local(): lax.all_to_all(payload, 'seq', split_axis=0, concat_axis=0, tiled=True)  11.3 us
    all_to_all x1, starting transfers between devices, local(): back = lax.all_to_all(conv, 'seq', split_axis=1, concat_axis=0, tiled=True)  5.26 us
    ppermute x1, waiting for transfers between devices, local(): across = lax.ppermute(mine, 'grp', [(g, g ^ 2) for g in range(copies)])  4.1 us
    concatenate x1, other arithmetic, local(): jnp.concatenate([gated_t, jnp.transpose(taps_part, (1, 2, 0))], axis=1)  2.01 us
    pallas_call x1, Pallas kernels, prologue(): pl.pallas_call(prologue_kernel, grid=(rows // block,), in_specs=[pl.Block...  1.97 us
  transfers between devices with their start and end apart: 4, of which 4 were waited for; matrix products, arithmetic and copies ran while one was open for 3% of the time, Pallas kernels for 0%

profile of v10, /device:TPU:8, one launch (start us, length us, event | category | flops | bytes accessed | tf_op | source)
XLA Modules:
  0.0 76.0 jit_solution(11337567759590626100)
XLA Ops:
  0.0 1.1 %copy.10 = f32[256,512]{0,1:T(8,128)S(1)} copy(bf16[256,512]{1,0:T(8,128)(2,1)} %param.8) | data formatting | bytes 786432 | tf_op jit(solution)/shard_map/reshape | solution.py:86
  1.1 0.1 reshape.74
  1.3 2.0 %shard_map.55 = f32[512,256]{1,0:T(8,128)} custom-call(bf16[256,512]{1,0:T(8,128)(2,1)} %gate_ref.1, bf16[256,512]{1,0:T(8,128)(2,1)} %values_ref.1), custom_call_target="tpu_custom_call" | custom-call | tf_op jit(solution)/shard_map/pallas_call | solution.py:69
  3.3 2.0 %pad_maximum_fusion = f32[32,20,256]{2,1,0:T(8,128)} fusion(f32[32,4,256]{2,1,0:T(4,128)S(1)} %dynamic-slice_bitcast_fusion, f32[32,16,256]{2,1,0:T(8,128)} %bitcast.72), kind=kLoop, calls=%fused_computation.19 | loop fusion | flops 163840 | bytes 1310720 | tf_op jit(solution)/shard_map/concatenate | solution.py:88
  5.3 11.3 %all-to-all-start = ((f32[32,20,256]{2,1,0:T(8,128)}), f32[32,20,256]{2,1,0:T(8,128)S(1)}, u32[]{:S(2)}, u32[]{:S(2)}) async-start(f32[32,20,256]{2,1,0:T(8,128)} %pad_maximum_fusion), calls=%async_computation | async-start | bytes 1572864 | tf_op jit(solution)/shard_map/all_to_all | solution.py:89
  16.7 0.1 sine_negate_fusion
  16.9 0.3 fusion.56
  17.1 0.2 fusion.57
  17.3 0.3 fusion.51
  17.6 21.9 %all-to-all-done = f32[32,20,256]{2,1,0:T(8,128)S(1)} async-done(((f32[32,20,256]{2,1,0:T(8,128)}), f32[32,20,256]{2,1,0:T(8,128)S(1)}, u32[]{:S(2)}, u32[]{:S(2)}) %all-to-all-start) | async-done | bytes 655392 | tf_op jit(solution)/shard_map/all_to_all | solution.py:89
  39.5 0.5 collective-permute-start
  40.1 0.3 copy.11
  40.4 4.1 %collective-permute-done = f32[4,8192]{1,0:T(4,128)S(1)} collective-permute-done((f32[4,8192]{1,0:T(4,128)S(1)}, f32[4,8192]{1,0:T(4,128)S(1)}, u32[]{:S(2)}, u32[]{:S(2)}) %collective-permute-start) | collective-permute-done | bytes 131104 | tf_op jit(solution)/shard_map/ppermute | solution.py:92
  44.7 0.7 convolution_bitcast_fusion.1
  45.5 0.8 %collective-permute-done.1 = f32[2,4,8192]{2,1,0:T(4,128)S(1)} collective-permute-done((f32[2,4,8192]{2,1,0:T(4,128)S(1)}, f32[2,4,8192]{2,1,0:T(4,128)S(1)}, u32[]{:S(2)}, u32[]{:S(2)}) %collective-permute-start.1) | collective-permute-done | bytes 262176 | tf_op jit(solution)/shard_map/ppermute | solution.py:93
  46.6 0.7 convolution_bitcast_fusion
  47.4 0.2 multiply_add_fusion.3
  47.6 0.6 fusion.1
  48.3 0.6 fusion.5
  48.9 0.1 multiply_subtract_fusion.1
  49.1 0.6 fusion.9
  49.7 0.1 multiply_subtract_fusion
  49.8 0.5 fusion
  50.3 0.1 mul.404
  50.5 1.1 %copy.12 = f32[16,32,256]{2,0,1:T(8,128)} copy(f32[16,32,256]{2,1,0:T(8,128)S(1)} %mul.404) | data formatting | bytes 1048576 | tf_op jit(solution)/shard_map/mul | solution.py:58
  51.6 5.3 %all-to-all-start.1 = ((f32[16,32,256]{2,0,1:T(8,128)}), f32[16,32,256]{2,0,1:T(8,128)S(1)}, u32[]{:S(2)}, u32[]{:S(2)}) async-start(f32[16,32,256]{2,0,1:T(8,128)} %copy.12), calls=%async_computation.1 | async-start | bytes 1048576 | tf_op jit(solution)/shard_map/all_to_all | solution.py:106
  56.9 0.1 copy.13
  57.0 0.1 copy.14
  57.2 0.1 copy.9
  57.3 17.7 %all-to-all-done.1 = f32[16,32,256]{2,0,1:T(8,128)S(1)} async-done(((f32[16,32,256]{2,0,1:T(8,128)}), f32[16,32,256]{2,0,1:T(8,128)S(1)}, u32[]{:S(2)}, u32[]{:S(2)}) %all-to-all-start.1) | async-done | bytes 524320 | tf_op jit(solution)/shard_map/all_to_all | solution.py:106
  75.0 0.2 fusion.17
  75.1 0.8 %copy.15 = bf16[256,512]{1,0:T(8,128)(2,1)} copy(bf16[256,512]{0,1:T(8,128)(2,1)S(1)} %fusion.17) | data formatting | bytes 524288 | tf_op jit(solution)/shard_map/convert_element_type | solution.py:109
  (20 shorter events, 0.8 us)
Async XLA Ops:
  5.3 34.2 %all-to-all-start = ((f32[32,20,256]{2,1,0:T(8,128)}), f32[32,20,256]{2,1,0:T(8,128)S(1)}, u32[]{:S(2)}, u32[]{:S(2)}) async-start(f32[32,20,256]{2,1,0:T(8,128)} %pad_maximum_fusion), calls=%async_computation | async-start | bytes 1572864 | tf_op jit(solution)/shard_map/all_to_all | solution.py:89
  39.5 5.1 %collective-permute-start = (f32[4,8192]{1,0:T(4,128)S(1)}, f32[4,8192]{1,0:T(4,128)S(1)}, u32[]{:S(2)}, u32[]{:S(2)}) collective-permute-start(f32[4,8192]{1,0:T(4,128)S(1)} %bitcast.68), channel_id=1, source_target_pairs={{0,2},{1,3},{2,0},{3,1},{4,6},{5,7},{6,4},{7,5},{8,10},{9,11},{10,... | collective-permute-start | bytes 393224 | tf_op jit(solution)/shard_map/ppermute | solution.py:92
  44.6 1.6 %collective-permute-start.1 = (f32[2,4,8192]{2,1,0:T(4,128)S(1)}, f32[2,4,8192]{2,1,0:T(4,128)S(1)}, u32[]{:S(2)}, u32[]{:S(2)}) collective-permute-start(f32[2,4,8192]{2,1,0:T(4,128)S(1)} %pad_maximum_fusion.6), channel_id=1, source_target_pairs={{0,1},{1,0},{2,3},{3,2},{4,5},{5,4},{6,7},{7,6},{8,9},{9,8},{10,11... | collective-permute-start | bytes 786440 | tf_op jit(solution)/shard_map/ppermute | solution.py:93
  50.5 6.4 %copy-start = (bf16[256,512]{1,0:T(8,128)(2,1)S(1)}, bf16[256,512]{1,0:T(8,128)(2,1)}, u32[]{:S(2)}) copy-start(bf16[256,512]{1,0:T(8,128)(2,1)} %gate_ref.1) | copy-start | bytes 786436
  50.5 6.5 %copy-start.1 = (bf16[256,512]{1,0:T(8,128)(2,1)S(1)}, bf16[256,512]{1,0:T(8,128)(2,1)}, u32[]{:S(2)}) copy-start(bf16[256,512]{1,0:T(8,128)(2,1)} %values_ref.1) | copy-start | bytes 786436
  51.6 5.6 %copy-start.2 = (bf16[256,512]{1,0:T(8,128)(2,1)S(1)}, bf16[256,512]{1,0:T(8,128)(2,1)}, u32[]{:S(2)}) copy-start(bf16[256,512]{1,0:T(8,128)(2,1)} %param.7) | copy-start | bytes 786436
  51.6 23.4 %copy-start.3 = (f32[512]{0:T(512)S(1)}, f32[512]{0:T(512)}, u32[]{:S(2)}) copy-start(f32[512]{0:T(512)} %param.9) | copy-start | bytes 6148
  51.6 23.4 %all-to-all-start.1 = ((f32[16,32,256]{2,0,1:T(8,128)}), f32[16,32,256]{2,0,1:T(8,128)S(1)}, u32[]{:S(2)}, u32[]{:S(2)}) async-start(f32[16,32,256]{2,0,1:T(8,128)} %copy.12), calls=%async_computation.1 | async-start | bytes 1048576 | tf_op jit(solution)/shard_map/all_to_all | solution.py:106

commit v11 on v7

--- a/solution.py
+++ b/solution.py
@@ -92,6 +92,22 @@
     )(core.reshape(1), in_gate, values, filter_taps)
 
 
+def regroup_kernel(x_ref, out_ref):
+    width = out_ref.shape[2]
+    for d in range(out_ref.shape[0]):
+        out_ref[d] = x_ref[:, d * width:(d + 1) * width]
+
+
+def regroup(x, groups):
+    ch, n = x.shape
+    return pl.pallas_call(
+        regroup_kernel,
+        in_specs=[pl.BlockSpec(memory_space=pltpu.VMEM)],
+        out_specs=pl.BlockSpec(memory_space=pltpu.VMEM),
+        out_shape=jax.ShapeDtypeStruct((groups, ch, n // groups), x.dtype),
+    )(x)
+
+
 def local(in_gate, values, out_gate, filter_taps, skip_gain):
     own_rows, channels = in_gate.shape
     copies = lax.axis_size("grp")
@@ -112,7 +128,9 @@
     taps_full = jnp.stack([first, second], axis=2).reshape(ch, -1)
     spec_h = spectrum(taps_full, tables)
     conv = inverse_prefix(spec_g, spec_h, tables, n)
-    back = lax.all_to_all(conv, "seq", split_axis=1, concat_axis=0, tiled=True)
+    groups = lax.axis_size("seq")
+    back = lax.all_to_all(regroup(conv, groups), "seq", split_axis=0, concat_axis=0, tiled=True)
+    back = back.reshape(channels, own_rows)
     gated = in_gate.astype(jnp.float32) * values.astype(jnp.float32)
     total = back.T + skip_gain[None, :] * gated
     return (out_gate.astype(jnp.float32) * total).astype(jnp.bfloat16)

time: 68.8 us -> 70.7 us (1.028)
  blocking collectives: 0 us -> 23.4 us
  waiting for transfers between devices: 40 us -> 22.3 us
  starting transfers between devices: 16.7 us -> 11.4 us
  Pallas kernels: 2.73 us -> 4.63 us
  local copies, waits for them, and re-layouts: 3.33 us -> 2.14 us
    all_to_all x0 -> x1, blocking collectives: none -> 23.4 us  [local(): lax.all_to_all(regroup(conv, groups), 'seq', split_axis=0, concat_axis=0,...]
    all_to_all x1 -> x0, waiting for transfers between devices: 17.7 us -> none  [local(): back = lax.all_to_all(conv, 'seq', split_axis=1, concat_axis=0, tiled=True)]
    all_to_all x1 -> x0, starting transfers between devices: 5.26 us -> none  [local(): back = lax.all_to_all(conv, 'seq', split_axis=1, concat_axis=0, tiled=True)]
    pallas_call x0 -> x1, Pallas kernels: none -> 1.86 us  [regroup(): pl.pallas_call(regroup_kernel, in_specs=[pl.BlockSpec(memory_space=pltpu....]
    mul x2 -> x0, local copies, waits for them, and re-layouts: 1.25 us -> none  [inverse_prefix(): return y.reshape(y.shape[0], n) * (1.0 / (SIDE * SIDE))]
    convert_element_type x1 -> x0, local copies, waits for them, and re-layouts: 0.84 us -> none  [local(): return (out_gate.astype(jnp.float32) * total).astype(jnp.bfloat16)]
  transfers between devices with their start and end apart: 3 -> 2, of which waited for: 3 -> 2; matrix products, arithmetic and copies ran while one was open for 4% -> 3% of each run, Pallas kernels for 0% -> 0%
where the time goes in v11:
time: 70.7 us; the launch traced here: 70.3 us
  blocking collectives  23.4 us (33%)
  waiting for transfers between devices  22.3 us (32%)
  starting transfers between devices  11.4 us (16%)
  Pallas kernels  4.63 us (7%)
  matrix products  3.84 us (5%)
  other arithmetic  2.37 us (3%)
  local copies, waits for them, and re-layouts  2.14 us (3%)
    all_to_all x1, blocking collectives, local(): lax.all_to_all(regroup(conv, groups), 'seq', split_axis=0, concat_axis=0,...  23.4 us
    all_to_all x1, waiting for transfers between devices, local(): lax.all_to_all(payload, 'seq', split_axis=0, concat_axis=1, tiled=True)  21.9 us
    all_to_all x1, starting transfers between devices, local(): lax.all_to_all(payload, 'seq', split_axis=0, concat_axis=1, tiled=True)  11.3 us
    pallas_call x1, Pallas kernels, prologue(): pl.pallas_call(prologue_kernel, grid_spec=grid_spec, out_shape=jax.ShapeD...  2.77 us
    pallas_call x1, Pallas kernels, regroup(): pl.pallas_call(regroup_kernel, in_specs=[pl.BlockSpec(memory_space=pltpu....  1.86 us
    dot_general x2, matrix products, spectrum(): a = jnp.einsum('kn,bnm->bkm', stage_a, x, precision=exact_mode)  1.48 us
  transfers between devices with their start and end apart: 2, of which 2 were waited for; matrix products, arithmetic and copies ran while one was open for 3% of the time, Pallas kernels for 0%

profile of v11, /device:TPU:8, one launch (start us, length us, event | category | flops | bytes accessed | tf_op | source)
XLA Modules:
  0.0 70.3 jit_solution(1574397335351123036)
XLA Ops:
  0.0 2.8 %shard_map.55 = f32[512,384]{1,0:T(8,128)} custom-call(s32[1]{0:T(128)} %bitcast.core_ref, bf16[256,512]{1,0:T(8,128)(2,1)} %gate_ref.1, bf16[256,512]{1,0:T(8,128)(2,1)} %values_ref.1, bf16[256,512]{1,0:T(8,128)(2,1)} %taps_ref.1), custom_call_target="tpu_custom_call" | custom-call | tf_op jit(solution)/shard_map/pallas_call | solution.py:88
  2.8 11.3 %all-to-all-start = ((f32[32,16,384]{2,1,0:T(8,128)}), f32[32,16,384]{2,1,0:T(8,128)S(1)}, u32[]{:S(2)}, u32[]{:S(2)}) async-start(f32[32,16,384]{2,1,0:T(8,128)} %bitcast.44), calls=%async_computation | async-start | bytes 1572864 | tf_op jit(solution)/shard_map/all_to_all | solution.py:117
  14.1 0.1 pad_maximum_fusion.10
  14.2 0.1 sine_negate_fusion
  14.3 0.3 fusion.51
  14.6 0.2 fusion.52
  14.8 0.3 fusion.46
  15.0 21.9 %all-to-all-done = f32[32,16,384]{2,1,0:T(8,128)S(1)} async-done(((f32[32,16,384]{2,1,0:T(8,128)}), f32[32,16,384]{2,1,0:T(8,128)S(1)}, u32[]{:S(2)}, u32[]{:S(2)}) %all-to-all-start) | async-done | bytes 786464 | tf_op jit(solution)/shard_map/all_to_all | solution.py:117
  37.0 0.1 slice.48
  37.1 0.1 collective-permute-start
  37.2 0.3 copy.6
  37.5 0.7 %convolution_bitcast_fusion.1 = f32[16,144,128]{2,1,0:T(8,128)S(1)} fusion(f32[16,64,128]{2,1,0:T(8,128)S(1)} %reshape_reshape.6, f32[72,64]{0,1:T(8,128)S(1)} %get-tuple-element.17, f32[72,64]{0,1:T(8,128)S(1)} %get-tuple-element.18), kind=kOutput, calls=%fused_computation.1 | convolution fusion | flops 113255424 | bytes 1740800 | tf_op jit(solution)/shard_map/kn,bnm->bkm/dot_general | solution.py:37
  38.3 0.4 collective-permute-done
  38.7 0.1 select_bitcast_fusion.1
  38.8 0.4 copy.7
  39.2 0.7 %convolution_bitcast_fusion = f32[16,144,128]{2,1,0:T(8,128)S(1)} fusion(f32[16,64,128]{2,1,0:T(8,128)S(1)} %bitcast.46, f32[72,64]{0,1:T(8,128)S(1)} %get-tuple-element.17, f32[72,64]{0,1:T(8,128)S(1)} %get-tuple-element.18), kind=kOutput, calls=%fused_computation | convolution fusion | flops 113255424 | bytes 1740800 | tf_op jit(solution)/shard_map/kn,bnm->bkm/dot_general | solution.py:37
  39.9 0.2 multiply_add_fusion.3
  40.2 0.6 fusion
  40.8 0.6 fusion.4
  41.5 0.1 multiply_subtract_fusion.1
  41.6 0.6 fusion.8
  42.3 0.1 multiply_subtract_fusion
  42.4 0.5 convolution_multiply_fusion
  42.9 1.1 %copy.11 = f32[2,8,64,128]{3,1,2,0:T(8,128)} copy(f32[2,8,64,128]{3,2,1,0:T(8,128)S(1)} %bitcast.45) | data formatting | bytes 1048576
  44.0 1.9 %shard_map.56 = f32[32,16,256]{2,1,0:T(8,128)} custom-call(f32[16,8192]{1,0:T(8,128)} %bitcast.47), custom_call_target="tpu_custom_call" | custom-call | tf_op jit(solution)/shard_map/pallas_call | solution.py:103
  45.8 23.4 %all_to_all.21 = f32[32,16,256]{2,1,0:T(8,128)S(1)} all-to-all(f32[32,16,256]{2,1,0:T(8,128)} %shard_map.56), channel_id=1, replica_groups=mesh['seq'=32,'grp'=8] {'seq'}, dimensions={0} | all-to-all | bytes 1048576 | tf_op jit(solution)/shard_map/all_to_all | solution.py:132
  69.2 0.2 copy.8
  69.4 0.0 copy-done
  69.4 0.0 copy-done.1
  69.5 0.0 copy-done.2
  69.5 0.0 copy-done.3
  69.5 0.8 %fusion.16 = bf16[256,512]{1,0:T(8,128)(2,1)} fusion(f32[512,256]{0,1:T(8,128)S(1)} %copy.8, bf16[256,512]{1,0:T(8,128)(2,1)S(1)} %copy-done.1, bf16[256,512]{1,0:T(8,128)(2,1)S(1)} %copy-done, bf16[256,512]{1,0:T(8,128)(2,1)S(1)} %copy-done.2, f32[512]{0:T(512)S(1)} %copy-done.3), kind=kLoop, calls=%fused_computation.30 | loop fusion | flops 1048576 | bytes 1574912 | tf_op jit(solution)/shard_map/convert_element_type | solution.py:136
  (8 shorter events, 0.1 us)
Async XLA Ops:
  2.8 34.2 %all-to-all-start = ((f32[32,16,384]{2,1,0:T(8,128)}), f32[32,16,384]{2,1,0:T(8,128)S(1)}, u32[]{:S(2)}, u32[]{:S(2)}) async-start(f32[32,16,384]{2,1,0:T(8,128)} %bitcast.44), calls=%async_computation | async-start | bytes 1572864 | tf_op jit(solution)/shard_map/all_to_all | solution.py:117
  37.1 1.6 %collective-permute-start = (f32[16,32,128]{2,0,1:T(8,128)S(1)}, f32[16,32,128]{2,0,1:T(8,128)S(1)}, u32[]{:S(2)}, u32[]{:S(2)}) collective-permute-start(f32[16,32,128]{2,0,1:T(8,128)S(1)} %slice.52), channel_id=1, source_target_pairs={{0,1},{1,0},{2,3},{3,2},{4,5},{5,4},{6,7},{7,6},{8,9},{9,8},{10,11... | collective-permute-start | bytes 786440 | tf_op jit(solution)/shard_map/ppermute | solution.py:122
  45.8 23.6 %copy-start = (bf16[256,512]{1,0:T(8,128)(2,1)S(1)}, bf16[256,512]{1,0:T(8,128)(2,1)}, u32[]{:S(2)}) copy-start(bf16[256,512]{1,0:T(8,128)(2,1)} %gate_ref.1) | copy-start | bytes 786436
  45.8 23.6 %copy-start.1 = (bf16[256,512]{1,0:T(8,128)(2,1)S(1)}, bf16[256,512]{1,0:T(8,128)(2,1)}, u32[]{:S(2)}) copy-start(bf16[256,512]{1,0:T(8,128)(2,1)} %values_ref.1) | copy-start | bytes 786436
  45.8 23.6 %copy-start.2 = (bf16[256,512]{1,0:T(8,128)(2,1)S(1)}, bf16[256,512]{1,0:T(8,128)(2,1)}, u32[]{:S(2)}) copy-start(bf16[256,512]{1,0:T(8,128)(2,1)} %param.7) | copy-start | bytes 786436
  45.8 23.6 %copy-start.3 = (f32[512]{0:T(512)S(1)}, f32[512]{0:T(512)}, u32[]{:S(2)}) copy-start(f32[512]{0:T(512)} %param.9) | copy-start | bytes 6148

commit v12 on v7

--- a/solution.py
+++ b/solution.py
@@ -92,8 +92,8 @@
     )(core.reshape(1), in_gate, values, filter_taps)
 
 
-def local(in_gate, values, out_gate, filter_taps, skip_gain):
-    own_rows, channels = in_gate.shape
+def local_body(in_gate, values, out_gate, filter_taps, skip_gain):
+    own_rows, _ = in_gate.shape
     copies = lax.axis_size("grp")
     core = lax.axis_index("grp") % 2
     half = own_rows // 2
@@ -106,7 +106,7 @@
     theirs = lax.ppermute(mine, "grp", [(g, g ^ 1) for g in range(copies)])
     n = gated_spread.shape[1]
     tables = dft_tables(n // SIDE)
-    spec_g = spectrum(gated_spread, tables)
+    spec_g = spectrum(gated_spread, lax.optimization_barrier(tables))
     first = jnp.where(core == 0, mine, theirs)
     second = jnp.where(core == 0, theirs, mine)
     taps_full = jnp.stack([first, second], axis=2).reshape(ch, -1)
@@ -127,4 +127,4 @@
         P(),
     )
     out_specs = P(("grp", "seq"), None)
-    return jax.shard_map(local, mesh=mesh, in_specs=in_specs, out_specs=out_specs, check_vma=False)
+    return jax.shard_map(local_body, mesh=mesh, in_specs=in_specs, out_specs=out_specs, check_vma=False)

time: 68.8 us -> 68.7 us (level)
  no operation moved by 1% of the time
where the time goes in v12:
time: 68.7 us; the launch traced here: 68.4 us
  waiting for transfers between devices  39.8 us (58%)
  starting transfers between devices  16.7 us (24%)
  matrix products  3.76 us (5%)
  local copies, waits for them, and re-layouts  3.33 us (5%)
  Pallas kernels  2.75 us (4%)
  other arithmetic  1.78 us (3%)
    all_to_all x1, waiting for transfers between devices, local_body(): lax.all_to_all(payload, 'seq', split_axis=0, concat_axis=1, tiled=True)  21.8 us
    all_to_all x1, waiting for transfers between devices, local_body(): back = lax.all_to_all(conv, 'seq', split_axis=1, concat_axis=0, tiled=True)  17.9 us
    all_to_all x1, starting transfers between devices, local_body(): lax.all_to_all(payload, 'seq', split_axis=0, concat_axis=1, tiled=True)  11.3 us
    all_to_all x1, starting transfers between devices, local_body(): back = lax.all_to_all(conv, 'seq', split_axis=1, concat_axis=0, tiled=True)  5.26 us
    pallas_call x1, Pallas kernels, prologue(): pl.pallas_call(prologue_kernel, grid_spec=grid_spec, out_shape=jax.ShapeD...  2.75 us
    dot_general x2, matrix products, spectrum(): a = jnp.einsum('kn,bnm->bkm', stage_a, x, precision=exact_mode)  1.41 us
  transfers between devices with their start and end apart: 3, of which 3 were waited for; matrix products, arithmetic and copies ran while one was open for 4% of the time, Pallas kernels for 0%

profile of v12, /device:TPU:8, one launch (start us, length us, event | category | flops | bytes accessed | tf_op | source)
XLA Modules:
  0.0 68.4 jit_solution(12421677097694991577)
XLA Ops:
  0.0 2.8 %shard_map.55 = f32[512,384]{1,0:T(8,128)} custom-call(s32[1]{0:T(128)} %bitcast.core_ref, bf16[256,512]{1,0:T(8,128)(2,1)} %gate_ref.1, bf16[256,512]{1,0:T(8,128)(2,1)} %values_ref.1, bf16[256,512]{1,0:T(8,128)(2,1)} %taps_ref.1), custom_call_target="tpu_custom_call" | custom-call | tf_op jit(solution)/shard_map/pallas_call | solution.py:88
  2.8 11.3 %all-to-all-start = ((f32[32,16,384]{2,1,0:T(8,128)}), f32[32,16,384]{2,1,0:T(8,128)S(1)}, u32[]{:S(2)}, u32[]{:S(2)}) async-start(f32[32,16,384]{2,1,0:T(8,128)} %bitcast.47), calls=%async_computation | async-start | bytes 1572864 | tf_op jit(solution)/shard_map/all_to_all | solution.py:101
  14.1 0.1 pad_maximum_fusion.6
  14.2 0.3 fusion.46
  14.4 0.1 sine_negate_fusion
  14.6 0.2 fusion.47
  14.8 0.3 fusion.41
  15.1 0.1 broadcast_multiply_fusion
  15.2 21.8 %all-to-all-done = f32[32,16,384]{2,1,0:T(8,128)S(1)} async-done(((f32[32,16,384]{2,1,0:T(8,128)}), f32[32,16,384]{2,1,0:T(8,128)S(1)}, u32[]{:S(2)}, u32[]{:S(2)}) %all-to-all-start) | async-done | bytes 786464 | tf_op jit(solution)/shard_map/all_to_all | solution.py:101
  37.0 0.3 copy.10
  37.4 0.1 collective-permute-start
  37.5 0.7 convolution_bitcast_fusion.1
  38.2 0.1 multiply_add_fusion.3
  38.3 0.6 fusion.1
  39.0 0.1 collective-permute-done
  39.1 0.4 copy.11
  39.5 0.7 %convolution_bitcast_fusion = f32[16,144,128]{2,1,0:T(8,128)S(1)} fusion(f32[16,64,128]{2,1,0:T(8,128)S(1)} %bitcast.48, f32[72,64]{0,1:T(8,128)S(1)} %get-tuple-element.25, f32[72,64]{0,1:T(8,128)S(1)} %get-tuple-element.26), kind=kOutput, calls=%fused_computation | convolution fusion | flops 113255424 | bytes 1740800 | tf_op jit(solution)/shard_map/kn,bnm->bkm/dot_general | solution.py:37
  40.3 0.1 multiply_add_fusion.2
  40.4 0.6 fusion.5
  41.1 0.1 multiply_subtract_fusion.1
  41.2 0.6 fusion.9
  41.8 0.1 multiply_subtract_fusion
  42.0 0.4 fusion
  42.4 0.1 mul.386
  42.6 1.1 %copy.12 = f32[16,32,256]{2,0,1:T(8,128)} copy(f32[16,32,256]{2,1,0:T(8,128)S(1)} %mul.386) | data formatting | bytes 1048576 | tf_op jit(solution)/shard_map/mul | solution.py:58
  43.7 5.3 %all-to-all-start.1 = ((f32[16,32,256]{2,0,1:T(8,128)}), f32[16,32,256]{2,0,1:T(8,128)S(1)}, u32[]{:S(2)}, u32[]{:S(2)}) async-start(f32[16,32,256]{2,0,1:T(8,128)} %copy.12), calls=%async_computation.1 | async-start | bytes 1048576 | tf_op jit(solution)/shard_map/all_to_all | solution.py:115
  49.0 0.1 copy.13
  49.1 0.1 copy.14
  49.3 0.1 copy.9
  49.4 17.9 %all-to-all-done.1 = f32[16,32,256]{2,0,1:T(8,128)S(1)} async-done(((f32[16,32,256]{2,0,1:T(8,128)}), f32[16,32,256]{2,0,1:T(8,128)S(1)}, u32[]{:S(2)}, u32[]{:S(2)}) %all-to-all-start.1) | async-done | bytes 524320 | tf_op jit(solution)/shard_map/all_to_all | solution.py:115
  67.4 0.2 fusion.17
  67.5 0.8 %copy.15 = bf16[256,512]{1,0:T(8,128)(2,1)} copy(bf16[256,512]{0,1:T(8,128)(2,1)S(1)} %fusion.17) | data formatting | bytes 524288 | tf_op jit(solution)/shard_map/convert_element_type | solution.py:118
  (15 shorter events, 0.2 us)
Async XLA Ops:
  2.8 34.2 %all-to-all-start = ((f32[32,16,384]{2,1,0:T(8,128)}), f32[32,16,384]{2,1,0:T(8,128)S(1)}, u32[]{:S(2)}, u32[]{:S(2)}) async-start(f32[32,16,384]{2,1,0:T(8,128)} %bitcast.47), calls=%async_computation | async-start | bytes 1572864 | tf_op jit(solution)/shard_map/all_to_all | solution.py:101
  37.4 1.6 %collective-permute-start = (f32[16,32,128]{2,0,1:T(8,128)S(1)}, f32[16,32,128]{2,0,1:T(8,128)S(1)}, u32[]{:S(2)}, u32[]{:S(2)}) collective-permute-start(f32[16,32,128]{2,0,1:T(8,128)S(1)} %slice.52), channel_id=1, source_target_pairs={{0,1},{1,0},{2,3},{3,2},{4,5},{5,4},{6,7},{7,6},{8,9},{9,8},{10,11... | collective-permute-start | bytes 786440 | tf_op jit(solution)/shard_map/ppermute | solution.py:106
  42.6 6.4 %copy-start = (bf16[256,512]{1,0:T(8,128)(2,1)S(1)}, bf16[256,512]{1,0:T(8,128)(2,1)}, u32[]{:S(2)}) copy-start(bf16[256,512]{1,0:T(8,128)(2,1)} %gate_ref.1) | copy-start | bytes 786436
  42.6 6.5 %copy-start.1 = (bf16[256,512]{1,0:T(8,128)(2,1)S(1)}, bf16[256,512]{1,0:T(8,128)(2,1)}, u32[]{:S(2)}) copy-start(bf16[256,512]{1,0:T(8,128)(2,1)} %values_ref.1) | copy-start | bytes 786436
  43.7 5.6 %copy-start.2 = (bf16[256,512]{1,0:T(8,128)(2,1)S(1)}, bf16[256,512]{1,0:T(8,128)(2,1)}, u32[]{:S(2)}) copy-start(bf16[256,512]{1,0:T(8,128)(2,1)} %param.7) | copy-start | bytes 786436
  43.7 23.7 %copy-start.3 = (f32[512]{0:T(512)S(1)}, f32[512]{0:T(512)}, u32[]{:S(2)}) copy-start(f32[512]{0:T(512)} %param.9) | copy-start | bytes 6148
  43.7 23.6 %all-to-all-start.1 = ((f32[16,32,256]{2,0,1:T(8,128)}), f32[16,32,256]{2,0,1:T(8,128)S(1)}, u32[]{:S(2)}, u32[]{:S(2)}) async-start(f32[16,32,256]{2,0,1:T(8,128)} %copy.12), calls=%async_computation.1 | async-start | bytes 1048576 | tf_op jit(solution)/shard_map/all_to_all | solution.py:115

commit v13 on v12

--- a/solution.py
+++ b/solution.py
@@ -107,10 +107,10 @@
     n = gated_spread.shape[1]
     tables = dft_tables(n // SIDE)
     spec_g = spectrum(gated_spread, lax.optimization_barrier(tables))
-    first = jnp.where(core == 0, mine, theirs)
-    second = jnp.where(core == 0, theirs, mine)
-    taps_full = jnp.stack([first, second], axis=2).reshape(ch, -1)
-    spec_h = spectrum(taps_full, tables)
+    taps_full = jnp.stack([mine, theirs], axis=2).reshape(ch, -1)
+    stage_a = tables[0]
+    swapped = stage_a[:, jnp.arange(stage_a.shape[1]) ^ (half // SIDE)]
+    spec_h = spectrum(taps_full, (jnp.where(core == 0, stage_a, swapped),) + tuple(tables[1:]))
     conv = inverse_prefix(spec_g, spec_h, tables, n)
     back = lax.all_to_all(conv, "seq", split_axis=1, concat_axis=0, tiled=True)
     gated = in_gate.astype(jnp.float32) * values.astype(jnp.float32)

time: 68.7 us -> 68.6 us (level)
  waiting for transfers between devices: 39.8 us -> 39.1 us
  transfers between devices with their start and end apart: 3 -> 3, of which waited for: 3 -> 3; matrix products, arithmetic and copies ran while one was open for 4% -> 5% of each run, Pallas kernels for 0% -> 0%
where the time goes in v13:
time: 68.6 us; the launch traced here: 68.3 us
  waiting for transfers between devices  39.1 us (57%)
  starting transfers between devices  16.7 us (24%)
  local copies, waits for them, and re-layouts  4 us (6%)
  matrix products  3.76 us (5%)
  Pallas kernels  2.75 us (4%)
  other arithmetic  1.75 us (3%)
    all_to_all x1, waiting for transfers between devices, local_body(): lax.all_to_all(payload, 'seq', split_axis=0, concat_axis=1, tiled=True)  21.1 us
    all_to_all x1, waiting for transfers between devices, local_body(): back = lax.all_to_all(conv, 'seq', split_axis=1, concat_axis=0, tiled=True)  17.9 us
    all_to_all x1, starting transfers between devices, local_body(): lax.all_to_all(payload, 'seq', split_axis=0, concat_axis=1, tiled=True)  11.3 us
    all_to_all x1, starting transfers between devices, local_body(): back = lax.all_to_all(conv, 'seq', split_axis=1, concat_axis=0, tiled=True)  5.26 us
    pallas_call x1, Pallas kernels, prologue(): pl.pallas_call(prologue_kernel, grid_spec=grid_spec, out_shape=jax.ShapeD...  2.75 us
    dot_general x2, matrix products, spectrum(): a = jnp.einsum('kn,bnm->bkm', stage_a, x, precision=exact_mode)  1.41 us
  transfers between devices with their start and end apart: 3, of which 3 were waited for; matrix products, arithmetic and copies ran while one was open for 5% of the time, Pallas kernels for 0%

profile of v13, /device:TPU:8, one launch (start us, length us, event | category | flops | bytes accessed | tf_op | source)
XLA Modules:
  0.0 68.3 jit_solution(14288786266184119776)
XLA Ops:
  0.0 2.8 %shard_map.55 = f32[512,384]{1,0:T(8,128)} custom-call(s32[1]{0:T(128)} %bitcast.core_ref, bf16[256,512]{1,0:T(8,128)(2,1)} %gate_ref.1, bf16[256,512]{1,0:T(8,128)(2,1)} %values_ref.1, bf16[256,512]{1,0:T(8,128)(2,1)} %taps_ref.1), custom_call_target="tpu_custom_call" | custom-call | tf_op jit(solution)/shard_map/pallas_call | solution.py:88
  2.8 11.3 %all-to-all-start = ((f32[32,16,384]{2,1,0:T(8,128)}), f32[32,16,384]{2,1,0:T(8,128)S(1)}, u32[]{:S(2)}, u32[]{:S(2)}) async-start(f32[32,16,384]{2,1,0:T(8,128)} %bitcast.52), calls=%async_computation | async-start | bytes 1572864 | tf_op jit(solution)/shard_map/all_to_all | solution.py:101
  14.1 0.1 pad_maximum_fusion.6
  14.2 0.3 fusion.47
  14.4 0.1 sine_negate_fusion
  14.6 0.2 fusion.48
  14.8 0.3 fusion.41
  15.1 0.1 broadcast_multiply_fusion
  15.2 0.7 gather_fusion
  15.8 21.1 %all-to-all-done = f32[32,16,384]{2,1,0:T(8,128)S(1)} async-done(((f32[32,16,384]{2,1,0:T(8,128)}), f32[32,16,384]{2,1,0:T(8,128)S(1)}, u32[]{:S(2)}, u32[]{:S(2)}) %all-to-all-start) | async-done | bytes 786464 | tf_op jit(solution)/shard_map/all_to_all | solution.py:101
  37.1 0.3 copy.10
  37.4 0.1 collective-permute-start
  37.5 0.7 convolution_bitcast_fusion.1
  38.2 0.1 multiply_add_fusion.3
  38.3 0.6 fusion.1
  39.1 0.4 copy.11
  39.5 0.7 %convolution_bitcast_fusion = f32[16,144,128]{2,1,0:T(8,128)S(1)} fusion(f32[16,64,128]{2,1,0:T(8,128)S(1)} %bitcast.53, f32[64,144]{1,0:T(8,128)S(1)} %gather_fusion, pred[]{:T(512)S(6)} %eq.27, f32[72,64]{0,1:T(8,128)S(1)} %get-tuple-element.25, f32[72,64]{0,1:T(8,128)S(1)} %get-tuple-element.26), kind=kOutput, calls=%fused_computation.1 | convolution fusion | flops 113264640 | bytes 1777665 | tf_op jit(solution)/shard_map/kn,bnm->bkm/dot_general | solution.py:37
  40.2 0.1 multiply_add_fusion.2
  40.4 0.6 fusion.5
  41.0 0.1 multiply_subtract_fusion.1
  41.2 0.6 fusion.9
  41.8 0.1 multiply_subtract_fusion
  41.9 0.4 fusion
  42.4 0.1 mul.386
  42.6 1.1 %copy.12 = f32[16,32,256]{2,0,1:T(8,128)} copy(f32[16,32,256]{2,1,0:T(8,128)S(1)} %mul.386) | data formatting | bytes 1048576 | tf_op jit(solution)/shard_map/mul | solution.py:58
  43.7 5.3 %all-to-all-start.1 = ((f32[16,32,256]{2,0,1:T(8,128)}), f32[16,32,256]{2,0,1:T(8,128)S(1)}, u32[]{:S(2)}, u32[]{:S(2)}) async-start(f32[16,32,256]{2,0,1:T(8,128)} %copy.12), calls=%async_computation.1 | async-start | bytes 1048576 | tf_op jit(solution)/shard_map/all_to_all | solution.py:115
  48.9 0.1 copy.13
  49.1 0.1 copy.14
  49.2 0.1 copy.9
  49.4 17.9 %all-to-all-done.1 = f32[16,32,256]{2,0,1:T(8,128)S(1)} async-done(((f32[16,32,256]{2,0,1:T(8,128)}), f32[16,32,256]{2,0,1:T(8,128)S(1)}, u32[]{:S(2)}, u32[]{:S(2)}) %all-to-all-start.1) | async-done | bytes 524320 | tf_op jit(solution)/shard_map/all_to_all | solution.py:115
  67.3 0.2 fusion.17
  67.5 0.8 %copy.15 = bf16[256,512]{1,0:T(8,128)(2,1)} copy(bf16[256,512]{0,1:T(8,128)(2,1)S(1)} %fusion.17) | data formatting | bytes 524288 | tf_op jit(solution)/shard_map/convert_element_type | solution.py:118
  (17 shorter events, 0.3 us)
Async XLA Ops:
  2.8 34.2 %all-to-all-start = ((f32[32,16,384]{2,1,0:T(8,128)}), f32[32,16,384]{2,1,0:T(8,128)S(1)}, u32[]{:S(2)}, u32[]{:S(2)}) async-start(f32[32,16,384]{2,1,0:T(8,128)} %bitcast.52), calls=%async_computation | async-start | bytes 1572864 | tf_op jit(solution)/shard_map/all_to_all | solution.py:101
  37.4 1.6 %collective-permute-start = (f32[16,32,128]{2,0,1:T(8,128)S(1)}, f32[16,32,128]{2,0,1:T(8,128)S(1)}, u32[]{:S(2)}, u32[]{:S(2)}) collective-permute-start(f32[16,32,128]{2,0,1:T(8,128)S(1)} %get-tuple-element.22), channel_id=1, source_target_pairs={{0,1},{1,0},{2,3},{3,2},{4,5},{5,4},{6,7},{7,6},{8,9},{9,8},{10,11... | collective-permute-start | bytes 786440 | tf_op jit(solution)/shard_map/ppermute | solution.py:106
  42.5 6.4 %copy-start = (bf16[256,512]{1,0:T(8,128)(2,1)S(1)}, bf16[256,512]{1,0:T(8,128)(2,1)}, u32[]{:S(2)}) copy-start(bf16[256,512]{1,0:T(8,128)(2,1)} %gate_ref.1) | copy-start | bytes 786436
  42.6 6.5 %copy-start.1 = (bf16[256,512]{1,0:T(8,128)(2,1)S(1)}, bf16[256,512]{1,0:T(8,128)(2,1)}, u32[]{:S(2)}) copy-start(bf16[256,512]{1,0:T(8,128)(2,1)} %values_ref.1) | copy-start | bytes 786436
  43.7 5.6 %copy-start.2 = (bf16[256,512]{1,0:T(8,128)(2,1)S(1)}, bf16[256,512]{1,0:T(8,128)(2,1)}, u32[]{:S(2)}) copy-start(bf16[256,512]{1,0:T(8,128)(2,1)} %param.7) | copy-start | bytes 786436
  43.7 23.6 %copy-start.3 = (f32[512]{0:T(512)S(1)}, f32[512]{0:T(512)}, u32[]{:S(2)}) copy-start(f32[512]{0:T(512)} %param.9) | copy-start | bytes 6148
  43.7 23.6 %all-to-all-start.1 = ((f32[16,32,256]{2,0,1:T(8,128)}), f32[16,32,256]{2,0,1:T(8,128)S(1)}, u32[]{:S(2)}, u32[]{:S(2)}) async-start(f32[16,32,256]{2,0,1:T(8,128)} %copy.12), calls=%async_computation.1 | async-start | bytes 1048576 | tf_op jit(solution)/shard_map/all_to_all | solution.py:115
